TPU v7x, 512 devices: a whole 4x8x8 slice. The times are simulated.
512 devices in a mesh: lon: 128 (over z, x, y_hi, core), lat: 4 (over y_lo).
Axes of the slice: x: 4, y: 8 (y_hi: 2, y_lo: 4; y = y_hi * 4 + y_lo), z: 8, core: 2. Of those that a mesh axis runs over, the one named last changes fastest.
Arguments:
- state: float32 [2, 4, 5760, 512], P(None, None, 'lon', 'lat'), may hold values from -6 to 6
- courant: float32 [2, 5760, 512], P(None, 'lon', 'lat'), may hold values from 1 to 34560
- band_mask: int32 [512], P('lat'), may hold values 0 or 1
Outputs:
- updated: float32 [2, 4, 5760, 512], P(None, None, 'lon', 'lat')
All inputs are finite; a program needn't handle non-finite values. No bound on the sum of `band_mask` on one device may be relied on, other than what follows from the above.
Results may differ from a plain program's by a relative error of at most 0.00029.
Values sent between devices are 32-bit elements; how exact they have to be, the bound alone decides.
No kernel may reach another device: no remote copies, remote signals or barrier semaphores. Data moves between devices by JAX's collectives and lax.ppermute only.
A program may use at most 64 MiB of HBM per device.

v0:
```python
import jax
import jax.numpy as jnp
from jax import lax
from jax.sharding import PartitionSpec as P

ITERS = 2


def padded_2(block, sides, width):
    for axis, dim in sides:
        count = lax.axis_size(axis)
        forward = [(i, i + 1) for i in range(count - 1)]
        forward.append((count - 1, 0))
        backward = [(target, source) for source, target in forward]
        low = lax.ppermute(
            lax.slice_in_dim(block, block.shape[dim] - width, None, axis=dim), axis, forward
        )
        high = lax.ppermute(lax.slice_in_dim(block, 0, width, axis=dim), axis, backward)
        block = jnp.concatenate([low, block, high], axis=dim)
    return block


def from_behind(value, axis, steps):
    count = lax.axis_size(axis)
    pairs = [(source, (source + steps) % count) for source in range(count)]
    return lax.ppermute(value, axis, pairs)


def carried_in(part, axis, combine, identity):
    place = lax.axis_index(axis)
    gathered = jax.tree.map(lambda a: lax.all_gather(a, axis), part)
    state = jax.tree.map(lambda a, e: jnp.zeros_like(a) + jnp.asarray(e, a.dtype), part, identity)

    def one(lap, state):
        return combine(
            state, jax.tree.map(lambda a: lax.dynamic_index_in_dim(a, lap, 0, False), gathered)
        )

    return lax.fori_loop(0, place, one, state)


def broadcast(value, axis, source):
    kept = jnp.where(lax.axis_index(axis) == source, value, 0).astype(value.dtype)
    return lax.psum(kept, axis)


def compose(earlier, later):
    return (later[0] * earlier[0], later[0][..., None, :] * earlier[1] + later[1])


def local_level(operands):
    logs_level, weights_level = operands
    spread_log = logs_level[:, None, :] - logs_level[None, :, :]
    count = logs_level.shape[0]
    below_diag = (jnp.arange(count)[:, None] >= jnp.arange(count)[None, :])[:, :, None]
    green = jnp.where(below_diag, jnp.exp(jnp.minimum(spread_log, 0.0)), 0.0)
    return jnp.einsum("ikr,fkr->fir", green, weights_level, precision=lax.Precision.HIGHEST)


def tendency(field, turning, first_band, last_band, half_cycle):
    padded = padded_2(field, (("lon", 2), ("lat", 3)), 1)
    poles = jnp.stack((field[..., 0], field[..., -1]), 0)
    across = from_behind(poles, "lon", half_cycle)
    flips = jnp.array([-1.0, -1.0, 1.0, 1.0], jnp.float32)[None, :, None]
    north_rim = jnp.where(first_band, across[0] * flips, padded[:, :, 1:-1, 0])
    south_rim = jnp.where(last_band, across[1] * flips, padded[:, :, 1:-1, -1])
    padded = padded.at[:, :, 1:-1, 0].set(north_rim).at[:, :, 1:-1, -1].set(south_rim)
    north_rows = padded[:, :, 1:-1, :-2]
    south_rows = padded[:, :, 1:-1, 2:]
    east_cells = padded[:, :, 2:, 1:-1]
    west_cells = padded[:, :, :-2, 1:-1]
    u_wind = field[:, 0:1]
    v_wind = field[:, 1:2]
    result = 0.1 * (east_cells + west_cells - 2.0 * field) + 0.1 * (
        north_rows + south_rows - 2.0 * field
    )
    result = result - 0.25 * v_wind * (north_rows - south_rows)
    coriolis = jnp.concatenate(
        [turning * v_wind, -turning * u_wind, jnp.zeros_like(field[:, 2:])], axis=1
    )
    return result + coriolis


def local(state, courant, band_mask):
    rows = state.shape[3]
    lat_index = lax.axis_index("lat")
    lat_count = lax.axis_size("lat")
    half_cycle = lax.axis_size("lon") // 2
    total_rows = rows * lat_count
    row_ids = lat_index * rows + jnp.arange(rows, dtype=jnp.int32)
    latitude = jnp.pi / 2 - (row_ids.astype(jnp.float32) + 0.5) * jnp.pi / total_rows
    turning = 0.5 * jnp.sin(latitude)
    first_band = lat_index == 0
    last_band = lat_index == lat_count - 1
    inverse = 1.0 / (1.0 + courant)
    logs = jnp.cumsum(-jnp.log1p(1.0 / courant), axis=1)
    carried = jnp.exp(logs)
    map_gain = carried[:, -1, :]
    in_band = (band_mask == 1)[None, None, None, :]
    estimate = state
    for sweep in range(ITERS):
        middle = 0.5 * (state + estimate)
        star = state + tendency(middle, turning, first_band, last_band, half_cycle)
        partial_value = lax.map(local_level, (logs, star * inverse[:, None]))
        ends = partial_value[:, :, -1, :]
        identity = (jnp.ones_like(map_gain), jnp.zeros_like(ends))
        prior_a, prior_b = carried_in((map_gain, ends), "lon", compose, identity)
        whole = compose((prior_a, prior_b), (map_gain, ends))
        total_a, total_b = (
            broadcast(whole[0], "lon", lax.axis_size("lon") - 1),
            broadcast(whole[1], "lon", lax.axis_size("lon") - 1),
        )
        wrapped = total_b / (1.0 - total_a)[:, None, :]
        inflow = prior_b + prior_a[:, None, :] * wrapped
        solved = partial_value + carried[:, None] * inflow[:, :, None, :]
        estimate = jnp.where(in_band, solved, star)
    return estimate


def solution(mesh):
    in_specs = (P(None, None, "lon", "lat"), P(None, "lon", "lat"), P("lat"))
    out_specs = P(None, None, "lon", "lat")
    return jax.shard_map(local, mesh=mesh, in_specs=in_specs, out_specs=out_specs, check_vma=False)
```

profile of v0, /device:TPU:1, one launch (start us, length us, event | category | flops | bytes accessed | tf_op | source)
XLA Modules:
  0.0 1611.4 jit_solution(11507833808939434225)
XLA Ops:
  0.0 1.0 add_multiply_fusion
  1.0 8.8 collective-permute-start
  9.9 2.1 collective-permute-start.1
  12.0 0.3 fusion.57
  12.2 0.1 copy.304
  12.4 0.1 copy.305
  12.5 10.6 collective-permute-start.4
  23.2 0.1 log-plus-one_negate_fusion
  23.5 221.4 %all-gather = f32[256,1,128]{2,1,0:T(1,128)S(1)} all-gather(f32[2,1,128]{2,1,0:T(1,128)S(1)} %slice.276), channel_id=2, replica_groups=mesh['lon'=128,'lat'=4] {'lon'}, dimensions={0}, use_global_device_ids=true | all-gather | bytes 132096 | tf_op jit(solution)/shard_map/all_gather | solution.py:31
  244.9 0.1 copy.311
  245.2 0.1 pad_maximum_fusion.2
  245.3 0.3 fusion.54
  245.5 2.3 collective-permute-start.2
  247.9 5.0 collective-permute-start.3
  252.8 0.2 copy.306
  253.0 0.2 copy.307
  253.2 2.3 collective-permute-done.2
  255.5 4.6 collective-permute-done.3
  260.1 0.7 pad_maximum_fusion
  260.8 0.3 slice_select_fusion.2
  261.1 2.8 scatter.14
  263.9 14.9 scatter.15
  278.8 0.7 broadcast_multiply_fusion.1
  279.6 11.2 while.48
  279.7 0.2 copy.343
  279.9 5.3 fusion.69
  285.1 0.1 constant_dynamic-slice_fusion.4
  285.2 0.2 copy.343
  285.4 5.3 fusion.69
  290.7 0.2 copy.313
  290.9 0.2 copy.315
  291.2 218.4 %all-gather.1 = f32[256,4,1,128]{3,1,2,0:T(4,128)S(1)} all-gather(f32[2,4,1,128]{3,1,2,0:T(4,128)S(1)} %slice.277), channel_id=3, replica_groups=mesh['lon'=128,'lat'=4] {'lon'}, dimensions={0}, use_global_device_ids=true | all-gather | bytes 528384 | tf_op jit(solution)/shard_map/all_gather | solution.py:31
  509.7 405.4 %all-reduce.1 = (f32[2,4,128]{2,1,0:T(4,128)S(1)}, f32[2,128]{1,0:T(2,128)S(1)}) all-reduce(f32[2,4,128]{2,1,0:T(4,128)S(1)} %fusion.47, f32[2,128]{1,0:T(2,128)S(1)} %multiply_select_fusion.1), channel_id=1, replica_groups=mesh['lon'=128,'lat'=4] {'lon'}, use_global_device_ids=true, to_apply=%region_5.6 | all-reduce | flops 1280 | bytes 10240 | tf_op jit(solution)/shard_map/psum | solution.py:44
  915.1 0.2 broadcast_multiply_fusion.2
  915.3 0.3 fusion.55
  915.7 0.1 copy.317
  915.8 0.1 copy.318
  915.9 7.5 collective-permute-start.5
  923.4 6.8 collective-permute-start.6
  930.2 3.8 collective-permute-start.9
  934.1 0.1 pad_maximum_fusion.3
  934.2 0.3 fusion.53
  934.5 2.1 collective-permute-start.7
  936.6 4.9 collective-permute-start.8
  941.6 0.2 copy.319
  941.7 0.2 copy.320
  941.9 0.9 collective-permute-done.7
  942.8 2.0 collective-permute-done.8
  944.8 0.7 pad_maximum_fusion.1
  945.4 0.3 slice_select_fusion
  945.7 2.8 scatter.16
  948.5 14.9 scatter.19
  963.4 0.7 broadcast_multiply_fusion
  964.2 11.2 while.50
  964.3 0.2 copy.344
  964.5 5.3 fusion.73
  969.9 0.2 copy.344
  970.1 5.3 fusion.73
  975.4 0.2 copy.324
  975.6 0.2 copy.327
  975.9 226.5 %all-gather.2 = f32[256,4,1,128]{3,1,2,0:T(4,128)S(1)} all-gather(f32[2,4,1,128]{3,1,2,0:T(4,128)S(1)} %slice_bitcast_fusion.4), channel_id=4, replica_groups=mesh['lon'=128,'lat'=4] {'lon'}, dimensions={0}, use_global_device_ids=true | all-gather | bytes 528384 | tf_op jit(solution)/shard_map/all_gather | solution.py:31
  1202.4 408.1 %all-reduce = (f32[2,4,128]{2,1,0:T(4,128)S(1)}, f32[2,128]{1,0:T(2,128)S(1)}) all-reduce(f32[2,4,128]{2,1,0:T(4,128)S(1)} %fusion.46, f32[2,128]{1,0:T(2,128)S(1)} %multiply_select_fusion), channel_id=1, replica_groups=mesh['lon'=128,'lat'=4] {'lon'}, use_global_device_ids=true, to_apply=%region_11.12 | all-reduce | flops 1280 | bytes 10240 | tf_op jit(solution)/shard_map/psum | solution.py:44
  1610.6 0.1 add_select_fusion
  1610.7 0.7 copy.328
  (66 shorter events, 1.1 us)
Async XLA Ops:
  1.0 244.2 %collective-permute-start = (f32[2,4,1,128]{3,0,2,1:T(2,128)S(1)}, f32[2,4,1,128]{3,0,2,1:T(2,128)S(1)}, u32[]{:S(2)}, u32[]{:S(2)}) collective-permute-start(f32[2,4,1,128]{3,0,2,1:T(2,128)S(1)} %get-tuple-element.316), channel_id=1, source_target_pairs={{0,4},{4,8},{8,12},{12,16},{16,20},{20,24},{24,28},{28,32},{32,36}... | collective-permute-start | bytes 12296 | tf_op jit(solution)/shard_map/ppermute | solution.py:15
  9.9 13.3 copy-start.1
  9.9 235.3 %collective-permute-start.1 = (f32[2,4,1,128]{3,0,2,1:T(2,128)S(1)}, f32[2,4,1,128]{3,0,2,1:T(2,128)S(1)}, u32[]{:S(2)}, u32[]{:S(2)}) collective-permute-start(f32[2,4,1,128]{3,0,2,1:T(2,128)S(1)} %get-tuple-element.317), channel_id=1, source_target_pairs={{4,0},{8,4},{12,8},{16,12},{20,16},{24,20},{28,24},{32,28},{36,32}... | collective-permute-start | bytes 12296 | tf_op jit(solution)/shard_map/ppermute | solution.py:18
  12.2 11.2 copy-start.3
  12.5 240.3 %collective-permute-start.4 = (f32[2,2,4,45]{3,2,1,0:T(4,128)S(1)}, f32[2,2,4,45]{3,2,1,0:T(4,128)S(1)}, u32[]{:S(2)}, u32[]{:S(2)}) collective-permute-start(f32[2,2,4,45]{3,2,1,0:T(4,128)S(1)} %pad_maximum_fusion.4), channel_id=1, source_target_pairs={{0,256},{4,260},{8,264},{12,268},{16,272},{20,276},{24,280},{28,28... | collective-permute-start | bytes 8648 | tf_op jit(solution)/shard_map/ppermute | solution.py:26
  245.5 10.0 collective-permute-start.2
  247.9 12.2 collective-permute-start.3
  253.2 7.6 copy-start.2
  261.0 17.8 %copy-start = (f32[2,4,45,128]{3,1,2,0:T(4,128)S(1)}, f32[2,4,45,128]{3,1,2,0:T(4,128)}, u32[]{:S(2)}) copy-start(f32[2,4,45,128]{3,1,2,0:T(4,128)} %param.21) | copy-start | bytes 552964
  915.9 18.1 %collective-permute-start.5 = (f32[2,4,1,128]{3,0,2,1:T(2,128)S(1)}, f32[2,4,1,128]{3,0,2,1:T(2,128)S(1)}, u32[]{:S(2)}, u32[]{:S(2)}) collective-permute-start(f32[2,4,1,128]{3,0,2,1:T(2,128)S(1)} %get-tuple-element.309), channel_id=1, source_target_pairs={{0,4},{4,8},{8,12},{12,16},{16,20},{20,24},{24,28},{28,32},{32,36}... | collective-permute-start | bytes 12296 | tf_op jit(solution)/shard_map/ppermute | solution.py:15
  923.4 10.7 collective-permute-start.6
  930.2 11.3 collective-permute-start.9
  934.5 8.3 collective-permute-start.7
  936.6 8.2 collective-permute-start.8
where the time goes:
time: 1620 us; the launch traced here: 1610 us
  blocking collectives  1480 us (91%)
  starting transfers between devices  54 us (3%)
  local copies, waits for them, and re-layouts  40.8 us (3%)
  matrix products  21.1 us (1%)
    psum x2, blocking collectives, broadcast(): return lax.psum(kept, axis)  814 us
    all_gather x3, blocking collectives, carried_in(): gathered = jax.tree.map(lambda a: lax.all_gather(a, axis), part)  666 us
    scatter x4, local copies, waits for them, and re-layouts, tendency(): padded.at[:, :, 1:-1, 0].set(north_rim).at[:, :, 1:-1, -1].set(south_rim)  35.5 us
  transfers between devices with their start and end apart: 10, of which 4 were waited for; matrix products, arithmetic and copies ran while one was open for 0% of the time, Pallas kernels for 0%

commit v1 on v0

v1 whole, which is shorter than its diff:
```python
import jax
import jax.numpy as jnp
from jax import lax
from jax.sharding import PartitionSpec as P

ITERS = 2


def from_behind(value, axis, steps):
    count = lax.axis_size(axis)
    pairs = [(source, (source + steps) % count) for source in range(count)]
    return lax.ppermute(value, axis, pairs)


def shift_along(x, steps, axis, fill):
    pad_shape = list(x.shape)
    pad_shape[axis] = steps
    head = jnp.full(pad_shape, fill, x.dtype)
    body = lax.slice_in_dim(x, 0, x.shape[axis] - steps, axis=axis)
    return jnp.concatenate([head, body], axis=axis)


def block_rates(rate):
    steps = []
    span = 1
    while span < rate.shape[1]:
        steps.append((span, rate))
        rate = rate * shift_along(rate, span, 1, 1.0)
        span *= 2
    return steps, rate


def block_scan(steps, source):
    for span, rate in steps:
        source = source + rate[:, None] * shift_along(source, span, 2, 0.0)
    return source


def lon_rates(gain):
    count = lax.axis_size("lon")
    rounds = []
    window = gain
    excl = jnp.ones_like(gain)
    span = 1
    while span < count:
        rounds.append((span, window, excl))
        got = from_behind(window, "lon", span)
        excl = excl * got
        window = window * got
        span *= 2
    return rounds, excl


def inflow(rounds, excl, gain, ends):
    window = ends
    excl_b = jnp.zeros_like(ends)
    for span, rate_w, rate_e in rounds:
        got = from_behind(window, "lon", span)
        excl_b = rate_e[:, None] * got + excl_b
        window = rate_w[:, None] * got + window
    return (excl[:, None] * ends + excl_b) / (1.0 - excl * gain)[:, None]


def halo_tendency(field, turning, first_band, last_band, half_cycle):
    east = from_behind(field[:, :, 0, :], "lon", -1)
    west = from_behind(field[:, :, -1, :], "lon", 1)
    north = from_behind(field[..., -1], "lat", 1)
    south = from_behind(field[..., 0], "lat", -1)
    pole_send = jnp.where(first_band, field[..., 0], field[..., -1])
    across = from_behind(pole_send, "lon", half_cycle)
    flips = jnp.array([-1.0, -1.0, 1.0, 1.0], jnp.float32)[None, :, None]
    north = jnp.where(first_band, across * flips, north)
    south = jnp.where(last_band, across * flips, south)
    north_rows = jnp.concatenate([north[..., None], field[..., :-1]], axis=3)
    south_rows = jnp.concatenate([field[..., 1:], south[..., None]], axis=3)
    east_cells = jnp.concatenate([field[:, :, 1:], east[:, :, None]], axis=2)
    west_cells = jnp.concatenate([west[:, :, None], field[:, :, :-1]], axis=2)
    u_wind = field[:, 0:1]
    v_wind = field[:, 1:2]
    result = 0.1 * (east_cells + west_cells - 2.0 * field) + 0.1 * (
        north_rows + south_rows - 2.0 * field
    )
    result = result - 0.25 * v_wind * (north_rows - south_rows)
    coriolis = jnp.concatenate(
        [turning * v_wind, -turning * u_wind, jnp.zeros_like(field[:, 2:])], axis=1
    )
    return result + coriolis


def local(state, courant, band_mask):
    rows = state.shape[3]
    lat_index = lax.axis_index("lat")
    lat_count = lax.axis_size("lat")
    half_cycle = lax.axis_size("lon") // 2
    total_rows = rows * lat_count
    row_ids = lat_index * rows + jnp.arange(rows, dtype=jnp.int32)
    latitude = jnp.pi / 2 - (row_ids.astype(jnp.float32) + 0.5) * jnp.pi / total_rows
    turning = 0.5 * jnp.sin(latitude)
    first_band = lat_index == 0
    last_band = lat_index == lat_count - 1
    inverse = 1.0 / (1.0 + courant)
    rate = courant * inverse
    steps, carried = block_rates(rate)
    gain = carried[:, -1, :]
    rounds, excl = lon_rates(gain)
    in_band = (band_mask == 1)[None, None, None, :]
    estimate = state
    for sweep in range(ITERS):
        middle = 0.5 * (state + estimate)
        star = state + halo_tendency(middle, turning, first_band, last_band, half_cycle)
        partial_value = block_scan(steps, star * inverse[:, None])
        ends = partial_value[:, :, -1, :]
        entry = inflow(rounds, excl, gain, ends)
        solved = partial_value + carried[:, None] * entry[:, :, None, :]
        estimate = jnp.where(in_band, solved, star)
    return estimate


def solution(mesh):
    in_specs = (P(None, None, "lon", "lat"), P(None, "lon", "lat"), P("lat"))
    out_specs = P(None, None, "lon", "lat")
    return jax.shard_map(local, mesh=mesh, in_specs=in_specs, out_specs=out_specs, check_vma=False)
```

time: 1620 us -> 235 us (0.15)
  the two profiles are of different devices: /device:TPU:1 before, /device:TPU:8 now
where the time goes in v1:
time: 235 us; the launch traced here: 234 us
  waiting for transfers between devices  126 us (54%)
  starting transfers between devices  97.6 us (42%)
  other arithmetic  4.76 us (2%)
  local copies, waits for them, and re-layouts  4.73 us (2%)
    ppermute x31, waiting for transfers between devices, from_behind(): return lax.ppermute(value, axis, pairs)  126 us
    ppermute x31, starting transfers between devices, from_behind(): return lax.ppermute(value, axis, pairs)  97.6 us
  transfers between devices with their start and end apart: 31, of which 16 were waited for; matrix products, arithmetic and copies ran while one was open for 1% of the time, Pallas kernels for 0%

profile of v1, /device:TPU:8, one launch (start us, length us, event | category | flops | bytes accessed | tf_op | source)
XLA Modules:
  0.0 234.4 jit_solution(2271303233467803697)
XLA Ops:
  0.0 1.0 add_multiply_fusion
  1.0 0.3 fusion.24
  1.4 0.1 copy.424
  1.6 10.9 %collective-permute-start.2 = (f32[2,4,45]{2,1,0:T(4,128)S(1)}, f32[2,4,45]{2,1,0:T(4,128)S(1)}, u32[]{:S(2)}, u32[]{:S(2)}) collective-permute-start(f32[2,4,45]{2,1,0:T(4,128)S(1)} %broadcast_select_fusion.1), channel_id=1, source_target_pairs={{0,256},{4,260},{8,264},{12,268},{16,272},{20,276},{24,280},{28,28... | collective-permute-start | bytes 4328 | tf_op jit(solution)/shard_map/ppermute | solution.py:12
  12.5 3.5 %collective-permute-start.3 = (f32[2,4,45]{2,1,0:T(4,128)S(1)}, f32[2,4,45]{2,1,0:T(4,128)S(1)}, u32[]{:S(2)}, u32[]{:S(2)}) collective-permute-start(f32[2,4,45]{2,1,0:T(4,128)S(1)} %bitcast.57), channel_id=1, source_target_pairs={{0,1},{1,2},{2,3},{3,0},{4,5},{5,6},{6,7},{7,4},{8,9},{9,10},{10,1... | collective-permute-start | bytes 4328 | tf_op jit(solution)/shard_map/ppermute | solution.py:12
  16.0 2.4 %collective-permute-start.4 = (f32[2,4,45]{2,1,0:T(4,128)S(1)}, f32[2,4,45]{2,1,0:T(4,128)S(1)}, u32[]{:S(2)}, u32[]{:S(2)}) collective-permute-start(f32[2,4,45]{2,1,0:T(4,128)S(1)} %bitcast.56), channel_id=1, source_target_pairs={{0,3},{1,0},{2,1},{3,2},{4,7},{5,4},{6,5},{7,6},{8,11},{9,8},{10,9... | collective-permute-start | bytes 4328 | tf_op jit(solution)/shard_map/ppermute | solution.py:12
  18.4 7.4 %collective-permute-start = (f32[2,4,128]{2,1,0:T(4,128)S(1)}, f32[2,4,128]{2,1,0:T(4,128)S(1)}, u32[]{:S(2)}, u32[]{:S(2)}) collective-permute-start(f32[2,4,128]{2,1,0:T(4,128)S(1)} %bitcast.60), channel_id=1, source_target_pairs={{0,508},{4,0},{8,4},{12,8},{16,12},{20,16},{24,20},{28,24},{32,28}... | collective-permute-start | bytes 12296 | tf_op jit(solution)/shard_map/ppermute | solution.py:12
  25.8 1.9 collective-permute-start.1
  27.7 0.3 fusion.23
  28.1 0.7 copy-done.1
  29.3 0.6 copy-done.2
  30.0 0.2 copy.425
  30.1 0.2 copy.426
  30.3 8.5 %collective-permute-done.1 = f32[2,4,128]{2,1,0:T(4,128)S(1)} collective-permute-done((f32[2,4,128]{2,1,0:T(4,128)S(1)}, f32[2,4,128]{2,1,0:T(4,128)S(1)}, u32[]{:S(2)}, u32[]{:S(2)}) %collective-permute-start.1) | collective-permute-done | bytes 4128 | tf_op jit(solution)/shard_map/ppermute | solution.py:12
  38.8 0.7 broadcast_multiply_fusion.1
  40.4 1.9 collective-permute-start.12
  42.3 1.9 collective-permute-start.5
  44.2 9.2 %collective-permute-done.12 = f32[2,4,128]{2,1,0:T(4,128)S(1)} collective-permute-done((f32[2,4,128]{2,1,0:T(4,128)S(1)}, f32[2,4,128]{2,1,0:T(4,128)S(1)}, u32[]{:S(2)}, u32[]{:S(2)}) %collective-permute-start.12) | collective-permute-done | bytes 4128 | tf_op jit(solution)/shard_map/ppermute | solution.py:12
  53.4 1.9 collective-permute-start.13
  55.4 11.7 %collective-permute-done.13 = f32[2,4,128]{2,1,0:T(4,128)S(1)} collective-permute-done((f32[2,4,128]{2,1,0:T(4,128)S(1)}, f32[2,4,128]{2,1,0:T(4,128)S(1)}, u32[]{:S(2)}, u32[]{:S(2)}) %collective-permute-start.13) | collective-permute-done | bytes 4128 | tf_op jit(solution)/shard_map/ppermute | solution.py:12
  67.0 1.9 collective-permute-start.14
  69.0 1.9 collective-permute-start.6
  70.9 11.7 %collective-permute-done.6 = f32[2,128]{1,0:T(2,128)S(1)} collective-permute-done((f32[2,128]{1,0:T(2,128)S(1)}, f32[2,128]{1,0:T(2,128)S(1)}, u32[]{:S(2)}, u32[]{:S(2)}) %collective-permute-start.6) | collective-permute-done | bytes 1056 | tf_op jit(solution)/shard_map/ppermute | solution.py:12
  82.6 1.9 collective-permute-start.15
  84.5 1.9 collective-permute-start.7
  86.4 6.9 %collective-permute-done.7 = f32[2,128]{1,0:T(2,128)S(1)} collective-permute-done((f32[2,128]{1,0:T(2,128)S(1)}, f32[2,128]{1,0:T(2,128)S(1)}, u32[]{:S(2)}, u32[]{:S(2)}) %collective-permute-start.7) | collective-permute-done | bytes 1056 | tf_op jit(solution)/shard_map/ppermute | solution.py:12
  93.3 1.9 collective-permute-start.16
  95.2 1.9 collective-permute-start.8
  97.2 7.1 %collective-permute-done.8 = f32[2,128]{1,0:T(2,128)S(1)} collective-permute-done((f32[2,128]{1,0:T(2,128)S(1)}, f32[2,128]{1,0:T(2,128)S(1)}, u32[]{:S(2)}, u32[]{:S(2)}) %collective-permute-start.8) | collective-permute-done | bytes 1056 | tf_op jit(solution)/shard_map/ppermute | solution.py:12
  104.3 1.9 collective-permute-start.9
  106.2 4.7 %collective-permute-done.9 = f32[2,128]{1,0:T(2,128)S(1)} collective-permute-done((f32[2,128]{1,0:T(2,128)S(1)}, f32[2,128]{1,0:T(2,128)S(1)}, u32[]{:S(2)}, u32[]{:S(2)}) %collective-permute-start.9) | collective-permute-done | bytes 1056 | tf_op jit(solution)/shard_map/ppermute | solution.py:12
  111.0 4.1 %collective-permute-start.10 = (f32[2,128]{1,0:T(2,128)S(1)}, f32[2,128]{1,0:T(2,128)S(1)}, u32[]{:S(2)}, u32[]{:S(2)}) collective-permute-start(f32[2,128]{1,0:T(2,128)S(1)} %mul.527), channel_id=1, source_target_pairs={{0,128},{4,132},{8,136},{12,140},{16,144},{20,148},{24,152},{28,15... | collective-permute-start | bytes 3080 | tf_op jit(solution)/shard_map/ppermute | solution.py:12
  115.1 6.0 %collective-permute-start.17 = (f32[2,4,128]{2,1,0:T(4,128)S(1)}, f32[2,4,128]{2,1,0:T(4,128)S(1)}, u32[]{:S(2)}, u32[]{:S(2)}) collective-permute-start(f32[2,4,128]{2,1,0:T(4,128)S(1)} %multiply_add_fusion.19), channel_id=1, source_target_pairs={{0,128},{4,132},{8,136},{12,140},{16,144},{20,148},{24,152},{28,15... | collective-permute-start | bytes 12296 | tf_op jit(solution)/shard_map/ppermute | solution.py:12
  121.2 5.0 %collective-permute-start.11 = (f32[2,128]{1,0:T(2,128)S(1)}, f32[2,128]{1,0:T(2,128)S(1)}, u32[]{:S(2)}, u32[]{:S(2)}) collective-permute-start(f32[2,128]{1,0:T(2,128)S(1)} %mul.529), channel_id=1, source_target_pairs={{0,256},{4,260},{8,264},{12,268},{16,272},{20,276},{24,280},{28,28... | collective-permute-start | bytes 3080 | tf_op jit(solution)/shard_map/ppermute | solution.py:12
  126.2 4.7 %collective-permute-start.18 = (f32[2,4,128]{2,1,0:T(4,128)S(1)}, f32[2,4,128]{2,1,0:T(4,128)S(1)}, u32[]{:S(2)}, u32[]{:S(2)}) collective-permute-start(f32[2,4,128]{2,1,0:T(4,128)S(1)} %multiply_add_fusion.18), channel_id=1, source_target_pairs={{0,256},{4,260},{8,264},{12,268},{16,272},{20,276},{24,280},{28,28... | collective-permute-start | bytes 12296 | tf_op jit(solution)/shard_map/ppermute | solution.py:12
  131.0 4.6 %collective-permute-done.18 = f32[2,4,128]{2,1,0:T(4,128)S(1)} collective-permute-done((f32[2,4,128]{2,1,0:T(4,128)S(1)}, f32[2,4,128]{2,1,0:T(4,128)S(1)}, u32[]{:S(2)}, u32[]{:S(2)}) %collective-permute-start.18) | collective-permute-done | bytes 4128 | tf_op jit(solution)/shard_map/ppermute | solution.py:12
  135.7 0.2 broadcast_multiply_fusion.2
  135.9 0.3 fusion.20
  136.1 0.3 fusion.19
  136.7 0.1 copy.436
  136.8 4.7 %collective-permute-start.21 = (f32[2,4,45]{2,1,0:T(4,128)S(1)}, f32[2,4,45]{2,1,0:T(4,128)S(1)}, u32[]{:S(2)}, u32[]{:S(2)}) collective-permute-start(f32[2,4,45]{2,1,0:T(4,128)S(1)} %broadcast_select_fusion), channel_id=1, source_target_pairs={{0,256},{4,260},{8,264},{12,268},{16,272},{20,276},{24,280},{28,28... | collective-permute-start | bytes 4328 | tf_op jit(solution)/shard_map/ppermute | solution.py:12
  141.6 2.6 %collective-permute-start.22 = (f32[2,4,45]{2,1,0:T(4,128)S(1)}, f32[2,4,45]{2,1,0:T(4,128)S(1)}, u32[]{:S(2)}, u32[]{:S(2)}) collective-permute-start(f32[2,4,45]{2,1,0:T(4,128)S(1)} %bitcast.59), channel_id=1, source_target_pairs={{0,1},{1,2},{2,3},{3,0},{4,5},{5,6},{6,7},{7,4},{8,9},{9,10},{10,1... | collective-permute-start | bytes 4328 | tf_op jit(solution)/shard_map/ppermute | solution.py:12
  144.2 4.4 %collective-permute-start.23 = (f32[2,4,45]{2,1,0:T(4,128)S(1)}, f32[2,4,45]{2,1,0:T(4,128)S(1)}, u32[]{:S(2)}, u32[]{:S(2)}) collective-permute-start(f32[2,4,45]{2,1,0:T(4,128)S(1)} %bitcast.58), channel_id=1, source_target_pairs={{0,3},{1,0},{2,1},{3,2},{4,7},{5,4},{6,5},{7,6},{8,11},{9,8},{10,9... | collective-permute-start | bytes 4328 | tf_op jit(solution)/shard_map/ppermute | solution.py:12
  148.6 1.9 collective-permute-start.19
  150.6 2.4 %collective-permute-start.20 = (f32[2,4,128]{2,1,0:T(4,128)S(1)}, f32[2,4,128]{2,1,0:T(4,128)S(1)}, u32[]{:S(2)}, u32[]{:S(2)}) collective-permute-start(f32[2,4,128]{2,1,0:T(4,128)S(1)} %bitcast.66), channel_id=1, source_target_pairs={{0,4},{4,8},{8,12},{12,16},{16,20},{20,24},{24,28},{28,32},{32,36}... | collective-permute-start | bytes 12296 | tf_op jit(solution)/shard_map/ppermute | solution.py:12
  153.1 0.2 copy.437
  153.2 0.2 copy.438
  153.4 10.2 %collective-permute-done.20 = f32[2,4,128]{2,1,0:T(4,128)S(1)} collective-permute-done((f32[2,4,128]{2,1,0:T(4,128)S(1)}, f32[2,4,128]{2,1,0:T(4,128)S(1)}, u32[]{:S(2)}, u32[]{:S(2)}) %collective-permute-start.20) | collective-permute-done | bytes 4128 | tf_op jit(solution)/shard_map/ppermute | solution.py:12
  163.6 0.8 broadcast_multiply_fusion
  165.2 1.9 collective-permute-start.24
  167.2 11.1 %collective-permute-done.24 = f32[2,4,128]{2,1,0:T(4,128)S(1)} collective-permute-done((f32[2,4,128]{2,1,0:T(4,128)S(1)}, f32[2,4,128]{2,1,0:T(4,128)S(1)}, u32[]{:S(2)}, u32[]{:S(2)}) %collective-permute-start.24) | collective-permute-done | bytes 4128 | tf_op jit(solution)/shard_map/ppermute | solution.py:12
  178.3 1.9 collective-permute-start.25
  180.2 11.7 %collective-permute-done.25 = f32[2,4,128]{2,1,0:T(4,128)S(1)} collective-permute-done((f32[2,4,128]{2,1,0:T(4,128)S(1)}, f32[2,4,128]{2,1,0:T(4,128)S(1)}, u32[]{:S(2)}, u32[]{:S(2)}) %collective-permute-start.25) | collective-permute-done | bytes 4128 | tf_op jit(solution)/shard_map/ppermute | solution.py:12
  191.9 1.9 collective-permute-start.26
  193.8 6.9 %collective-permute-done.26 = f32[2,4,128]{2,1,0:T(4,128)S(1)} collective-permute-done((f32[2,4,128]{2,1,0:T(4,128)S(1)}, f32[2,4,128]{2,1,0:T(4,128)S(1)}, u32[]{:S(2)}, u32[]{:S(2)}) %collective-permute-start.26) | collective-permute-done | bytes 4128 | tf_op jit(solution)/shard_map/ppermute | solution.py:12
  200.7 1.9 collective-permute-start.27
  202.6 7.2 %collective-permute-done.27 = f32[2,4,128]{2,1,0:T(4,128)S(1)} collective-permute-done((f32[2,4,128]{2,1,0:T(4,128)S(1)}, f32[2,4,128]{2,1,0:T(4,128)S(1)}, u32[]{:S(2)}, u32[]{:S(2)}) %collective-permute-start.27) | collective-permute-done | bytes 4128 | tf_op jit(solution)/shard_map/ppermute | solution.py:12
  209.8 1.9 collective-permute-start.28
  211.8 4.8 %collective-permute-done.28 = f32[2,4,128]{2,1,0:T(4,128)S(1)} collective-permute-done((f32[2,4,128]{2,1,0:T(4,128)S(1)}, f32[2,4,128]{2,1,0:T(4,128)S(1)}, u32[]{:S(2)}, u32[]{:S(2)}) %collective-permute-start.28) | collective-permute-done | bytes 4128 | tf_op jit(solution)/shard_map/ppermute | solution.py:12
  216.5 1.9 collective-permute-start.29
  218.5 5.7 %collective-permute-done.29 = f32[2,4,128]{2,1,0:T(4,128)S(1)} collective-permute-done((f32[2,4,128]{2,1,0:T(4,128)S(1)}, f32[2,4,128]{2,1,0:T(4,128)S(1)}, u32[]{:S(2)}, u32[]{:S(2)}) %collective-permute-start.29) | collective-permute-done | bytes 4128 | tf_op jit(solution)/shard_map/ppermute | solution.py:12
  224.1 5.0 %collective-permute-start.30 = (f32[2,4,128]{2,1,0:T(4,128)S(1)}, f32[2,4,128]{2,1,0:T(4,128)S(1)}, u32[]{:S(2)}, u32[]{:S(2)}) collective-permute-start(f32[2,4,128]{2,1,0:T(4,128)S(1)} %multiply_add_fusion.12), channel_id=1, source_target_pairs={{0,256},{4,260},{8,264},{12,268},{16,272},{20,276},{24,280},{28,28... | collective-permute-start | bytes 12296 | tf_op jit(solution)/shard_map/ppermute | solution.py:12
  229.1 4.4 %collective-permute-done.30 = f32[2,4,128]{2,1,0:T(4,128)S(1)} collective-permute-done((f32[2,4,128]{2,1,0:T(4,128)S(1)}, f32[2,4,128]{2,1,0:T(4,128)S(1)}, u32[]{:S(2)}, u32[]{:S(2)}) %collective-permute-start.30) | collective-permute-done | bytes 4128 | tf_op jit(solution)/shard_map/ppermute | solution.py:12
  233.7 0.7 copy.442
  (111 shorter events, 2.8 us)
Async XLA Ops:
  1.6 27.7 %collective-permute-start.2 = (f32[2,4,45]{2,1,0:T(4,128)S(1)}, f32[2,4,45]{2,1,0:T(4,128)S(1)}, u32[]{:S(2)}, u32[]{:S(2)}) collective-permute-start(f32[2,4,45]{2,1,0:T(4,128)S(1)} %broadcast_select_fusion.1), channel_id=1, source_target_pairs={{0,256},{4,260},{8,264},{12,268},{16,272},{20,276},{24,280},{28,28... | collective-permute-start | bytes 4328 | tf_op jit(solution)/shard_map/ppermute | solution.py:12
  12.5 16.8 %collective-permute-start.3 = (f32[2,4,45]{2,1,0:T(4,128)S(1)}, f32[2,4,45]{2,1,0:T(4,128)S(1)}, u32[]{:S(2)}, u32[]{:S(2)}) collective-permute-start(f32[2,4,45]{2,1,0:T(4,128)S(1)} %bitcast.57), channel_id=1, source_target_pairs={{0,1},{1,2},{2,3},{3,0},{4,5},{5,6},{6,7},{7,4},{8,9},{9,10},{10,1... | collective-permute-start | bytes 4328 | tf_op jit(solution)/shard_map/ppermute | solution.py:12
  16.0 13.3 %collective-permute-start.4 = (f32[2,4,45]{2,1,0:T(4,128)S(1)}, f32[2,4,45]{2,1,0:T(4,128)S(1)}, u32[]{:S(2)}, u32[]{:S(2)}) collective-permute-start(f32[2,4,45]{2,1,0:T(4,128)S(1)} %bitcast.56), channel_id=1, source_target_pairs={{0,3},{1,0},{2,1},{3,2},{4,7},{5,4},{6,5},{7,6},{8,11},{9,8},{10,9... | collective-permute-start | bytes 4328 | tf_op jit(solution)/shard_map/ppermute | solution.py:12
  18.4 11.9 %collective-permute-start = (f32[2,4,128]{2,1,0:T(4,128)S(1)}, f32[2,4,128]{2,1,0:T(4,128)S(1)}, u32[]{:S(2)}, u32[]{:S(2)}) collective-permute-start(f32[2,4,128]{2,1,0:T(4,128)S(1)} %bitcast.60), channel_id=1, source_target_pairs={{0,508},{4,0},{8,4},{12,8},{16,12},{20,16},{24,20},{28,24},{32,28}... | collective-permute-start | bytes 12296 | tf_op jit(solution)/shard_map/ppermute | solution.py:12
  25.8 13.1 %collective-permute-start.1 = (f32[2,4,128]{2,1,0:T(4,128)S(1)}, f32[2,4,128]{2,1,0:T(4,128)S(1)}, u32[]{:S(2)}, u32[]{:S(2)}) collective-permute-start(f32[2,4,128]{2,1,0:T(4,128)S(1)} %bitcast.62), channel_id=1, source_target_pairs={{0,4},{4,8},{8,12},{12,16},{16,20},{20,24},{24,28},{28,32},{32,36}... | collective-permute-start | bytes 12296 | tf_op jit(solution)/shard_map/ppermute | solution.py:12
  28.0 0.8 copy-start.1
  29.2 0.7 copy-start.2
  29.9 8.9 %copy-start = (f32[2,4,45,128]{3,1,2,0:T(4,128)S(1)}, f32[2,4,45,128]{3,1,2,0:T(4,128)}, u32[]{:S(2)}) copy-start(f32[2,4,45,128]{3,1,2,0:T(4,128)} %param.5) | copy-start | bytes 552964
  40.4 13.1 %collective-permute-start.12 = (f32[2,4,128]{2,1,0:T(4,128)S(1)}, f32[2,4,128]{2,1,0:T(4,128)S(1)}, u32[]{:S(2)}, u32[]{:S(2)}) collective-permute-start(f32[2,4,128]{2,1,0:T(4,128)S(1)} %bitcast.68), channel_id=1, source_target_pairs={{0,4},{4,8},{8,12},{12,16},{16,20},{20,24},{24,28},{28,32},{32,36}... | collective-permute-start | bytes 12296 | tf_op jit(solution)/shard_map/ppermute | solution.py:12
  42.3 13.0 %collective-permute-start.5 = (f32[2,128]{1,0:T(2,128)S(1)}, f32[2,128]{1,0:T(2,128)S(1)}, u32[]{:S(2)}, u32[]{:S(2)}) collective-permute-start(f32[2,128]{1,0:T(2,128)S(1)} %slice_bitcast_fusion), channel_id=1, source_target_pairs={{0,4},{4,8},{8,12},{12,16},{16,20},{20,24},{24,28},{28,32},{32,36}... | collective-permute-start | bytes 3080 | tf_op jit(solution)/shard_map/ppermute | solution.py:12
  53.4 13.6 %collective-permute-start.13 = (f32[2,4,128]{2,1,0:T(4,128)S(1)}, f32[2,4,128]{2,1,0:T(4,128)S(1)}, u32[]{:S(2)}, u32[]{:S(2)}) collective-permute-start(f32[2,4,128]{2,1,0:T(4,128)S(1)} %multiply_add_fusion.23), channel_id=1, source_target_pairs={{0,8},{4,12},{8,16},{12,20},{16,24},{20,28},{24,32},{28,36},{32,40... | collective-permute-start | bytes 12296 | tf_op jit(solution)/shard_map/ppermute | solution.py:12
  67.0 15.5 %collective-permute-start.14 = (f32[2,4,128]{2,1,0:T(4,128)S(1)}, f32[2,4,128]{2,1,0:T(4,128)S(1)}, u32[]{:S(2)}, u32[]{:S(2)}) collective-permute-start(f32[2,4,128]{2,1,0:T(4,128)S(1)} %multiply_add_fusion.22), channel_id=1, source_target_pairs={{0,16},{4,20},{8,24},{12,28},{16,32},{20,36},{24,40},{28,44},{32,4... | collective-permute-start | bytes 12296 | tf_op jit(solution)/shard_map/ppermute | solution.py:12
  69.0 13.6 %collective-permute-start.6 = (f32[2,128]{1,0:T(2,128)S(1)}, f32[2,128]{1,0:T(2,128)S(1)}, u32[]{:S(2)}, u32[]{:S(2)}) collective-permute-start(f32[2,128]{1,0:T(2,128)S(1)} %fusion.13), channel_id=1, source_target_pairs={{0,8},{4,12},{8,16},{12,20},{16,24},{20,28},{24,32},{28,36},{32,40... | collective-permute-start | bytes 3080 | tf_op jit(solution)/shard_map/ppermute | solution.py:12
  82.6 10.7 %collective-permute-start.15 = (f32[2,4,128]{2,1,0:T(4,128)S(1)}, f32[2,4,128]{2,1,0:T(4,128)S(1)}, u32[]{:S(2)}, u32[]{:S(2)}) collective-permute-start(f32[2,4,128]{2,1,0:T(4,128)S(1)} %multiply_add_fusion.21), channel_id=1, source_target_pairs={{0,32},{4,36},{8,40},{12,44},{16,48},{20,52},{24,56},{28,60},{32,6... | collective-permute-start | bytes 12296 | tf_op jit(solution)/shard_map/ppermute | solution.py:12
  84.5 8.8 %collective-permute-start.7 = (f32[2,128]{1,0:T(2,128)S(1)}, f32[2,128]{1,0:T(2,128)S(1)}, u32[]{:S(2)}, u32[]{:S(2)}) collective-permute-start(f32[2,128]{1,0:T(2,128)S(1)} %mul.521), channel_id=1, source_target_pairs={{0,16},{4,20},{8,24},{12,28},{16,32},{20,36},{24,40},{28,44},{32,4... | collective-permute-start | bytes 3080 | tf_op jit(solution)/shard_map/ppermute | solution.py:12
  93.3 21.8 %collective-permute-start.16 = (f32[2,4,128]{2,1,0:T(4,128)S(1)}, f32[2,4,128]{2,1,0:T(4,128)S(1)}, u32[]{:S(2)}, u32[]{:S(2)}) collective-permute-start(f32[2,4,128]{2,1,0:T(4,128)S(1)} %multiply_add_fusion.20), channel_id=1, source_target_pairs={{0,64},{4,68},{8,72},{12,76},{16,80},{20,84},{24,88},{28,92},{32,9... | collective-permute-start | bytes 12296 | tf_op jit(solution)/shard_map/ppermute | solution.py:12
  95.2 9.1 %collective-permute-start.8 = (f32[2,128]{1,0:T(2,128)S(1)}, f32[2,128]{1,0:T(2,128)S(1)}, u32[]{:S(2)}, u32[]{:S(2)}) collective-permute-start(f32[2,128]{1,0:T(2,128)S(1)} %mul.523), channel_id=1, source_target_pairs={{0,32},{4,36},{8,40},{12,44},{16,48},{20,52},{24,56},{28,60},{32,6... | collective-permute-start | bytes 3080 | tf_op jit(solution)/shard_map/ppermute | solution.py:12
  104.3 6.7 %collective-permute-start.9 = (f32[2,128]{1,0:T(2,128)S(1)}, f32[2,128]{1,0:T(2,128)S(1)}, u32[]{:S(2)}, u32[]{:S(2)}) collective-permute-start(f32[2,128]{1,0:T(2,128)S(1)} %mul.525), channel_id=1, source_target_pairs={{0,64},{4,68},{8,72},{12,76},{16,80},{20,84},{24,88},{28,92},{32,9... | collective-permute-start | bytes 3080 | tf_op jit(solution)/shard_map/ppermute | solution.py:12
  111.0 10.2 %copy-start.3 = (s32[128]{0:T(128)S(1)}, s32[128]{0:T(128)}, u32[]{:S(2)}) copy-start(s32[128]{0:T(128)} %param.7) | copy-start | bytes 1540
  111.0 10.2 %collective-permute-start.10 = (f32[2,128]{1,0:T(2,128)S(1)}, f32[2,128]{1,0:T(2,128)S(1)}, u32[]{:S(2)}, u32[]{:S(2)}) collective-permute-start(f32[2,128]{1,0:T(2,128)S(1)} %mul.527), channel_id=1, source_target_pairs={{0,128},{4,132},{8,136},{12,140},{16,144},{20,148},{24,152},{28,15... | collective-permute-start | bytes 3080 | tf_op jit(solution)/shard_map/ppermute | solution.py:12
  115.1 11.1 %collective-permute-start.17 = (f32[2,4,128]{2,1,0:T(4,128)S(1)}, f32[2,4,128]{2,1,0:T(4,128)S(1)}, u32[]{:S(2)}, u32[]{:S(2)}) collective-permute-start(f32[2,4,128]{2,1,0:T(4,128)S(1)} %multiply_add_fusion.19), channel_id=1, source_target_pairs={{0,128},{4,132},{8,136},{12,140},{16,144},{20,148},{24,152},{28,15... | collective-permute-start | bytes 12296 | tf_op jit(solution)/shard_map/ppermute | solution.py:12
  121.2 9.8 %collective-permute-start.11 = (f32[2,128]{1,0:T(2,128)S(1)}, f32[2,128]{1,0:T(2,128)S(1)}, u32[]{:S(2)}, u32[]{:S(2)}) collective-permute-start(f32[2,128]{1,0:T(2,128)S(1)} %mul.529), channel_id=1, source_target_pairs={{0,256},{4,260},{8,264},{12,268},{16,272},{20,276},{24,280},{28,28... | collective-permute-start | bytes 3080 | tf_op jit(solution)/shard_map/ppermute | solution.py:12
  126.2 9.4 %collective-permute-start.18 = (f32[2,4,128]{2,1,0:T(4,128)S(1)}, f32[2,4,128]{2,1,0:T(4,128)S(1)}, u32[]{:S(2)}, u32[]{:S(2)}) collective-permute-start(f32[2,4,128]{2,1,0:T(4,128)S(1)} %multiply_add_fusion.18), channel_id=1, source_target_pairs={{0,256},{4,260},{8,264},{12,268},{16,272},{20,276},{24,280},{28,28... | collective-permute-start | bytes 12296 | tf_op jit(solution)/shard_map/ppermute | solution.py:12
  136.8 16.1 %collective-permute-start.21 = (f32[2,4,45]{2,1,0:T(4,128)S(1)}, f32[2,4,45]{2,1,0:T(4,128)S(1)}, u32[]{:S(2)}, u32[]{:S(2)}) collective-permute-start(f32[2,4,45]{2,1,0:T(4,128)S(1)} %broadcast_select_fusion), channel_id=1, source_target_pairs={{0,256},{4,260},{8,264},{12,268},{16,272},{20,276},{24,280},{28,28... | collective-permute-start | bytes 4328 | tf_op jit(solution)/shard_map/ppermute | solution.py:12
  141.6 11.4 %collective-permute-start.22 = (f32[2,4,45]{2,1,0:T(4,128)S(1)}, f32[2,4,45]{2,1,0:T(4,128)S(1)}, u32[]{:S(2)}, u32[]{:S(2)}) collective-permute-start(f32[2,4,45]{2,1,0:T(4,128)S(1)} %bitcast.59), channel_id=1, source_target_pairs={{0,1},{1,2},{2,3},{3,0},{4,5},{5,6},{6,7},{7,4},{8,9},{9,10},{10,1... | collective-permute-start | bytes 4328 | tf_op jit(solution)/shard_map/ppermute | solution.py:12
  144.2 8.8 %collective-permute-start.23 = (f32[2,4,45]{2,1,0:T(4,128)S(1)}, f32[2,4,45]{2,1,0:T(4,128)S(1)}, u32[]{:S(2)}, u32[]{:S(2)}) collective-permute-start(f32[2,4,45]{2,1,0:T(4,128)S(1)} %bitcast.58), channel_id=1, source_target_pairs={{0,3},{1,0},{2,1},{3,2},{4,7},{5,4},{6,5},{7,6},{8,11},{9,8},{10,9... | collective-permute-start | bytes 4328 | tf_op jit(solution)/shard_map/ppermute | solution.py:12
  148.6 4.8 %collective-permute-start.19 = (f32[2,4,128]{2,1,0:T(4,128)S(1)}, f32[2,4,128]{2,1,0:T(4,128)S(1)}, u32[]{:S(2)}, u32[]{:S(2)}) collective-permute-start(f32[2,4,128]{2,1,0:T(4,128)S(1)} %bitcast.64), channel_id=1, source_target_pairs={{0,508},{4,0},{8,4},{12,8},{16,12},{20,16},{24,20},{28,24},{32,28}... | collective-permute-start | bytes 12296 | tf_op jit(solution)/shard_map/ppermute | solution.py:12
  150.6 13.1 %collective-permute-start.20 = (f32[2,4,128]{2,1,0:T(4,128)S(1)}, f32[2,4,128]{2,1,0:T(4,128)S(1)}, u32[]{:S(2)}, u32[]{:S(2)}) collective-permute-start(f32[2,4,128]{2,1,0:T(4,128)S(1)} %bitcast.66), channel_id=1, source_target_pairs={{0,4},{4,8},{8,12},{12,16},{16,20},{20,24},{24,28},{28,32},{32,36}... | collective-permute-start | bytes 12296 | tf_op jit(solution)/shard_map/ppermute | solution.py:12
  165.2 13.1 %collective-permute-start.24 = (f32[2,4,128]{2,1,0:T(4,128)S(1)}, f32[2,4,128]{2,1,0:T(4,128)S(1)}, u32[]{:S(2)}, u32[]{:S(2)}) collective-permute-start(f32[2,4,128]{2,1,0:T(4,128)S(1)} %bitcast.69), channel_id=1, source_target_pairs={{0,4},{4,8},{8,12},{12,16},{16,20},{20,24},{24,28},{28,32},{32,36}... | collective-permute-start | bytes 12296 | tf_op jit(solution)/shard_map/ppermute | solution.py:12
  178.3 13.6 %collective-permute-start.25 = (f32[2,4,128]{2,1,0:T(4,128)S(1)}, f32[2,4,128]{2,1,0:T(4,128)S(1)}, u32[]{:S(2)}, u32[]{:S(2)}) collective-permute-start(f32[2,4,128]{2,1,0:T(4,128)S(1)} %multiply_add_fusion.17), channel_id=1, source_target_pairs={{0,8},{4,12},{8,16},{12,20},{16,24},{20,28},{24,32},{28,36},{32,40... | collective-permute-start | bytes 12296 | tf_op jit(solution)/shard_map/ppermute | solution.py:12
  191.9 8.8 %collective-permute-start.26 = (f32[2,4,128]{2,1,0:T(4,128)S(1)}, f32[2,4,128]{2,1,0:T(4,128)S(1)}, u32[]{:S(2)}, u32[]{:S(2)}) collective-permute-start(f32[2,4,128]{2,1,0:T(4,128)S(1)} %multiply_add_fusion.16), channel_id=1, source_target_pairs={{0,16},{4,20},{8,24},{12,28},{16,32},{20,36},{24,40},{28,44},{32,4... | collective-permute-start | bytes 12296 | tf_op jit(solution)/shard_map/ppermute | solution.py:12
  200.7 9.1 %collective-permute-start.27 = (f32[2,4,128]{2,1,0:T(4,128)S(1)}, f32[2,4,128]{2,1,0:T(4,128)S(1)}, u32[]{:S(2)}, u32[]{:S(2)}) collective-permute-start(f32[2,4,128]{2,1,0:T(4,128)S(1)} %multiply_add_fusion.15), channel_id=1, source_target_pairs={{0,32},{4,36},{8,40},{12,44},{16,48},{20,52},{24,56},{28,60},{32,6... | collective-permute-start | bytes 12296 | tf_op jit(solution)/shard_map/ppermute | solution.py:12
  209.8 6.7 %collective-permute-start.28 = (f32[2,4,128]{2,1,0:T(4,128)S(1)}, f32[2,4,128]{2,1,0:T(4,128)S(1)}, u32[]{:S(2)}, u32[]{:S(2)}) collective-permute-start(f32[2,4,128]{2,1,0:T(4,128)S(1)} %multiply_add_fusion.14), channel_id=1, source_target_pairs={{0,64},{4,68},{8,72},{12,76},{16,80},{20,84},{24,88},{28,92},{32,9... | collective-permute-start | bytes 12296 | tf_op jit(solution)/shard_map/ppermute | solution.py:12
  216.5 7.6 %collective-permute-start.29 = (f32[2,4,128]{2,1,0:T(4,128)S(1)}, f32[2,4,128]{2,1,0:T(4,128)S(1)}, u32[]{:S(2)}, u32[]{:S(2)}) collective-permute-start(f32[2,4,128]{2,1,0:T(4,128)S(1)} %multiply_add_fusion.13), channel_id=1, source_target_pairs={{0,128},{4,132},{8,136},{12,140},{16,144},{20,148},{24,152},{28,15... | collective-permute-start | bytes 12296 | tf_op jit(solution)/shard_map/ppermute | solution.py:12
  224.1 9.4 %collective-permute-start.30 = (f32[2,4,128]{2,1,0:T(4,128)S(1)}, f32[2,4,128]{2,1,0:T(4,128)S(1)}, u32[]{:S(2)}, u32[]{:S(2)}) collective-permute-start(f32[2,4,128]{2,1,0:T(4,128)S(1)} %multiply_add_fusion.12), channel_id=1, source_target_pairs={{0,256},{4,260},{8,264},{12,268},{16,272},{20,276},{24,280},{28,28... | collective-permute-start | bytes 12296 | tf_op jit(solution)/shard_map/ppermute | solution.py:12

commit v2 on v1

--- a/solution.py
+++ b/solution.py
@@ -4,6 +4,7 @@
 from jax.sharding import PartitionSpec as P
 
 ITERS = 2
+RADIX = 4
 
 
 def from_behind(value, axis, steps):
@@ -36,41 +37,84 @@
     return source
 
 
-def lon_rates(gain):
-    count = lax.axis_size("lon")
-    rounds = []
-    window = gain
-    excl = jnp.ones_like(gain)
+def scan_plan(count):
+    plan = []
     span = 1
     while span < count:
-        rounds.append((span, window, excl))
-        got = from_behind(window, "lon", span)
-        excl = excl * got
-        window = window * got
-        span *= 2
-    return rounds, excl
+        radix = min(RADIX, count // span)
+        plan.append((span, radix))
+        span *= radix
+    assert span == count
+    return plan
 
 
-def inflow(rounds, excl, gain, ends):
-    window = ends
-    excl_b = jnp.zeros_like(ends)
-    for span, rate_w, rate_e in rounds:
-        got = from_behind(window, "lon", span)
-        excl_b = rate_e[:, None] * got + excl_b
-        window = rate_w[:, None] * got + window
-    return (excl[:, None] * ends + excl_b) / (1.0 - excl * gain)[:, None]
+def lon_inflow(gain, ends, saved):
+    count = lax.axis_size("lon")
+    first = saved is None
+    if first:
+        saved = []
+        rate_w, rate_e = gain, jnp.ones_like(gain)
+    window, excl = ends, jnp.zeros_like(ends)
+    for number, (span, radix) in enumerate(scan_plan(count)):
+        if first:
+            message = jnp.concatenate([window, rate_w[:, None]], axis=1)
+        else:
+            message = window
+        got = [from_behind(message, "lon", span * j) for j in range(1, radix)]
+        if first:
+            rates = [g[:, -1] for g in got]
+            got = [g[:, :-1] for g in got]
+            saved.append((rate_w, rate_e, rates))
+        else:
+            rate_w, rate_e, rates = saved[number]
+        joined_b = got[-1]
+        joined_a = rates[-1]
+        for j in range(len(got) - 2, -1, -1):
+            joined_b = rates[j][:, None] * joined_b + got[j]
+            joined_a = rates[j] * joined_a
+        excl = rate_e[:, None] * joined_b + excl
+        window = rate_w[:, None] * joined_b + window
+        if first:
+            rate_e = rate_e * joined_a
+            rate_w = rate_w * joined_a
+    if first:
+        saved.append(rate_e)
+    rate_e = saved[-1]
+    entry = (rate_e[:, None] * ends + excl) / (1.0 - rate_e * gain)[:, None]
+    return entry, saved
 
 
-def halo_tendency(field, turning, first_band, last_band, half_cycle):
+def halo_tendency(field, turning, lat_index, half_cycle):
+    lon_count = lax.axis_size("lon")
+    lat_count = lax.axis_size("lat")
+    assert lat_count % 2 == 0
     east = from_behind(field[:, :, 0, :], "lon", -1)
     west = from_behind(field[:, :, -1, :], "lon", 1)
-    north = from_behind(field[..., -1], "lat", 1)
-    south = from_behind(field[..., 0], "lat", -1)
-    pole_send = jnp.where(first_band, field[..., 0], field[..., -1])
-    across = from_behind(pole_send, "lon", half_cycle)
+    top = field[..., 0]
+    bottom = field[..., -1]
+    odd = lat_index % 2 == 1
+    pairs_a = []
+    pairs_b = []
+    for d in range(lon_count):
+        for l in range(lat_count):
+            me = d * lat_count + l
+            if l % 2 == 0:
+                pairs_a.append((me, d * lat_count + l + 1))
+            else:
+                pairs_a.append((me, d * lat_count + l - 1))
+            if l == 0 or l == lat_count - 1:
+                pairs_b.append((me, ((d + half_cycle) % lon_count) * lat_count + l))
+            elif l % 2 == 1:
+                pairs_b.append((me, d * lat_count + l + 1))
+            else:
+                pairs_b.append((me, d * lat_count + l - 1))
+    got_a = lax.ppermute(jnp.where(odd, top, bottom), ("lon", "lat"), pairs_a)
+    got_b = lax.ppermute(jnp.where(odd, bottom, top), ("lon", "lat"), pairs_b)
     flips = jnp.array([-1.0, -1.0, 1.0, 1.0], jnp.float32)[None, :, None]
-    north = jnp.where(first_band, across * flips, north)
-    south = jnp.where(last_band, across * flips, south)
+    pole = (lat_index == 0) | (lat_index == lat_count - 1)
+    got_b = jnp.where(pole, got_b * flips, got_b)
+    north = jnp.where(odd, got_a, got_b)
+    south = jnp.where(odd, got_b, got_a)
     north_rows = jnp.concatenate([north[..., None], field[..., :-1]], axis=3)
     south_rows = jnp.concatenate([field[..., 1:], south[..., None]], axis=3)
     east_cells = jnp.concatenate([field[:, :, 1:], east[:, :, None]], axis=2)
@@ -96,21 +140,19 @@
     row_ids = lat_index * rows + jnp.arange(rows, dtype=jnp.int32)
     latitude = jnp.pi / 2 - (row_ids.astype(jnp.float32) + 0.5) * jnp.pi / total_rows
     turning = 0.5 * jnp.sin(latitude)
-    first_band = lat_index == 0
-    last_band = lat_index == lat_count - 1
     inverse = 1.0 / (1.0 + courant)
     rate = courant * inverse
     steps, carried = block_rates(rate)
     gain = carried[:, -1, :]
-    rounds, excl = lon_rates(gain)
     in_band = (band_mask == 1)[None, None, None, :]
     estimate = state
+    saved = None
     for sweep in range(ITERS):
         middle = 0.5 * (state + estimate)
-        star = state + halo_tendency(middle, turning, first_band, last_band, half_cycle)
+        star = state + halo_tendency(middle, turning, lat_index, half_cycle)
         partial_value = block_scan(steps, star * inverse[:, None])
         ends = partial_value[:, :, -1, :]
-        entry = inflow(rounds, excl, gain, ends)
+        entry, saved = lon_inflow(gain, ends, saved)
         solved = partial_value + carried[:, None] * entry[:, :, None, :]
         estimate = jnp.where(in_band, solved, star)
     return estimate

time: 235 us -> 176 us (0.75)
  the two profiles are of different devices: /device:TPU:8 before, /device:TPU:56 now
where the time goes in v2:
time: 176 us; the launch traced here: 175 us
  starting transfers between devices  121 us (69%)
  waiting for transfers between devices  43.7 us (25%)
  other arithmetic  5.18 us (3%)
  local copies, waits for them, and re-layouts  4.65 us (3%)
    ppermute x24, starting transfers between devices, from_behind(): return lax.ppermute(value, axis, pairs)  102 us
    ppermute x24, waiting for transfers between devices, from_behind(): return lax.ppermute(value, axis, pairs)  43.6 us
    ppermute x2, starting transfers between devices, halo_tendency(): got_b = lax.ppermute(jnp.where(odd, bottom, top), ('lon', 'lat'), pairs_b)  13.7 us
    ppermute x2, starting transfers between devices, halo_tendency(): got_a = lax.ppermute(jnp.where(odd, top, bottom), ('lon', 'lat'), pairs_a)  5.18 us
  transfers between devices with their start and end apart: 28, of which 15 were waited for; matrix products, arithmetic and copies ran while one was open for 1% of the time, Pallas kernels for 0%

profile of v2, /device:TPU:56, one launch (start us, length us, event | category | flops | bytes accessed | tf_op | source)
XLA Modules:
  0.0 175.2 jit_solution(1092899480604373562)
XLA Ops:
  0.0 1.0 add_multiply_fusion
  1.0 1.9 %collective-permute-start.1 = (f32[2,4,128]{2,1,0:T(4,128)S(1)}, f32[2,4,128]{2,1,0:T(4,128)S(1)}, u32[]{:S(2)}, u32[]{:S(2)}) collective-permute-start(f32[2,4,128]{2,1,0:T(4,128)S(1)} %bitcast.99), channel_id=1, source_target_pairs={{0,4},{4,8},{8,12},{12,16},{16,20},{20,24},{24,28},{28,32},{32,36}... | collective-permute-start | bytes 12296 | tf_op jit(solution)/shard_map/ppermute | solution.py:13
  3.0 7.5 %collective-permute-start = (f32[2,4,128]{2,1,0:T(4,128)S(1)}, f32[2,4,128]{2,1,0:T(4,128)S(1)}, u32[]{:S(2)}, u32[]{:S(2)}) collective-permute-start(f32[2,4,128]{2,1,0:T(4,128)S(1)} %bitcast.101), channel_id=1, source_target_pairs={{0,508},{4,0},{8,4},{12,8},{16,12},{20,16},{24,20},{28,24},{32,28}... | collective-permute-start | bytes 12296 | tf_op jit(solution)/shard_map/ppermute | solution.py:13
  10.6 0.3 broadcast_select_fusion.2
  10.8 0.1 copy.474
  11.0 3.3 %collective-permute-start.2 = (f32[2,4,45]{2,1,0:T(4,128)S(1)}, f32[2,4,45]{2,1,0:T(4,128)S(1)}, u32[]{:S(2)}, u32[]{:S(2)}) collective-permute-start(f32[2,4,45]{2,1,0:T(4,128)S(1)} %bitcast.95), channel_id=1, source_target_pairs={{0,1},{1,0},{2,3},{3,2},{4,5},{5,4},{6,7},{7,6},{8,9},{9,8},{10,11... | collective-permute-start | bytes 4328 | tf_op jit(solution)/shard_map/ppermute | solution.py:111
  14.2 0.1 copy.475
  14.4 10.9 %collective-permute-start.3 = (f32[2,4,45]{2,1,0:T(4,128)S(1)}, f32[2,4,45]{2,1,0:T(4,128)S(1)}, u32[]{:S(2)}, u32[]{:S(2)}) collective-permute-start(f32[2,4,45]{2,1,0:T(4,128)S(1)} %bitcast.96), channel_id=1, source_target_pairs={{0,256},{1,2},{2,1},{3,259},{4,260},{5,6},{6,5},{7,263},{8,264},{9... | collective-permute-start | bytes 4328 | tf_op jit(solution)/shard_map/ppermute | solution.py:112
  25.4 0.3 fusion.34
  25.7 0.5 copy-done.1
  26.9 0.5 copy-done.2
  27.4 0.2 copy.476
  27.6 0.2 copy.477
  27.8 0.5 copy-done
  28.3 0.7 broadcast_multiply_fusion.1
  29.2 0.1 multiply_add_fusion.10
  29.9 2.3 %collective-permute-start.6 = (f32[2,5,128]{2,1,0:T(8,128)S(1)}, f32[2,5,128]{2,1,0:T(8,128)S(1)}, u32[]{:S(2)}, u32[]{:S(2)}) collective-permute-start(f32[2,5,128]{2,1,0:T(8,128)S(1)} %pad_maximum_fusion.4), channel_id=1, source_target_pairs={{0,12},{4,16},{8,20},{12,24},{16,28},{20,32},{24,36},{28,40},{32,4... | collective-permute-start | bytes 15368 | tf_op jit(solution)/shard_map/ppermute | solution.py:13
  32.2 5.3 %collective-permute-start.5 = (f32[2,5,128]{2,1,0:T(8,128)S(1)}, f32[2,5,128]{2,1,0:T(8,128)S(1)}, u32[]{:S(2)}, u32[]{:S(2)}) collective-permute-start(f32[2,5,128]{2,1,0:T(8,128)S(1)} %pad_maximum_fusion.4), channel_id=1, source_target_pairs={{0,8},{4,12},{8,16},{12,20},{16,24},{20,28},{24,32},{28,36},{32,40... | collective-permute-start | bytes 15368 | tf_op jit(solution)/shard_map/ppermute | solution.py:13
  37.4 3.2 %collective-permute-start.4 = (f32[2,5,128]{2,1,0:T(8,128)S(1)}, f32[2,5,128]{2,1,0:T(8,128)S(1)}, u32[]{:S(2)}, u32[]{:S(2)}) collective-permute-start(f32[2,5,128]{2,1,0:T(8,128)S(1)} %pad_maximum_fusion.4), channel_id=1, source_target_pairs={{0,4},{4,8},{8,12},{12,16},{16,20},{20,24},{24,28},{28,32},{32,36}... | collective-permute-start | bytes 15368 | tf_op jit(solution)/shard_map/ppermute | solution.py:13
  40.7 1.5 collective-permute-done.5
  42.2 4.2 %collective-permute-done.4 = f32[2,5,128]{2,1,0:T(8,128)S(1)} collective-permute-done((f32[2,5,128]{2,1,0:T(8,128)S(1)}, f32[2,5,128]{2,1,0:T(8,128)S(1)}, u32[]{:S(2)}, u32[]{:S(2)}) %collective-permute-start.4) | collective-permute-done | bytes 5152 | tf_op jit(solution)/shard_map/ppermute | solution.py:13
  46.4 6.7 %collective-permute-start.9 = (f32[2,5,128]{2,1,0:T(8,128)S(1)}, f32[2,5,128]{2,1,0:T(8,128)S(1)}, u32[]{:S(2)}, u32[]{:S(2)}) collective-permute-start(f32[2,5,128]{2,1,0:T(8,128)S(1)} %pad_maximum_fusion.5), channel_id=1, source_target_pairs={{0,48},{4,52},{8,56},{12,60},{16,64},{20,68},{24,72},{28,76},{32,8... | collective-permute-start | bytes 15368 | tf_op jit(solution)/shard_map/ppermute | solution.py:13
  53.0 1.9 %collective-permute-start.8 = (f32[2,5,128]{2,1,0:T(8,128)S(1)}, f32[2,5,128]{2,1,0:T(8,128)S(1)}, u32[]{:S(2)}, u32[]{:S(2)}) collective-permute-start(f32[2,5,128]{2,1,0:T(8,128)S(1)} %pad_maximum_fusion.5), channel_id=1, source_target_pairs={{0,32},{4,36},{8,40},{12,44},{16,48},{20,52},{24,56},{28,60},{32,6... | collective-permute-start | bytes 15368 | tf_op jit(solution)/shard_map/ppermute | solution.py:13
  55.0 2.8 %collective-permute-start.7 = (f32[2,5,128]{2,1,0:T(8,128)S(1)}, f32[2,5,128]{2,1,0:T(8,128)S(1)}, u32[]{:S(2)}, u32[]{:S(2)}) collective-permute-start(f32[2,5,128]{2,1,0:T(8,128)S(1)} %pad_maximum_fusion.5), channel_id=1, source_target_pairs={{0,16},{4,20},{8,24},{12,28},{16,32},{20,36},{24,40},{28,44},{32,4... | collective-permute-start | bytes 15368 | tf_op jit(solution)/shard_map/ppermute | solution.py:13
  57.8 4.4 %collective-permute-done.8 = f32[2,5,128]{2,1,0:T(8,128)S(1)} collective-permute-done((f32[2,5,128]{2,1,0:T(8,128)S(1)}, f32[2,5,128]{2,1,0:T(8,128)S(1)}, u32[]{:S(2)}, u32[]{:S(2)}) %collective-permute-start.8) | collective-permute-done | bytes 5152 | tf_op jit(solution)/shard_map/ppermute | solution.py:13
  62.2 1.6 collective-permute-done.7
  63.9 6.5 %collective-permute-start.12 = (f32[2,5,128]{2,1,0:T(8,128)S(1)}, f32[2,5,128]{2,1,0:T(8,128)S(1)}, u32[]{:S(2)}, u32[]{:S(2)}) collective-permute-start(f32[2,5,128]{2,1,0:T(8,128)S(1)} %pad_maximum_fusion.6), channel_id=1, source_target_pairs={{0,192},{4,196},{8,200},{12,204},{16,208},{20,212},{24,216},{28,22... | collective-permute-start | bytes 15368 | tf_op jit(solution)/shard_map/ppermute | solution.py:13
  70.4 3.0 %collective-permute-start.11 = (f32[2,5,128]{2,1,0:T(8,128)S(1)}, f32[2,5,128]{2,1,0:T(8,128)S(1)}, u32[]{:S(2)}, u32[]{:S(2)}) collective-permute-start(f32[2,5,128]{2,1,0:T(8,128)S(1)} %pad_maximum_fusion.6), channel_id=1, source_target_pairs={{0,128},{4,132},{8,136},{12,140},{16,144},{20,148},{24,152},{28,15... | collective-permute-start | bytes 15368 | tf_op jit(solution)/shard_map/ppermute | solution.py:13
  73.4 3.4 %collective-permute-start.10 = (f32[2,5,128]{2,1,0:T(8,128)S(1)}, f32[2,5,128]{2,1,0:T(8,128)S(1)}, u32[]{:S(2)}, u32[]{:S(2)}) collective-permute-start(f32[2,5,128]{2,1,0:T(8,128)S(1)} %pad_maximum_fusion.6), channel_id=1, source_target_pairs={{0,64},{4,68},{8,72},{12,76},{16,80},{20,84},{24,88},{28,92},{32,9... | collective-permute-start | bytes 15368 | tf_op jit(solution)/shard_map/ppermute | solution.py:13
  76.8 1.3 collective-permute-done.11
  78.1 2.1 %collective-permute-done.10 = f32[2,5,128]{2,1,0:T(8,128)S(1)} collective-permute-done((f32[2,5,128]{2,1,0:T(8,128)S(1)}, f32[2,5,128]{2,1,0:T(8,128)S(1)}, u32[]{:S(2)}, u32[]{:S(2)}) %collective-permute-start.10) | collective-permute-done | bytes 5152 | tf_op jit(solution)/shard_map/ppermute | solution.py:13
  80.2 2.8 %collective-permute-start.13 = (f32[2,5,128]{2,1,0:T(8,128)S(1)}, f32[2,5,128]{2,1,0:T(8,128)S(1)}, u32[]{:S(2)}, u32[]{:S(2)}) collective-permute-start(f32[2,5,128]{2,1,0:T(8,128)S(1)} %pad_maximum_fusion.7), channel_id=1, source_target_pairs={{0,256},{4,260},{8,264},{12,268},{16,272},{20,276},{24,280},{28,28... | collective-permute-start | bytes 15368 | tf_op jit(solution)/shard_map/ppermute | solution.py:13
  83.1 6.6 %collective-permute-done.13 = f32[2,5,128]{2,1,0:T(8,128)S(1)} collective-permute-done((f32[2,5,128]{2,1,0:T(8,128)S(1)}, f32[2,5,128]{2,1,0:T(8,128)S(1)}, u32[]{:S(2)}, u32[]{:S(2)}) %collective-permute-start.13) | collective-permute-done | bytes 5152 | tf_op jit(solution)/shard_map/ppermute | solution.py:13
  89.7 0.2 broadcast_multiply_fusion.2
  90.1 0.3 broadcast_select_fusion
  90.4 0.3 fusion.31
  90.6 0.1 copy.497
  90.8 0.1 copy.496
  90.9 1.9 %collective-permute-start.16 = (f32[2,4,45]{2,1,0:T(4,128)S(1)}, f32[2,4,45]{2,1,0:T(4,128)S(1)}, u32[]{:S(2)}, u32[]{:S(2)}) collective-permute-start(f32[2,4,45]{2,1,0:T(4,128)S(1)} %bitcast.98), channel_id=1, source_target_pairs={{0,1},{1,0},{2,3},{3,2},{4,5},{5,4},{6,7},{7,6},{8,9},{9,8},{10,11... | collective-permute-start | bytes 4328 | tf_op jit(solution)/shard_map/ppermute | solution.py:111
  92.8 2.8 %collective-permute-start.17 = (f32[2,4,45]{2,1,0:T(4,128)S(1)}, f32[2,4,45]{2,1,0:T(4,128)S(1)}, u32[]{:S(2)}, u32[]{:S(2)}) collective-permute-start(f32[2,4,45]{2,1,0:T(4,128)S(1)} %bitcast.97), channel_id=1, source_target_pairs={{0,256},{1,2},{2,1},{3,259},{4,260},{5,6},{6,5},{7,263},{8,264},{9... | collective-permute-start | bytes 4328 | tf_op jit(solution)/shard_map/ppermute | solution.py:112
  95.7 1.9 %collective-permute-start.15 = (f32[2,4,128]{2,1,0:T(4,128)S(1)}, f32[2,4,128]{2,1,0:T(4,128)S(1)}, u32[]{:S(2)}, u32[]{:S(2)}) collective-permute-start(f32[2,4,128]{2,1,0:T(4,128)S(1)} %bitcast.105), channel_id=1, source_target_pairs={{0,4},{4,8},{8,12},{12,16},{16,20},{20,24},{24,28},{28,32},{32,36}... | collective-permute-start | bytes 12296 | tf_op jit(solution)/shard_map/ppermute | solution.py:13
  97.6 7.5 %collective-permute-start.14 = (f32[2,4,128]{2,1,0:T(4,128)S(1)}, f32[2,4,128]{2,1,0:T(4,128)S(1)}, u32[]{:S(2)}, u32[]{:S(2)}) collective-permute-start(f32[2,4,128]{2,1,0:T(4,128)S(1)} %bitcast.103), channel_id=1, source_target_pairs={{0,508},{4,0},{8,4},{12,8},{16,12},{20,16},{24,20},{28,24},{32,28}... | collective-permute-start | bytes 12296 | tf_op jit(solution)/shard_map/ppermute | solution.py:13
  105.3 0.2 copy.498
  105.5 0.2 copy.499
  105.7 0.8 collective-permute-done.14
  106.5 0.8 broadcast_multiply_fusion
  107.5 0.1 multiply_add_fusion.4
  108.1 4.0 %collective-permute-start.19 = (f32[2,4,128]{2,1,0:T(4,128)S(1)}, f32[2,4,128]{2,1,0:T(4,128)S(1)}, u32[]{:S(2)}, u32[]{:S(2)}) collective-permute-start(f32[2,4,128]{2,1,0:T(4,128)S(1)} %bitcast.107), channel_id=1, source_target_pairs={{0,8},{4,12},{8,16},{12,20},{16,24},{20,28},{24,32},{28,36},{32,40... | collective-permute-start | bytes 12296 | tf_op jit(solution)/shard_map/ppermute | solution.py:13
  112.1 9.1 %collective-permute-start.18 = (f32[2,4,128]{2,1,0:T(4,128)S(1)}, f32[2,4,128]{2,1,0:T(4,128)S(1)}, u32[]{:S(2)}, u32[]{:S(2)}) collective-permute-start(f32[2,4,128]{2,1,0:T(4,128)S(1)} %bitcast.108), channel_id=1, source_target_pairs={{0,12},{4,16},{8,20},{12,24},{16,28},{20,32},{24,36},{28,40},{32,4... | collective-permute-start | bytes 12296 | tf_op jit(solution)/shard_map/ppermute | solution.py:13
  121.2 1.9 %collective-permute-start.20 = (f32[2,4,128]{2,1,0:T(4,128)S(1)}, f32[2,4,128]{2,1,0:T(4,128)S(1)}, u32[]{:S(2)}, u32[]{:S(2)}) collective-permute-start(f32[2,4,128]{2,1,0:T(4,128)S(1)} %bitcast.109), channel_id=1, source_target_pairs={{0,4},{4,8},{8,12},{12,16},{16,20},{20,24},{24,28},{28,32},{32,36}... | collective-permute-start | bytes 12296 | tf_op jit(solution)/shard_map/ppermute | solution.py:13
  123.2 1.6 collective-permute-done.18
  124.7 5.3 %collective-permute-done.20 = f32[2,4,128]{2,1,0:T(4,128)S(1)} collective-permute-done((f32[2,4,128]{2,1,0:T(4,128)S(1)}, f32[2,4,128]{2,1,0:T(4,128)S(1)}, u32[]{:S(2)}, u32[]{:S(2)}) %collective-permute-start.20) | collective-permute-done | bytes 4128 | tf_op jit(solution)/shard_map/ppermute | solution.py:13
  130.1 4.2 %collective-permute-start.23 = (f32[2,4,128]{2,1,0:T(4,128)S(1)}, f32[2,4,128]{2,1,0:T(4,128)S(1)}, u32[]{:S(2)}, u32[]{:S(2)}) collective-permute-start(f32[2,4,128]{2,1,0:T(4,128)S(1)} %get-tuple-element.9), channel_id=1, source_target_pairs={{0,16},{4,20},{8,24},{12,28},{16,32},{20,36},{24,40},{28,44},{32,4... | collective-permute-start | bytes 12296 | tf_op jit(solution)/shard_map/ppermute | solution.py:13
  134.3 6.2 %collective-permute-start.22 = (f32[2,4,128]{2,1,0:T(4,128)S(1)}, f32[2,4,128]{2,1,0:T(4,128)S(1)}, u32[]{:S(2)}, u32[]{:S(2)}) collective-permute-start(f32[2,4,128]{2,1,0:T(4,128)S(1)} %get-tuple-element.9), channel_id=1, source_target_pairs={{0,32},{4,36},{8,40},{12,44},{16,48},{20,52},{24,56},{28,60},{32,6... | collective-permute-start | bytes 12296 | tf_op jit(solution)/shard_map/ppermute | solution.py:13
  140.5 6.2 %collective-permute-start.21 = (f32[2,4,128]{2,1,0:T(4,128)S(1)}, f32[2,4,128]{2,1,0:T(4,128)S(1)}, u32[]{:S(2)}, u32[]{:S(2)}) collective-permute-start(f32[2,4,128]{2,1,0:T(4,128)S(1)} %get-tuple-element.9), channel_id=1, source_target_pairs={{0,48},{4,52},{8,56},{12,60},{16,64},{20,68},{24,72},{28,76},{32,8... | collective-permute-start | bytes 12296 | tf_op jit(solution)/shard_map/ppermute | solution.py:13
  146.8 1.3 collective-permute-done.21
  148.1 3.1 %collective-permute-start.26 = (f32[2,4,128]{2,1,0:T(4,128)S(1)}, f32[2,4,128]{2,1,0:T(4,128)S(1)}, u32[]{:S(2)}, u32[]{:S(2)}) collective-permute-start(f32[2,4,128]{2,1,0:T(4,128)S(1)} %get-tuple-element.7), channel_id=1, source_target_pairs={{0,64},{4,68},{8,72},{12,76},{16,80},{20,84},{24,88},{28,92},{32,9... | collective-permute-start | bytes 12296 | tf_op jit(solution)/shard_map/ppermute | solution.py:13
  151.3 5.2 %collective-permute-start.25 = (f32[2,4,128]{2,1,0:T(4,128)S(1)}, f32[2,4,128]{2,1,0:T(4,128)S(1)}, u32[]{:S(2)}, u32[]{:S(2)}) collective-permute-start(f32[2,4,128]{2,1,0:T(4,128)S(1)} %get-tuple-element.7), channel_id=1, source_target_pairs={{0,128},{4,132},{8,136},{12,140},{16,144},{20,148},{24,152},{28,15... | collective-permute-start | bytes 12296 | tf_op jit(solution)/shard_map/ppermute | solution.py:13
  156.4 2.2 %collective-permute-start.24 = (f32[2,4,128]{2,1,0:T(4,128)S(1)}, f32[2,4,128]{2,1,0:T(4,128)S(1)}, u32[]{:S(2)}, u32[]{:S(2)}) collective-permute-start(f32[2,4,128]{2,1,0:T(4,128)S(1)} %get-tuple-element.7), channel_id=1, source_target_pairs={{0,192},{4,196},{8,200},{12,204},{16,208},{20,212},{24,216},{28,22... | collective-permute-start | bytes 12296 | tf_op jit(solution)/shard_map/ppermute | solution.py:13
  158.7 0.2 collective-permute-done.25
  158.9 6.1 %collective-permute-done.24 = f32[2,4,128]{2,1,0:T(4,128)S(1)} collective-permute-done((f32[2,4,128]{2,1,0:T(4,128)S(1)}, f32[2,4,128]{2,1,0:T(4,128)S(1)}, u32[]{:S(2)}, u32[]{:S(2)}) %collective-permute-start.24) | collective-permute-done | bytes 4128 | tf_op jit(solution)/shard_map/ppermute | solution.py:13
  165.0 2.8 %collective-permute-start.27 = (f32[2,4,128]{2,1,0:T(4,128)S(1)}, f32[2,4,128]{2,1,0:T(4,128)S(1)}, u32[]{:S(2)}, u32[]{:S(2)}) collective-permute-start(f32[2,4,128]{2,1,0:T(4,128)S(1)} %get-tuple-element.5), channel_id=1, source_target_pairs={{0,256},{4,260},{8,264},{12,268},{16,272},{20,276},{24,280},{28,28... | collective-permute-start | bytes 12296 | tf_op jit(solution)/shard_map/ppermute | solution.py:13
  167.8 6.6 %collective-permute-done.27 = f32[2,4,128]{2,1,0:T(4,128)S(1)} collective-permute-done((f32[2,4,128]{2,1,0:T(4,128)S(1)}, f32[2,4,128]{2,1,0:T(4,128)S(1)}, u32[]{:S(2)}, u32[]{:S(2)}) %collective-permute-start.27) | collective-permute-done | bytes 4128 | tf_op jit(solution)/shard_map/ppermute | solution.py:13
  174.5 0.7 copy.503
  (103 shorter events, 2.5 us)
Async XLA Ops:
  1.0 26.7 %collective-permute-start.1 = (f32[2,4,128]{2,1,0:T(4,128)S(1)}, f32[2,4,128]{2,1,0:T(4,128)S(1)}, u32[]{:S(2)}, u32[]{:S(2)}) collective-permute-start(f32[2,4,128]{2,1,0:T(4,128)S(1)} %bitcast.99), channel_id=1, source_target_pairs={{0,4},{4,8},{8,12},{12,16},{16,20},{20,24},{24,28},{28,32},{32,36}... | collective-permute-start | bytes 12296 | tf_op jit(solution)/shard_map/ppermute | solution.py:13
  3.0 24.8 %collective-permute-start = (f32[2,4,128]{2,1,0:T(4,128)S(1)}, f32[2,4,128]{2,1,0:T(4,128)S(1)}, u32[]{:S(2)}, u32[]{:S(2)}) collective-permute-start(f32[2,4,128]{2,1,0:T(4,128)S(1)} %bitcast.101), channel_id=1, source_target_pairs={{0,508},{4,0},{8,4},{12,8},{16,12},{20,16},{24,20},{28,24},{32,28}... | collective-permute-start | bytes 12296 | tf_op jit(solution)/shard_map/ppermute | solution.py:13
  11.0 15.8 %collective-permute-start.2 = (f32[2,4,45]{2,1,0:T(4,128)S(1)}, f32[2,4,45]{2,1,0:T(4,128)S(1)}, u32[]{:S(2)}, u32[]{:S(2)}) collective-permute-start(f32[2,4,45]{2,1,0:T(4,128)S(1)} %bitcast.95), channel_id=1, source_target_pairs={{0,1},{1,0},{2,3},{3,2},{4,5},{5,4},{6,7},{7,6},{8,9},{9,8},{10,11... | collective-permute-start | bytes 4328 | tf_op jit(solution)/shard_map/ppermute | solution.py:111
  14.4 12.5 %collective-permute-start.3 = (f32[2,4,45]{2,1,0:T(4,128)S(1)}, f32[2,4,45]{2,1,0:T(4,128)S(1)}, u32[]{:S(2)}, u32[]{:S(2)}) collective-permute-start(f32[2,4,45]{2,1,0:T(4,128)S(1)} %bitcast.96), channel_id=1, source_target_pairs={{0,256},{1,2},{2,1},{3,259},{4,260},{5,6},{6,5},{7,263},{8,264},{9... | collective-permute-start | bytes 4328 | tf_op jit(solution)/shard_map/ppermute | solution.py:112
  25.4 0.8 copy-start.1
  26.7 0.7 copy-start.2
  27.4 0.9 copy-start
  29.9 10.8 %collective-permute-start.6 = (f32[2,5,128]{2,1,0:T(8,128)S(1)}, f32[2,5,128]{2,1,0:T(8,128)S(1)}, u32[]{:S(2)}, u32[]{:S(2)}) collective-permute-start(f32[2,5,128]{2,1,0:T(8,128)S(1)} %pad_maximum_fusion.4), channel_id=1, source_target_pairs={{0,12},{4,16},{8,20},{12,24},{16,28},{20,32},{24,36},{28,40},{32,4... | collective-permute-start | bytes 15368 | tf_op jit(solution)/shard_map/ppermute | solution.py:13
  32.2 10.0 %collective-permute-start.5 = (f32[2,5,128]{2,1,0:T(8,128)S(1)}, f32[2,5,128]{2,1,0:T(8,128)S(1)}, u32[]{:S(2)}, u32[]{:S(2)}) collective-permute-start(f32[2,5,128]{2,1,0:T(8,128)S(1)} %pad_maximum_fusion.4), channel_id=1, source_target_pairs={{0,8},{4,12},{8,16},{12,20},{16,24},{20,28},{24,32},{28,36},{32,40... | collective-permute-start | bytes 15368 | tf_op jit(solution)/shard_map/ppermute | solution.py:13
  37.4 8.9 %collective-permute-start.4 = (f32[2,5,128]{2,1,0:T(8,128)S(1)}, f32[2,5,128]{2,1,0:T(8,128)S(1)}, u32[]{:S(2)}, u32[]{:S(2)}) collective-permute-start(f32[2,5,128]{2,1,0:T(8,128)S(1)} %pad_maximum_fusion.4), channel_id=1, source_target_pairs={{0,4},{4,8},{8,12},{12,16},{16,20},{20,24},{24,28},{28,32},{32,36}... | collective-permute-start | bytes 15368 | tf_op jit(solution)/shard_map/ppermute | solution.py:13
  46.4 11.4 %collective-permute-start.9 = (f32[2,5,128]{2,1,0:T(8,128)S(1)}, f32[2,5,128]{2,1,0:T(8,128)S(1)}, u32[]{:S(2)}, u32[]{:S(2)}) collective-permute-start(f32[2,5,128]{2,1,0:T(8,128)S(1)} %pad_maximum_fusion.5), channel_id=1, source_target_pairs={{0,48},{4,52},{8,56},{12,60},{16,64},{20,68},{24,72},{28,76},{32,8... | collective-permute-start | bytes 15368 | tf_op jit(solution)/shard_map/ppermute | solution.py:13
  53.0 9.2 %collective-permute-start.8 = (f32[2,5,128]{2,1,0:T(8,128)S(1)}, f32[2,5,128]{2,1,0:T(8,128)S(1)}, u32[]{:S(2)}, u32[]{:S(2)}) collective-permute-start(f32[2,5,128]{2,1,0:T(8,128)S(1)} %pad_maximum_fusion.5), channel_id=1, source_target_pairs={{0,32},{4,36},{8,40},{12,44},{16,48},{20,52},{24,56},{28,60},{32,6... | collective-permute-start | bytes 15368 | tf_op jit(solution)/shard_map/ppermute | solution.py:13
  55.0 8.9 %collective-permute-start.7 = (f32[2,5,128]{2,1,0:T(8,128)S(1)}, f32[2,5,128]{2,1,0:T(8,128)S(1)}, u32[]{:S(2)}, u32[]{:S(2)}) collective-permute-start(f32[2,5,128]{2,1,0:T(8,128)S(1)} %pad_maximum_fusion.5), channel_id=1, source_target_pairs={{0,16},{4,20},{8,24},{12,28},{16,32},{20,36},{24,40},{28,44},{32,4... | collective-permute-start | bytes 15368 | tf_op jit(solution)/shard_map/ppermute | solution.py:13
  63.9 12.9 %collective-permute-start.12 = (f32[2,5,128]{2,1,0:T(8,128)S(1)}, f32[2,5,128]{2,1,0:T(8,128)S(1)}, u32[]{:S(2)}, u32[]{:S(2)}) collective-permute-start(f32[2,5,128]{2,1,0:T(8,128)S(1)} %pad_maximum_fusion.6), channel_id=1, source_target_pairs={{0,192},{4,196},{8,200},{12,204},{16,208},{20,212},{24,216},{28,22... | collective-permute-start | bytes 15368 | tf_op jit(solution)/shard_map/ppermute | solution.py:13
  70.4 7.7 %collective-permute-start.11 = (f32[2,5,128]{2,1,0:T(8,128)S(1)}, f32[2,5,128]{2,1,0:T(8,128)S(1)}, u32[]{:S(2)}, u32[]{:S(2)}) collective-permute-start(f32[2,5,128]{2,1,0:T(8,128)S(1)} %pad_maximum_fusion.6), channel_id=1, source_target_pairs={{0,128},{4,132},{8,136},{12,140},{16,144},{20,148},{24,152},{28,15... | collective-permute-start | bytes 15368 | tf_op jit(solution)/shard_map/ppermute | solution.py:13
  73.4 6.8 %collective-permute-start.10 = (f32[2,5,128]{2,1,0:T(8,128)S(1)}, f32[2,5,128]{2,1,0:T(8,128)S(1)}, u32[]{:S(2)}, u32[]{:S(2)}) collective-permute-start(f32[2,5,128]{2,1,0:T(8,128)S(1)} %pad_maximum_fusion.6), channel_id=1, source_target_pairs={{0,64},{4,68},{8,72},{12,76},{16,80},{20,84},{24,88},{28,92},{32,9... | collective-permute-start | bytes 15368 | tf_op jit(solution)/shard_map/ppermute | solution.py:13
  80.2 2.9 %copy-start.3 = (s32[128]{0:T(128)S(1)}, s32[128]{0:T(128)}, u32[]{:S(2)}) copy-start(s32[128]{0:T(128)} %param.7) | copy-start | bytes 1540
  80.2 9.5 %collective-permute-start.13 = (f32[2,5,128]{2,1,0:T(8,128)S(1)}, f32[2,5,128]{2,1,0:T(8,128)S(1)}, u32[]{:S(2)}, u32[]{:S(2)}) collective-permute-start(f32[2,5,128]{2,1,0:T(8,128)S(1)} %pad_maximum_fusion.7), channel_id=1, source_target_pairs={{0,256},{4,260},{8,264},{12,268},{16,272},{20,276},{24,280},{28,28... | collective-permute-start | bytes 15368 | tf_op jit(solution)/shard_map/ppermute | solution.py:13
  90.9 14.3 %collective-permute-start.16 = (f32[2,4,45]{2,1,0:T(4,128)S(1)}, f32[2,4,45]{2,1,0:T(4,128)S(1)}, u32[]{:S(2)}, u32[]{:S(2)}) collective-permute-start(f32[2,4,45]{2,1,0:T(4,128)S(1)} %bitcast.98), channel_id=1, source_target_pairs={{0,1},{1,0},{2,3},{3,2},{4,5},{5,4},{6,7},{7,6},{8,9},{9,8},{10,11... | collective-permute-start | bytes 4328 | tf_op jit(solution)/shard_map/ppermute | solution.py:111
  92.8 12.4 %collective-permute-start.17 = (f32[2,4,45]{2,1,0:T(4,128)S(1)}, f32[2,4,45]{2,1,0:T(4,128)S(1)}, u32[]{:S(2)}, u32[]{:S(2)}) collective-permute-start(f32[2,4,45]{2,1,0:T(4,128)S(1)} %bitcast.97), channel_id=1, source_target_pairs={{0,256},{1,2},{2,1},{3,259},{4,260},{5,6},{6,5},{7,263},{8,264},{9... | collective-permute-start | bytes 4328 | tf_op jit(solution)/shard_map/ppermute | solution.py:112
  95.7 9.9 %collective-permute-start.15 = (f32[2,4,128]{2,1,0:T(4,128)S(1)}, f32[2,4,128]{2,1,0:T(4,128)S(1)}, u32[]{:S(2)}, u32[]{:S(2)}) collective-permute-start(f32[2,4,128]{2,1,0:T(4,128)S(1)} %bitcast.105), channel_id=1, source_target_pairs={{0,4},{4,8},{8,12},{12,16},{16,20},{20,24},{24,28},{28,32},{32,36}... | collective-permute-start | bytes 12296 | tf_op jit(solution)/shard_map/ppermute | solution.py:13
  97.6 8.9 %collective-permute-start.14 = (f32[2,4,128]{2,1,0:T(4,128)S(1)}, f32[2,4,128]{2,1,0:T(4,128)S(1)}, u32[]{:S(2)}, u32[]{:S(2)}) collective-permute-start(f32[2,4,128]{2,1,0:T(4,128)S(1)} %bitcast.103), channel_id=1, source_target_pairs={{0,508},{4,0},{8,4},{12,8},{16,12},{20,16},{24,20},{28,24},{32,28}... | collective-permute-start | bytes 12296 | tf_op jit(solution)/shard_map/ppermute | solution.py:13
  108.1 15.0 %collective-permute-start.19 = (f32[2,4,128]{2,1,0:T(4,128)S(1)}, f32[2,4,128]{2,1,0:T(4,128)S(1)}, u32[]{:S(2)}, u32[]{:S(2)}) collective-permute-start(f32[2,4,128]{2,1,0:T(4,128)S(1)} %bitcast.107), channel_id=1, source_target_pairs={{0,8},{4,12},{8,16},{12,20},{16,24},{20,28},{24,32},{28,36},{32,40... | collective-permute-start | bytes 12296 | tf_op jit(solution)/shard_map/ppermute | solution.py:13
  112.1 12.6 %collective-permute-start.18 = (f32[2,4,128]{2,1,0:T(4,128)S(1)}, f32[2,4,128]{2,1,0:T(4,128)S(1)}, u32[]{:S(2)}, u32[]{:S(2)}) collective-permute-start(f32[2,4,128]{2,1,0:T(4,128)S(1)} %bitcast.108), channel_id=1, source_target_pairs={{0,12},{4,16},{8,20},{12,24},{16,28},{20,32},{24,36},{28,40},{32,4... | collective-permute-start | bytes 12296 | tf_op jit(solution)/shard_map/ppermute | solution.py:13
  121.2 8.8 %collective-permute-start.20 = (f32[2,4,128]{2,1,0:T(4,128)S(1)}, f32[2,4,128]{2,1,0:T(4,128)S(1)}, u32[]{:S(2)}, u32[]{:S(2)}) collective-permute-start(f32[2,4,128]{2,1,0:T(4,128)S(1)} %bitcast.109), channel_id=1, source_target_pairs={{0,4},{4,8},{8,12},{12,16},{16,20},{20,24},{24,28},{28,32},{32,36}... | collective-permute-start | bytes 12296 | tf_op jit(solution)/shard_map/ppermute | solution.py:13
  130.1 16.7 %collective-permute-start.23 = (f32[2,4,128]{2,1,0:T(4,128)S(1)}, f32[2,4,128]{2,1,0:T(4,128)S(1)}, u32[]{:S(2)}, u32[]{:S(2)}) collective-permute-start(f32[2,4,128]{2,1,0:T(4,128)S(1)} %get-tuple-element.9), channel_id=1, source_target_pairs={{0,16},{4,20},{8,24},{12,28},{16,32},{20,36},{24,40},{28,44},{32,4... | collective-permute-start | bytes 12296 | tf_op jit(solution)/shard_map/ppermute | solution.py:13
  134.3 12.5 %collective-permute-start.22 = (f32[2,4,128]{2,1,0:T(4,128)S(1)}, f32[2,4,128]{2,1,0:T(4,128)S(1)}, u32[]{:S(2)}, u32[]{:S(2)}) collective-permute-start(f32[2,4,128]{2,1,0:T(4,128)S(1)} %get-tuple-element.9), channel_id=1, source_target_pairs={{0,32},{4,36},{8,40},{12,44},{16,48},{20,52},{24,56},{28,60},{32,6... | collective-permute-start | bytes 12296 | tf_op jit(solution)/shard_map/ppermute | solution.py:13
  140.5 7.6 %collective-permute-start.21 = (f32[2,4,128]{2,1,0:T(4,128)S(1)}, f32[2,4,128]{2,1,0:T(4,128)S(1)}, u32[]{:S(2)}, u32[]{:S(2)}) collective-permute-start(f32[2,4,128]{2,1,0:T(4,128)S(1)} %get-tuple-element.9), channel_id=1, source_target_pairs={{0,48},{4,52},{8,56},{12,60},{16,64},{20,68},{24,72},{28,76},{32,8... | collective-permute-start | bytes 12296 | tf_op jit(solution)/shard_map/ppermute | solution.py:13
  148.1 10.6 %collective-permute-start.26 = (f32[2,4,128]{2,1,0:T(4,128)S(1)}, f32[2,4,128]{2,1,0:T(4,128)S(1)}, u32[]{:S(2)}, u32[]{:S(2)}) collective-permute-start(f32[2,4,128]{2,1,0:T(4,128)S(1)} %get-tuple-element.7), channel_id=1, source_target_pairs={{0,64},{4,68},{8,72},{12,76},{16,80},{20,84},{24,88},{28,92},{32,9... | collective-permute-start | bytes 12296 | tf_op jit(solution)/shard_map/ppermute | solution.py:13
  151.3 7.6 %collective-permute-start.25 = (f32[2,4,128]{2,1,0:T(4,128)S(1)}, f32[2,4,128]{2,1,0:T(4,128)S(1)}, u32[]{:S(2)}, u32[]{:S(2)}) collective-permute-start(f32[2,4,128]{2,1,0:T(4,128)S(1)} %get-tuple-element.7), channel_id=1, source_target_pairs={{0,128},{4,132},{8,136},{12,140},{16,144},{20,148},{24,152},{28,15... | collective-permute-start | bytes 12296 | tf_op jit(solution)/shard_map/ppermute | solution.py:13
  156.4 8.5 %collective-permute-start.24 = (f32[2,4,128]{2,1,0:T(4,128)S(1)}, f32[2,4,128]{2,1,0:T(4,128)S(1)}, u32[]{:S(2)}, u32[]{:S(2)}) collective-permute-start(f32[2,4,128]{2,1,0:T(4,128)S(1)} %get-tuple-element.7), channel_id=1, source_target_pairs={{0,192},{4,196},{8,200},{12,204},{16,208},{20,212},{24,216},{28,22... | collective-permute-start | bytes 12296 | tf_op jit(solution)/shard_map/ppermute | solution.py:13
  165.0 9.4 %collective-permute-start.27 = (f32[2,4,128]{2,1,0:T(4,128)S(1)}, f32[2,4,128]{2,1,0:T(4,128)S(1)}, u32[]{:S(2)}, u32[]{:S(2)}) collective-permute-start(f32[2,4,128]{2,1,0:T(4,128)S(1)} %get-tuple-element.5), channel_id=1, source_target_pairs={{0,256},{4,260},{8,264},{12,268},{16,272},{20,276},{24,280},{28,28... | collective-permute-start | bytes 12296 | tf_op jit(solution)/shard_map/ppermute | solution.py:13

commit v3 on v2

v3 whole, which is shorter than its diff:
```python
import jax
import jax.numpy as jnp
from jax import lax
from jax.sharding import Mesh, PartitionSpec as P

ITERS = 2
LON = ("lz", "lx", "lyc")


def axis_count(axis):
    names = axis if isinstance(axis, tuple) else (axis,)
    count = 1
    for name in names:
        count *= lax.axis_size(name)
    return count


def from_behind(value, axis, steps):
    count = axis_count(axis)
    pairs = [(source, (source + steps) % count) for source in range(count)]
    return lax.ppermute(value, axis, pairs)


def shift_along(x, steps, axis, fill):
    pad_shape = list(x.shape)
    pad_shape[axis] = steps
    head = jnp.full(pad_shape, fill, x.dtype)
    body = lax.slice_in_dim(x, 0, x.shape[axis] - steps, axis=axis)
    return jnp.concatenate([head, body], axis=axis)


def block_rates(rate):
    steps = []
    span = 1
    while span < rate.shape[1]:
        steps.append((span, rate))
        rate = rate * shift_along(rate, span, 1, 1.0)
        span *= 2
    return steps, rate


def block_scan(steps, source):
    for span, rate in steps:
        source = source + rate[:, None] * shift_along(source, span, 2, 0.0)
    return source


def compose(later, earlier):
    return (later[0] * earlier[0], later[0][:, None] * earlier[1] + later[1])


def gathered(maps, axis):
    count = lax.axis_size(axis)
    packed = jnp.concatenate([maps[1], maps[0][:, None]], axis=1)
    spread = jnp.broadcast_to(packed[None], (count,) + packed.shape)
    got = lax.all_to_all(spread, axis, 0, 0, tiled=False)
    return [(got[i][:, -1], got[i][:, :-1]) for i in range(count)]


def pick(options, index):
    rates = jnp.stack([o[0] for o in options])
    offsets = jnp.stack([o[1] for o in options])
    return (
        lax.dynamic_index_in_dim(rates, index, 0, False),
        lax.dynamic_index_in_dim(offsets, index, 0, False),
    )


def group_parts(members, index):
    count = len(members)
    ident = (jnp.ones_like(members[0][0]), jnp.zeros_like(members[0][1]))
    before = [ident]
    for i in range(1, count):
        before.append(compose(members[i - 1], before[-1]))
    after = [ident]
    for i in range(count - 2, -1, -1):
        after.insert(0, compose(after[0], members[i + 1]))
    total = compose(members[-1], before[-1])
    return total, pick(before, index), pick(after, index)


def cyclic_rest(members, index):
    count = len(members)
    options = []
    for g in range(count):
        rest = members[(g + 1) % count]
        for k in range(2, count):
            rest = compose(members[(g + k) % count], rest)
        options.append(rest)
    return pick(options, index)


def lon_inflow(own):
    members = gathered(own, "lyc")
    total_yc, pre_yc, suf_yc = group_parts(members, lax.axis_index("lyc"))
    groups = gathered(total_yc, "lx")
    total_x, pre_x, suf_x = group_parts(groups, lax.axis_index("lx"))
    circle = gathered(total_x, "lz")
    rest = cyclic_rest(circle, lax.axis_index("lz"))
    excl = compose(pre_yc, compose(pre_x, compose(rest, compose(suf_x, suf_yc))))
    rate, offset = own
    return (excl[0][:, None] * offset + excl[1]) / (1.0 - excl[0] * rate)[:, None]


def halo_tendency(field, turning, lat_index, half_cycle):
    lon_count = axis_count(LON)
    lat_count = lax.axis_size("lat")
    assert lat_count % 2 == 0
    east = from_behind(field[:, :, 0, :], LON, -1)
    west = from_behind(field[:, :, -1, :], LON, 1)
    top = field[..., 0]
    bottom = field[..., -1]
    odd = lat_index % 2 == 1
    pairs_a = []
    pairs_b = []
    for d in range(lon_count):
        for l in range(lat_count):
            me = d * lat_count + l
            if l % 2 == 0:
                pairs_a.append((me, d * lat_count + l + 1))
            else:
                pairs_a.append((me, d * lat_count + l - 1))
            if l == 0 or l == lat_count - 1:
                pairs_b.append((me, ((d + half_cycle) % lon_count) * lat_count + l))
            elif l % 2 == 1:
                pairs_b.append((me, d * lat_count + l + 1))
            else:
                pairs_b.append((me, d * lat_count + l - 1))
    got_a = lax.ppermute(jnp.where(odd, top, bottom), LON + ("lat",), pairs_a)
    got_b = lax.ppermute(jnp.where(odd, bottom, top), LON + ("lat",), pairs_b)
    flips = jnp.array([-1.0, -1.0, 1.0, 1.0], jnp.float32)[None, :, None]
    pole = (lat_index == 0) | (lat_index == lat_count - 1)
    got_b = jnp.where(pole, got_b * flips, got_b)
    north = jnp.where(odd, got_a, got_b)
    south = jnp.where(odd, got_b, got_a)
    north_rows = jnp.concatenate([north[..., None], field[..., :-1]], axis=3)
    south_rows = jnp.concatenate([field[..., 1:], south[..., None]], axis=3)
    east_cells = jnp.concatenate([field[:, :, 1:], east[:, :, None]], axis=2)
    west_cells = jnp.concatenate([west[:, :, None], field[:, :, :-1]], axis=2)
    u_wind = field[:, 0:1]
    v_wind = field[:, 1:2]
    result = 0.1 * (east_cells + west_cells - 2.0 * field) + 0.1 * (
        north_rows + south_rows - 2.0 * field
    )
    result = result - 0.25 * v_wind * (north_rows - south_rows)
    coriolis = jnp.concatenate(
        [turning * v_wind, -turning * u_wind, jnp.zeros_like(field[:, 2:])], axis=1
    )
    return result + coriolis


def local(state, courant, band_mask):
    rows = state.shape[3]
    lat_index = lax.axis_index("lat")
    lat_count = lax.axis_size("lat")
    half_cycle = axis_count(LON) // 2
    total_rows = rows * lat_count
    row_ids = lat_index * rows + jnp.arange(rows, dtype=jnp.int32)
    latitude = jnp.pi / 2 - (row_ids.astype(jnp.float32) + 0.5) * jnp.pi / total_rows
    turning = 0.5 * jnp.sin(latitude)
    inverse = 1.0 / (1.0 + courant)
    rate = courant * inverse
    steps, carried = block_rates(rate)
    gain = carried[:, -1, :]
    in_band = (band_mask == 1)[None, None, None, :]
    estimate = state
    for sweep in range(ITERS):
        middle = 0.5 * (state + estimate)
        star = state + halo_tendency(middle, turning, lat_index, half_cycle)
        partial_value = block_scan(steps, star * inverse[:, None])
        ends = partial_value[:, :, -1, :]
        entry = lon_inflow((gain, ends))
        solved = partial_value + carried[:, None] * entry[:, :, None, :]
        estimate = jnp.where(in_band, solved, star)
    return estimate


def solution(mesh):
    lon_count = mesh.shape["lon"]
    inner = 4
    split = Mesh(
        mesh.devices.reshape(lon_count // (inner * inner), inner, inner, mesh.shape["lat"]),
        ("lz", "lx", "lyc", "lat"),
    )
    in_specs = (P(None, None, LON, "lat"), P(None, LON, "lat"), P("lat"))
    out_specs = P(None, None, LON, "lat")
    return jax.shard_map(local, mesh=split, in_specs=in_specs, out_specs=out_specs, check_vma=False)
```

time: 176 us -> 135 us (0.77)
  the two profiles are of different devices: /device:TPU:56 before, /device:TPU:1 now
where the time goes in v3:
time: 135 us; the launch traced here: 133 us
  starting transfers between devices  67.5 us (50%)
  waiting for transfers between devices  35.7 us (26%)
  blocking collectives  14.8 us (11%)
  local copies, waits for them, and re-layouts  7.91 us (6%)
  other arithmetic  6.18 us (5%)
    all_to_all x5, starting transfers between devices, gathered(): got = lax.all_to_all(spread, axis, 0, 0, tiled=False)  32.3 us
    all_to_all x5, waiting for transfers between devices, gathered(): got = lax.all_to_all(spread, axis, 0, 0, tiled=False)  29.3 us
    ppermute x4, starting transfers between devices, from_behind(): return lax.ppermute(value, axis, pairs)  18.2 us
    all_to_all x1, blocking collectives, gathered(): got = lax.all_to_all(spread, axis, 0, 0, tiled=False)  14.8 us
    ppermute x2, starting transfers between devices, halo_tendency(): got_b = lax.ppermute(jnp.where(odd, bottom, top), LON + ('lat',), pairs_b)  12.8 us
    ppermute x4, waiting for transfers between devices, from_behind(): return lax.ppermute(value, axis, pairs)  6.38 us
    ppermute x2, starting transfers between devices, halo_tendency(): got_a = lax.ppermute(jnp.where(odd, top, bottom), LON + ('lat',), pairs_a)  4.22 us
    broadcast_in_dim x6, local copies, waits for them, and re-layouts, gathered(): spread = jnp.broadcast_to(packed[None], (count,) + packed.shape)  3.1 us
  transfers between devices with their start and end apart: 13, of which 6 were waited for; matrix products, arithmetic and copies ran while one was open for 2% of the time, Pallas kernels for 0%

profile of v3, /device:TPU:1, one launch (start us, length us, event | category | flops | bytes accessed | tf_op | source)
XLA Modules:
  0.0 133.2 jit_solution(417525485180468983)
XLA Ops:
  0.0 1.0 add_multiply_fusion
  1.0 8.8 %collective-permute-start.1 = (f32[2,4,128]{2,1,0:T(4,128)S(1)}, f32[2,4,128]{2,1,0:T(4,128)S(1)}, u32[]{:S(2)}, u32[]{:S(2)}) collective-permute-start(f32[2,4,128]{2,1,0:T(4,128)S(1)} %bitcast.806), channel_id=1, source_target_pairs={{0,4},{4,8},{8,12},{12,16},{16,20},{20,24},{24,28},{28,32},{32,36}... | collective-permute-start | bytes 12296 | tf_op jit(solution)/shard_map/ppermute | solution.py:21
  9.9 1.9 %collective-permute-start = (f32[2,4,128]{2,1,0:T(4,128)S(1)}, f32[2,4,128]{2,1,0:T(4,128)S(1)}, u32[]{:S(2)}, u32[]{:S(2)}) collective-permute-start(f32[2,4,128]{2,1,0:T(4,128)S(1)} %bitcast.808), channel_id=1, source_target_pairs={{0,508},{4,0},{8,4},{12,8},{16,12},{20,16},{24,20},{28,24},{32,28}... | collective-permute-start | bytes 12296 | tf_op jit(solution)/shard_map/ppermute | solution.py:21
  11.9 0.3 broadcast_select_fusion.2
  12.1 0.1 copy.726
  12.3 2.3 %collective-permute-start.2 = (f32[2,4,45]{2,1,0:T(4,128)S(1)}, f32[2,4,45]{2,1,0:T(4,128)S(1)}, u32[]{:S(2)}, u32[]{:S(2)}) collective-permute-start(f32[2,4,45]{2,1,0:T(4,128)S(1)} %bitcast.802), channel_id=1, source_target_pairs={{0,1},{1,0},{2,3},{3,2},{4,5},{5,4},{6,7},{7,6},{8,9},{9,8},{10,11... | collective-permute-start | bytes 4328 | tf_op jit(solution)/shard_map/ppermute | solution.py:129
  14.6 0.1 copy.727
  14.7 10.6 %collective-permute-start.3 = (f32[2,4,45]{2,1,0:T(4,128)S(1)}, f32[2,4,45]{2,1,0:T(4,128)S(1)}, u32[]{:S(2)}, u32[]{:S(2)}) collective-permute-start(f32[2,4,45]{2,1,0:T(4,128)S(1)} %bitcast.803), channel_id=1, source_target_pairs={{0,256},{1,2},{2,1},{3,259},{4,260},{5,6},{6,5},{7,263},{8,264},{9... | collective-permute-start | bytes 4328 | tf_op jit(solution)/shard_map/ppermute | solution.py:130
  25.3 0.1 fusion.182
  25.5 0.3 fusion.184
  25.8 0.5 copy-done.1
  26.7 0.1 pad.107.clone
  26.8 0.6 copy-done.2
  27.5 0.2 copy.728
  27.6 0.2 copy.729
  27.8 0.5 copy-done
  28.4 0.7 broadcast_multiply_fusion.1
  29.1 0.1 multiply_add_fusion.11
  29.3 0.1 multiply_add_fusion.10
  29.4 0.1 multiply_add_fusion.9
  29.5 0.1 multiply_add_fusion.8
  29.7 0.1 multiply_add_fusion.7
  29.8 0.1 multiply_add_fusion.6
  29.9 0.6 broadcast_in_dim.41
  30.6 10.9 %all-to-all-start = ((f32[4,2,5,128]{3,1,2,0:T(2,128)}), f32[4,2,5,128]{3,1,2,0:T(2,128)S(1)}, u32[]{:S(2)}, u32[]{:S(2)}) async-start(f32[4,2,5,128]{3,1,2,0:T(2,128)} %broadcast_in_dim.41), calls=%async_computation | async-start | bytes 40960 | tf_op jit(solution)/shard_map/all_to_all | solution.py:56
  41.5 7.0 %all-to-all-done = f32[4,2,5,128]{3,1,2,0:T(2,128)S(1)} async-done(((f32[4,2,5,128]{3,1,2,0:T(2,128)}), f32[4,2,5,128]{3,1,2,0:T(2,128)S(1)}, u32[]{:S(2)}, u32[]{:S(2)}) %all-to-all-start) | async-done | bytes 20512 | tf_op jit(solution)/shard_map/all_to_all | solution.py:56
  48.5 0.6 broadcast_in_dim.42
  49.1 3.3 %all-to-all-start.1 = ((f32[4,2,5,128]{3,1,2,0:T(2,128)}), f32[4,2,5,128]{3,1,2,0:T(2,128)S(1)}, u32[]{:S(2)}, u32[]{:S(2)}) async-start(f32[4,2,5,128]{3,1,2,0:T(2,128)} %broadcast_in_dim.42), calls=%async_computation.1 | async-start | bytes 40960 | tf_op jit(solution)/shard_map/all_to_all | solution.py:56
  52.4 4.2 %all-to-all-done.1 = f32[4,2,5,128]{3,1,2,0:T(2,128)S(1)} async-done(((f32[4,2,5,128]{3,1,2,0:T(2,128)}), f32[4,2,5,128]{3,1,2,0:T(2,128)S(1)}, u32[]{:S(2)}, u32[]{:S(2)}) %all-to-all-start.1) | async-done | bytes 20512 | tf_op jit(solution)/shard_map/all_to_all | solution.py:56
  56.7 0.6 broadcast_in_dim.43
  57.3 4.8 %all-to-all-start.2 = ((f32[8,2,5,128]{3,1,2,0:T(2,128)}), f32[8,2,5,128]{3,1,2,0:T(2,128)S(1)}, u32[]{:S(2)}, u32[]{:S(2)}) async-start(f32[8,2,5,128]{3,1,2,0:T(2,128)} %broadcast_in_dim.43), calls=%async_computation.2 | async-start | bytes 81920 | tf_op jit(solution)/shard_map/all_to_all | solution.py:56
  62.1 7.0 %all-to-all-done.2 = f32[8,2,5,128]{3,1,2,0:T(2,128)S(1)} async-done(((f32[8,2,5,128]{3,1,2,0:T(2,128)}), f32[8,2,5,128]{3,1,2,0:T(2,128)S(1)}, u32[]{:S(2)}, u32[]{:S(2)}) %all-to-all-start.2) | async-done | bytes 40992 | tf_op jit(solution)/shard_map/all_to_all | solution.py:56
  69.7 0.1 divide_bitcast_fusion.1
  69.8 0.2 broadcast_multiply_fusion.2
  70.0 0.1 fusion.179
  70.1 0.3 broadcast_select_fusion
  70.4 0.3 fusion.181
  70.6 0.1 copy.762
  70.8 0.1 copy.761
  70.9 1.9 %collective-permute-start.6 = (f32[2,4,45]{2,1,0:T(4,128)S(1)}, f32[2,4,45]{2,1,0:T(4,128)S(1)}, u32[]{:S(2)}, u32[]{:S(2)}) collective-permute-start(f32[2,4,45]{2,1,0:T(4,128)S(1)} %bitcast.805), channel_id=1, source_target_pairs={{0,1},{1,0},{2,3},{3,2},{4,5},{5,4},{6,7},{7,6},{8,9},{9,8},{10,11... | collective-permute-start | bytes 4328 | tf_op jit(solution)/shard_map/ppermute | solution.py:129
  72.9 2.1 %collective-permute-start.7 = (f32[2,4,45]{2,1,0:T(4,128)S(1)}, f32[2,4,45]{2,1,0:T(4,128)S(1)}, u32[]{:S(2)}, u32[]{:S(2)}) collective-permute-start(f32[2,4,45]{2,1,0:T(4,128)S(1)} %bitcast.804), channel_id=1, source_target_pairs={{0,256},{1,2},{2,1},{3,259},{4,260},{5,6},{6,5},{7,263},{8,264},{9... | collective-permute-start | bytes 4328 | tf_op jit(solution)/shard_map/ppermute | solution.py:130
  75.0 5.1 %collective-permute-start.5 = (f32[2,4,128]{2,1,0:T(4,128)S(1)}, f32[2,4,128]{2,1,0:T(4,128)S(1)}, u32[]{:S(2)}, u32[]{:S(2)}) collective-permute-start(f32[2,4,128]{2,1,0:T(4,128)S(1)} %bitcast.812), channel_id=1, source_target_pairs={{0,4},{4,8},{8,12},{12,16},{16,20},{20,24},{24,28},{28,32},{32,36}... | collective-permute-start | bytes 12296 | tf_op jit(solution)/shard_map/ppermute | solution.py:21
  80.2 2.3 %collective-permute-start.4 = (f32[2,4,128]{2,1,0:T(4,128)S(1)}, f32[2,4,128]{2,1,0:T(4,128)S(1)}, u32[]{:S(2)}, u32[]{:S(2)}) collective-permute-start(f32[2,4,128]{2,1,0:T(4,128)S(1)} %bitcast.810), channel_id=1, source_target_pairs={{0,508},{4,0},{8,4},{12,8},{16,12},{20,16},{24,20},{28,24},{32,28}... | collective-permute-start | bytes 12296 | tf_op jit(solution)/shard_map/ppermute | solution.py:21
  82.5 0.1 select_bitcast_fusion.1
  82.6 0.2 copy.763
  82.7 0.2 copy.764
  82.9 6.4 %collective-permute-done.4 = f32[2,4,128]{2,1,0:T(4,128)S(1)} collective-permute-done((f32[2,4,128]{2,1,0:T(4,128)S(1)}, f32[2,4,128]{2,1,0:T(4,128)S(1)}, u32[]{:S(2)}, u32[]{:S(2)}) %collective-permute-start.4) | collective-permute-done | bytes 4128 | tf_op jit(solution)/shard_map/ppermute | solution.py:21
  89.3 0.8 broadcast_multiply_fusion
  90.1 0.1 multiply_add_fusion.5
  90.3 0.1 multiply_add_fusion.4
  90.4 0.1 multiply_add_fusion.3
  90.6 0.1 multiply_add_fusion.2
  90.7 0.1 multiply_add_fusion.1
  90.8 0.1 multiply_add_fusion
  91.0 14.8 %all_to_all.30 = f32[4,2,5,128]{3,1,2,0:T(2,128)S(1)} all-to-all(f32[4,2,5,128]{3,1,2,0:T(2,128)S(1)} %broadcast_in_dim.51), channel_id=1, replica_groups=mesh['lz'=8,'lx'=4,'lyc'=4,'lat'=4] {'lyc'}, dimensions={0} | all-to-all | bytes 40960 | tf_op jit(solution)/shard_map/all_to_all | solution.py:56
  105.8 0.6 broadcast_in_dim.52
  106.4 6.6 %all-to-all-start.4 = ((f32[4,2,5,128]{3,1,2,0:T(2,128)}), f32[4,2,5,128]{3,1,2,0:T(2,128)S(1)}, u32[]{:S(2)}, u32[]{:S(2)}) async-start(f32[4,2,5,128]{3,1,2,0:T(2,128)} %broadcast_in_dim.52), calls=%async_computation.4 | async-start | bytes 40960 | tf_op jit(solution)/shard_map/all_to_all | solution.py:56
  113.1 4.2 %all-to-all-done.4 = f32[4,2,5,128]{3,1,2,0:T(2,128)S(1)} async-done(((f32[4,2,5,128]{3,1,2,0:T(2,128)}), f32[4,2,5,128]{3,1,2,0:T(2,128)S(1)}, u32[]{:S(2)}, u32[]{:S(2)}) %all-to-all-start.4) | async-done | bytes 20512 | tf_op jit(solution)/shard_map/all_to_all | solution.py:56
  117.3 0.6 broadcast_in_dim.53
  118.0 6.7 %all-to-all-start.5 = ((f32[8,2,5,128]{3,1,2,0:T(2,128)}), f32[8,2,5,128]{3,1,2,0:T(2,128)S(1)}, u32[]{:S(2)}, u32[]{:S(2)}) async-start(f32[8,2,5,128]{3,1,2,0:T(2,128)} %broadcast_in_dim.53), calls=%async_computation.5 | async-start | bytes 81920 | tf_op jit(solution)/shard_map/all_to_all | solution.py:56
  124.7 7.0 %all-to-all-done.5 = f32[8,2,5,128]{3,1,2,0:T(2,128)S(1)} async-done(((f32[8,2,5,128]{3,1,2,0:T(2,128)}), f32[8,2,5,128]{3,1,2,0:T(2,128)S(1)}, u32[]{:S(2)}, u32[]{:S(2)}) %all-to-all-start.5) | async-done | bytes 40992 | tf_op jit(solution)/shard_map/all_to_all | solution.py:56
  132.2 0.1 divide_bitcast_fusion
  132.3 0.1 add_select_fusion
  132.4 0.7 copy.780
  (150 shorter events, 1.8 us)
Async XLA Ops:
  1.0 26.8 %collective-permute-start.1 = (f32[2,4,128]{2,1,0:T(4,128)S(1)}, f32[2,4,128]{2,1,0:T(4,128)S(1)}, u32[]{:S(2)}, u32[]{:S(2)}) collective-permute-start(f32[2,4,128]{2,1,0:T(4,128)S(1)} %bitcast.806), channel_id=1, source_target_pairs={{0,4},{4,8},{8,12},{12,16},{16,20},{20,24},{24,28},{28,32},{32,36}... | collective-permute-start | bytes 12296 | tf_op jit(solution)/shard_map/ppermute | solution.py:21
  9.9 17.9 %collective-permute-start = (f32[2,4,128]{2,1,0:T(4,128)S(1)}, f32[2,4,128]{2,1,0:T(4,128)S(1)}, u32[]{:S(2)}, u32[]{:S(2)}) collective-permute-start(f32[2,4,128]{2,1,0:T(4,128)S(1)} %bitcast.808), channel_id=1, source_target_pairs={{0,508},{4,0},{8,4},{12,8},{16,12},{20,16},{24,20},{28,24},{32,28}... | collective-permute-start | bytes 12296 | tf_op jit(solution)/shard_map/ppermute | solution.py:21
  12.3 14.6 %collective-permute-start.2 = (f32[2,4,45]{2,1,0:T(4,128)S(1)}, f32[2,4,45]{2,1,0:T(4,128)S(1)}, u32[]{:S(2)}, u32[]{:S(2)}) collective-permute-start(f32[2,4,45]{2,1,0:T(4,128)S(1)} %bitcast.802), channel_id=1, source_target_pairs={{0,1},{1,0},{2,3},{3,2},{4,5},{5,4},{6,7},{7,6},{8,9},{9,8},{10,11... | collective-permute-start | bytes 4328 | tf_op jit(solution)/shard_map/ppermute | solution.py:129
  14.7 12.1 %collective-permute-start.3 = (f32[2,4,45]{2,1,0:T(4,128)S(1)}, f32[2,4,45]{2,1,0:T(4,128)S(1)}, u32[]{:S(2)}, u32[]{:S(2)}) collective-permute-start(f32[2,4,45]{2,1,0:T(4,128)S(1)} %bitcast.803), channel_id=1, source_target_pairs={{0,256},{1,2},{2,1},{3,259},{4,260},{5,6},{6,5},{7,263},{8,264},{9... | collective-permute-start | bytes 4328 | tf_op jit(solution)/shard_map/ppermute | solution.py:130
  25.4 0.8 copy-start.1
  26.7 0.7 copy-start.2
  27.5 0.9 copy-start
  30.6 10.9 %copy-start.3 = (s32[128]{0:T(128)S(1)}, s32[128]{0:T(128)}, u32[]{:S(2)}) copy-start(s32[128]{0:T(128)} %param.7) | copy-start | bytes 1540
  30.6 17.9 %all-to-all-start = ((f32[4,2,5,128]{3,1,2,0:T(2,128)}), f32[4,2,5,128]{3,1,2,0:T(2,128)S(1)}, u32[]{:S(2)}, u32[]{:S(2)}) async-start(f32[4,2,5,128]{3,1,2,0:T(2,128)} %broadcast_in_dim.41), calls=%async_computation | async-start | bytes 40960 | tf_op jit(solution)/shard_map/all_to_all | solution.py:56
  49.1 7.5 %all-to-all-start.1 = ((f32[4,2,5,128]{3,1,2,0:T(2,128)}), f32[4,2,5,128]{3,1,2,0:T(2,128)S(1)}, u32[]{:S(2)}, u32[]{:S(2)}) async-start(f32[4,2,5,128]{3,1,2,0:T(2,128)} %broadcast_in_dim.42), calls=%async_computation.1 | async-start | bytes 40960 | tf_op jit(solution)/shard_map/all_to_all | solution.py:56
  57.3 11.8 %all-to-all-start.2 = ((f32[8,2,5,128]{3,1,2,0:T(2,128)}), f32[8,2,5,128]{3,1,2,0:T(2,128)S(1)}, u32[]{:S(2)}, u32[]{:S(2)}) async-start(f32[8,2,5,128]{3,1,2,0:T(2,128)} %broadcast_in_dim.43), calls=%async_computation.2 | async-start | bytes 81920 | tf_op jit(solution)/shard_map/all_to_all | solution.py:56
  70.9 11.6 %collective-permute-start.6 = (f32[2,4,45]{2,1,0:T(4,128)S(1)}, f32[2,4,45]{2,1,0:T(4,128)S(1)}, u32[]{:S(2)}, u32[]{:S(2)}) collective-permute-start(f32[2,4,45]{2,1,0:T(4,128)S(1)} %bitcast.805), channel_id=1, source_target_pairs={{0,1},{1,0},{2,3},{3,2},{4,5},{5,4},{6,7},{7,6},{8,9},{9,8},{10,11... | collective-permute-start | bytes 4328 | tf_op jit(solution)/shard_map/ppermute | solution.py:129
  72.9 9.6 %collective-permute-start.7 = (f32[2,4,45]{2,1,0:T(4,128)S(1)}, f32[2,4,45]{2,1,0:T(4,128)S(1)}, u32[]{:S(2)}, u32[]{:S(2)}) collective-permute-start(f32[2,4,45]{2,1,0:T(4,128)S(1)} %bitcast.804), channel_id=1, source_target_pairs={{0,256},{1,2},{2,1},{3,259},{4,260},{5,6},{6,5},{7,263},{8,264},{9... | collective-permute-start | bytes 4328 | tf_op jit(solution)/shard_map/ppermute | solution.py:130
  75.0 7.9 %collective-permute-start.5 = (f32[2,4,128]{2,1,0:T(4,128)S(1)}, f32[2,4,128]{2,1,0:T(4,128)S(1)}, u32[]{:S(2)}, u32[]{:S(2)}) collective-permute-start(f32[2,4,128]{2,1,0:T(4,128)S(1)} %bitcast.812), channel_id=1, source_target_pairs={{0,4},{4,8},{8,12},{12,16},{16,20},{20,24},{24,28},{28,32},{32,36}... | collective-permute-start | bytes 12296 | tf_op jit(solution)/shard_map/ppermute | solution.py:21
  80.2 9.1 %collective-permute-start.4 = (f32[2,4,128]{2,1,0:T(4,128)S(1)}, f32[2,4,128]{2,1,0:T(4,128)S(1)}, u32[]{:S(2)}, u32[]{:S(2)}) collective-permute-start(f32[2,4,128]{2,1,0:T(4,128)S(1)} %bitcast.810), channel_id=1, source_target_pairs={{0,508},{4,0},{8,4},{12,8},{16,12},{20,16},{24,20},{28,24},{32,28}... | collective-permute-start | bytes 12296 | tf_op jit(solution)/shard_map/ppermute | solution.py:21
  106.4 10.9 %all-to-all-start.4 = ((f32[4,2,5,128]{3,1,2,0:T(2,128)}), f32[4,2,5,128]{3,1,2,0:T(2,128)S(1)}, u32[]{:S(2)}, u32[]{:S(2)}) async-start(f32[4,2,5,128]{3,1,2,0:T(2,128)} %broadcast_in_dim.52), calls=%async_computation.4 | async-start | bytes 40960 | tf_op jit(solution)/shard_map/all_to_all | solution.py:56
  118.0 13.7 %all-to-all-start.5 = ((f32[8,2,5,128]{3,1,2,0:T(2,128)}), f32[8,2,5,128]{3,1,2,0:T(2,128)S(1)}, u32[]{:S(2)}, u32[]{:S(2)}) async-start(f32[8,2,5,128]{3,1,2,0:T(2,128)} %broadcast_in_dim.53), calls=%async_computation.5 | async-start | bytes 81920 | tf_op jit(solution)/shard_map/all_to_all | solution.py:56

commit v4 on v3

--- a/solution.py
+++ b/solution.py
@@ -50,7 +50,7 @@
 
 
 def gathered(maps, axis):
-    count = lax.axis_size(axis)
+    count = axis_count(axis)
     packed = jnp.concatenate([maps[1], maps[0][:, None]], axis=1)
     spread = jnp.broadcast_to(packed[None], (count,) + packed.shape)
     got = lax.all_to_all(spread, axis, 0, 0, tiled=False)
@@ -91,13 +91,12 @@
 
 
 def lon_inflow(own):
-    members = gathered(own, "lyc")
-    total_yc, pre_yc, suf_yc = group_parts(members, lax.axis_index("lyc"))
-    groups = gathered(total_yc, "lx")
-    total_x, pre_x, suf_x = group_parts(groups, lax.axis_index("lx"))
-    circle = gathered(total_x, "lz")
+    members = gathered(own, ("lx", "lyc"))
+    place = lax.axis_index("lx") * lax.axis_size("lyc") + lax.axis_index("lyc")
+    total, before, after = group_parts(members, place)
+    circle = gathered(total, "lz")
     rest = cyclic_rest(circle, lax.axis_index("lz"))
-    excl = compose(pre_yc, compose(pre_x, compose(rest, compose(suf_x, suf_yc))))
+    excl = compose(before, compose(rest, after))
     rate, offset = own
     return (excl[0][:, None] * offset + excl[1]) / (1.0 - excl[0] * rate)[:, None]
 

time: 135 us -> 123 us (0.911); the launches traced: 133 us -> 123 us
  blocking collectives: 14.8 us -> 0 us
  starting transfers between devices: 67.5 us -> 73 us
  waiting for transfers between devices: 35.7 us -> 32.6 us
    all_to_all x1 -> x0, blocking collectives: 14.8 us -> none  [gathered(): got = lax.all_to_all(spread, axis, 0, 0, tiled=False)]
    ppermute x4, waiting for transfers between devices: 6.38 us -> 0.28 us  [from_behind(): return lax.ppermute(value, axis, pairs)]
    all_to_all x5 -> x4, waiting for transfers between devices: 29.3 us -> 32.3 us  [gathered(): got = lax.all_to_all(spread, axis, 0, 0, tiled=False)]
    all_to_all x5 -> x4, starting transfers between devices: 32.3 us -> 34.9 us  [gathered(): got = lax.all_to_all(spread, axis, 0, 0, tiled=False)]
    ppermute x2, starting transfers between devices: 4.22 us -> 5.95 us  [halo_tendency(): got_a = lax.ppermute(jnp.where(odd, top, bottom), LON + ('lat',), pairs_a)]
    unnamed x8 -> x56, local copies, waits for them, and re-layouts: 1.59 us -> 2.74 us
    broadcast_in_dim x6 -> x4, local copies, waits for them, and re-layouts: 3.1 us -> 2.57 us  [gathered(): spread = jnp.broadcast_to(packed[None], (count,) + packed.shape)]
  transfers between devices with their start and end apart: 13 -> 12, of which waited for: 6 -> 5; matrix products, arithmetic and copies ran while one was open for 2% -> 2% of each run, Pallas kernels for 0% -> 0%
where the time goes in v4:
time: 123 us
  starting transfers between devices  73 us (59%)
  waiting for transfers between devices  32.6 us (27%)
  local copies, waits for them, and re-layouts  8.59 us (7%)
  other arithmetic  6.91 us (6%)
  between operations  1.5 us (1%)
    all_to_all x4, starting transfers between devices, gathered(): got = lax.all_to_all(spread, axis, 0, 0, tiled=False)  34.9 us
    all_to_all x4, waiting for transfers between devices, gathered(): got = lax.all_to_all(spread, axis, 0, 0, tiled=False)  32.3 us
    ppermute x4, starting transfers between devices, from_behind(): return lax.ppermute(value, axis, pairs)  19.1 us
    ppermute x2, starting transfers between devices, halo_tendency(): got_b = lax.ppermute(jnp.where(odd, bottom, top), LON + ('lat',), pairs_b)  13.1 us
    ppermute x2, starting transfers between devices, halo_tendency(): got_a = lax.ppermute(jnp.where(odd, top, bottom), LON + ('lat',), pairs_a)  5.95 us
    unnamed x56, local copies, waits for them, and re-layouts  2.74 us
    broadcast_in_dim x4, local copies, waits for them, and re-layouts, gathered(): spread = jnp.broadcast_to(packed[None], (count,) + packed.shape)  2.57 us
  transfers between devices with their start and end apart: 12, of which 5 were waited for; matrix products, arithmetic and copies ran while one was open for 2% of the time, Pallas kernels for 0%

profile of v4, /device:TPU:1, one launch (start us, length us, event | category | flops | bytes accessed | tf_op | source)
XLA Modules:
  0.0 122.5 jit_solution(13899770283876219632)
XLA Ops:
  0.0 1.0 add_multiply_fusion
  1.0 0.3 broadcast_select_fusion.2
  1.3 0.1 copy.634
  1.4 4.0 %collective-permute-start.2 = (f32[2,4,45]{2,1,0:T(4,128)S(1)}, f32[2,4,45]{2,1,0:T(4,128)S(1)}, u32[]{:S(2)}, u32[]{:S(2)}) collective-permute-start(f32[2,4,45]{2,1,0:T(4,128)S(1)} %bitcast.1155), channel_id=1, source_target_pairs={{0,1},{1,0},{2,3},{3,2},{4,5},{5,4},{6,7},{7,6},{8,9},{9,8},{10,11... | collective-permute-start | bytes 4328 | tf_op jit(solution)/shard_map/ppermute | solution.py:128
  5.5 0.1 copy.635
  5.6 10.6 %collective-permute-start.3 = (f32[2,4,45]{2,1,0:T(4,128)S(1)}, f32[2,4,45]{2,1,0:T(4,128)S(1)}, u32[]{:S(2)}, u32[]{:S(2)}) collective-permute-start(f32[2,4,45]{2,1,0:T(4,128)S(1)} %bitcast.1156), channel_id=1, source_target_pairs={{0,256},{1,2},{2,1},{3,259},{4,260},{5,6},{6,5},{7,263},{8,264},{9... | collective-permute-start | bytes 4328 | tf_op jit(solution)/shard_map/ppermute | solution.py:129
  16.3 3.1 %collective-permute-start = (f32[2,4,128]{2,1,0:T(4,128)S(1)}, f32[2,4,128]{2,1,0:T(4,128)S(1)}, u32[]{:S(2)}, u32[]{:S(2)}) collective-permute-start(f32[2,4,128]{2,1,0:T(4,128)S(1)} %bitcast.1162), channel_id=1, source_target_pairs={{0,508},{4,0},{8,4},{12,8},{16,12},{20,16},{24,20},{28,24},{32,28}... | collective-permute-start | bytes 12296 | tf_op jit(solution)/shard_map/ppermute | solution.py:21
  19.4 6.5 %collective-permute-start.1 = (f32[2,4,128]{2,1,0:T(4,128)S(1)}, f32[2,4,128]{2,1,0:T(4,128)S(1)}, u32[]{:S(2)}, u32[]{:S(2)}) collective-permute-start(f32[2,4,128]{2,1,0:T(4,128)S(1)} %bitcast.1164), channel_id=1, source_target_pairs={{0,4},{4,8},{8,12},{12,16},{16,20},{20,24},{24,28},{28,32},{32,36}... | collective-permute-start | bytes 12296 | tf_op jit(solution)/shard_map/ppermute | solution.py:21
  25.9 0.3 fusion.109
  26.2 0.1 fusion.107
  26.3 0.6 copy-done.1
  27.1 0.1 multiply_bitcast_fusion.1
  27.2 0.6 copy-done.3
  28.0 0.1 pad.39.clone
  28.1 0.6 copy-done.2
  28.7 0.1 select_bitcast_fusion.3
  28.8 0.2 copy.636
  28.9 0.2 copy.637
  29.1 0.5 copy-done
  29.7 0.7 broadcast_multiply_fusion.1
  30.4 0.1 multiply_add_fusion.11
  30.6 0.1 multiply_add_fusion.10
  30.7 0.1 multiply_add_fusion.9
  30.8 0.1 multiply_add_fusion.8
  31.0 0.1 multiply_add_fusion.7
  31.1 0.1 multiply_add_fusion.6
  31.2 0.7 broadcast_in_dim.37
  31.9 11.9 %all-to-all-start = ((f32[16,2,5,128]{3,1,2,0:T(2,128)}), f32[16,2,5,128]{3,1,2,0:T(2,128)S(1)}, u32[]{:S(2)}, u32[]{:S(2)}) async-start(f32[16,2,5,128]{3,1,2,0:T(2,128)} %broadcast_in_dim.37), calls=%async_computation | async-start | bytes 163840 | tf_op jit(solution)/shard_map/all_to_all | solution.py:56
  43.8 9.7 %all-to-all-done = f32[16,2,5,128]{3,1,2,0:T(2,128)S(1)} async-done(((f32[16,2,5,128]{3,1,2,0:T(2,128)}), f32[16,2,5,128]{3,1,2,0:T(2,128)S(1)}, u32[]{:S(2)}, u32[]{:S(2)}) %all-to-all-start) | async-done | bytes 81952 | tf_op jit(solution)/shard_map/all_to_all | solution.py:56
  54.1 0.1 multiply_add_fusion.53
  54.2 0.6 broadcast_in_dim.38
  54.8 6.6 %all-to-all-start.1 = ((f32[8,2,5,128]{3,1,2,0:T(2,128)}), f32[8,2,5,128]{3,1,2,0:T(2,128)S(1)}, u32[]{:S(2)}, u32[]{:S(2)}) async-start(f32[8,2,5,128]{3,1,2,0:T(2,128)} %broadcast_in_dim.38), calls=%async_computation.1 | async-start | bytes 81920 | tf_op jit(solution)/shard_map/all_to_all | solution.py:56
  61.9 6.6 %all-to-all-done.1 = f32[8,2,5,128]{3,1,2,0:T(2,128)S(1)} async-done(((f32[8,2,5,128]{3,1,2,0:T(2,128)}), f32[8,2,5,128]{3,1,2,0:T(2,128)S(1)}, u32[]{:S(2)}, u32[]{:S(2)}) %all-to-all-start.1) | async-done | bytes 40992 | tf_op jit(solution)/shard_map/all_to_all | solution.py:56
  69.0 0.2 broadcast_multiply_fusion.2
  69.2 0.3 broadcast_select_fusion
  69.5 0.3 fusion.106
  69.7 0.1 fusion.104
  69.9 0.1 copy.665
  70.0 1.9 %collective-permute-start.6 = (f32[2,4,45]{2,1,0:T(4,128)S(1)}, f32[2,4,45]{2,1,0:T(4,128)S(1)}, u32[]{:S(2)}, u32[]{:S(2)}) collective-permute-start(f32[2,4,45]{2,1,0:T(4,128)S(1)} %bitcast.1157), channel_id=1, source_target_pairs={{0,1},{1,0},{2,3},{3,2},{4,5},{5,4},{6,7},{7,6},{8,9},{9,8},{10,11... | collective-permute-start | bytes 4328 | tf_op jit(solution)/shard_map/ppermute | solution.py:128
  71.9 0.1 copy.666
  72.1 2.4 %collective-permute-start.7 = (f32[2,4,45]{2,1,0:T(4,128)S(1)}, f32[2,4,45]{2,1,0:T(4,128)S(1)}, u32[]{:S(2)}, u32[]{:S(2)}) collective-permute-start(f32[2,4,45]{2,1,0:T(4,128)S(1)} %bitcast.1158), channel_id=1, source_target_pairs={{0,256},{1,2},{2,1},{3,259},{4,260},{5,6},{6,5},{7,263},{8,264},{9... | collective-permute-start | bytes 4328 | tf_op jit(solution)/shard_map/ppermute | solution.py:129
  74.5 3.8 %collective-permute-start.4 = (f32[2,4,128]{2,1,0:T(4,128)S(1)}, f32[2,4,128]{2,1,0:T(4,128)S(1)}, u32[]{:S(2)}, u32[]{:S(2)}) collective-permute-start(f32[2,4,128]{2,1,0:T(4,128)S(1)} %bitcast.1166), channel_id=1, source_target_pairs={{0,508},{4,0},{8,4},{12,8},{16,12},{20,16},{24,20},{28,24},{32,28}... | collective-permute-start | bytes 12296 | tf_op jit(solution)/shard_map/ppermute | solution.py:21
  78.4 5.6 %collective-permute-start.5 = (f32[2,4,128]{2,1,0:T(4,128)S(1)}, f32[2,4,128]{2,1,0:T(4,128)S(1)}, u32[]{:S(2)}, u32[]{:S(2)}) collective-permute-start(f32[2,4,128]{2,1,0:T(4,128)S(1)} %bitcast.1168), channel_id=1, source_target_pairs={{0,4},{4,8},{8,12},{12,16},{16,20},{20,24},{24,28},{28,32},{32,36}... | collective-permute-start | bytes 12296 | tf_op jit(solution)/shard_map/ppermute | solution.py:21
  84.0 0.1 select_bitcast_fusion.1
  84.1 0.2 copy.667
  84.3 0.2 copy.668
  84.5 0.3 collective-permute-done.5
  84.8 0.8 broadcast_multiply_fusion
  85.6 0.1 multiply_add_fusion.5
  85.7 0.1 multiply_add_fusion.4
  85.9 0.1 multiply_add_fusion.3
  86.0 0.1 multiply_add_fusion.2
  86.1 0.1 multiply_add_fusion.1
  86.3 0.1 multiply_add_fusion
  86.4 0.7 broadcast_in_dim.43
  87.1 11.2 %all-to-all-start.2 = ((f32[16,2,5,128]{3,1,2,0:T(2,128)}), f32[16,2,5,128]{3,1,2,0:T(2,128)S(1)}, u32[]{:S(2)}, u32[]{:S(2)}) async-start(f32[16,2,5,128]{3,1,2,0:T(2,128)} %broadcast_in_dim.43), calls=%async_computation.2 | async-start | bytes 163840 | tf_op jit(solution)/shard_map/all_to_all | solution.py:56
  98.3 9.8 %all-to-all-done.2 = f32[16,2,5,128]{3,1,2,0:T(2,128)S(1)} async-done(((f32[16,2,5,128]{3,1,2,0:T(2,128)}), f32[16,2,5,128]{3,1,2,0:T(2,128)S(1)}, u32[]{:S(2)}, u32[]{:S(2)}) %all-to-all-start.2) | async-done | bytes 81952 | tf_op jit(solution)/shard_map/all_to_all | solution.py:56
  108.2 0.1 multiply_add_fusion.25
  108.3 0.6 broadcast_in_dim.44
  109.0 5.2 %all-to-all-start.3 = ((f32[8,2,5,128]{3,1,2,0:T(2,128)}), f32[8,2,5,128]{3,1,2,0:T(2,128)S(1)}, u32[]{:S(2)}, u32[]{:S(2)}) async-start(f32[8,2,5,128]{3,1,2,0:T(2,128)} %broadcast_in_dim.44), calls=%async_computation.3 | async-start | bytes 81920 | tf_op jit(solution)/shard_map/all_to_all | solution.py:56
  114.6 0.1 constant_dynamic-update-slice_fusion.135
  115.0 6.2 %all-to-all-done.3 = f32[8,2,5,128]{3,1,2,0:T(2,128)S(1)} async-done(((f32[8,2,5,128]{3,1,2,0:T(2,128)}), f32[8,2,5,128]{3,1,2,0:T(2,128)S(1)}, u32[]{:S(2)}, u32[]{:S(2)}) %all-to-all-start.3) | async-done | bytes 40992 | tf_op jit(solution)/shard_map/all_to_all | solution.py:56
  121.7 0.1 add_select_fusion
  121.8 0.7 copy.680
  (263 shorter events, 2.9 us)
Async XLA Ops:
  1.4 26.7 %collective-permute-start.2 = (f32[2,4,45]{2,1,0:T(4,128)S(1)}, f32[2,4,45]{2,1,0:T(4,128)S(1)}, u32[]{:S(2)}, u32[]{:S(2)}) collective-permute-start(f32[2,4,45]{2,1,0:T(4,128)S(1)} %bitcast.1155), channel_id=1, source_target_pairs={{0,1},{1,0},{2,3},{3,2},{4,5},{5,4},{6,7},{7,6},{8,9},{9,8},{10,11... | collective-permute-start | bytes 4328 | tf_op jit(solution)/shard_map/ppermute | solution.py:128
  5.6 22.5 %collective-permute-start.3 = (f32[2,4,45]{2,1,0:T(4,128)S(1)}, f32[2,4,45]{2,1,0:T(4,128)S(1)}, u32[]{:S(2)}, u32[]{:S(2)}) collective-permute-start(f32[2,4,45]{2,1,0:T(4,128)S(1)} %bitcast.1156), channel_id=1, source_target_pairs={{0,256},{1,2},{2,1},{3,259},{4,260},{5,6},{6,5},{7,263},{8,264},{9... | collective-permute-start | bytes 4328 | tf_op jit(solution)/shard_map/ppermute | solution.py:129
  16.3 12.8 %collective-permute-start = (f32[2,4,128]{2,1,0:T(4,128)S(1)}, f32[2,4,128]{2,1,0:T(4,128)S(1)}, u32[]{:S(2)}, u32[]{:S(2)}) collective-permute-start(f32[2,4,128]{2,1,0:T(4,128)S(1)} %bitcast.1162), channel_id=1, source_target_pairs={{0,508},{4,0},{8,4},{12,8},{16,12},{20,16},{24,20},{28,24},{32,28}... | collective-permute-start | bytes 12296 | tf_op jit(solution)/shard_map/ppermute | solution.py:21
  19.4 9.7 %collective-permute-start.1 = (f32[2,4,128]{2,1,0:T(4,128)S(1)}, f32[2,4,128]{2,1,0:T(4,128)S(1)}, u32[]{:S(2)}, u32[]{:S(2)}) collective-permute-start(f32[2,4,128]{2,1,0:T(4,128)S(1)} %bitcast.1164), channel_id=1, source_target_pairs={{0,4},{4,8},{8,12},{12,16},{16,20},{20,24},{24,28},{28,32},{32,36}... | collective-permute-start | bytes 12296 | tf_op jit(solution)/shard_map/ppermute | solution.py:21
  26.1 0.8 copy-start.1
  27.1 0.7 copy-start.3
  28.0 0.7 copy-start.2
  28.8 0.9 copy-start
  31.9 21.7 %all-to-all-start = ((f32[16,2,5,128]{3,1,2,0:T(2,128)}), f32[16,2,5,128]{3,1,2,0:T(2,128)S(1)}, u32[]{:S(2)}, u32[]{:S(2)}) async-start(f32[16,2,5,128]{3,1,2,0:T(2,128)} %broadcast_in_dim.37), calls=%async_computation | async-start | bytes 163840 | tf_op jit(solution)/shard_map/all_to_all | solution.py:56
  54.8 13.6 %all-to-all-start.1 = ((f32[8,2,5,128]{3,1,2,0:T(2,128)}), f32[8,2,5,128]{3,1,2,0:T(2,128)S(1)}, u32[]{:S(2)}, u32[]{:S(2)}) async-start(f32[8,2,5,128]{3,1,2,0:T(2,128)} %broadcast_in_dim.38), calls=%async_computation.1 | async-start | bytes 81920 | tf_op jit(solution)/shard_map/all_to_all | solution.py:56
  70.0 14.0 %collective-permute-start.6 = (f32[2,4,45]{2,1,0:T(4,128)S(1)}, f32[2,4,45]{2,1,0:T(4,128)S(1)}, u32[]{:S(2)}, u32[]{:S(2)}) collective-permute-start(f32[2,4,45]{2,1,0:T(4,128)S(1)} %bitcast.1157), channel_id=1, source_target_pairs={{0,1},{1,0},{2,3},{3,2},{4,5},{5,4},{6,7},{7,6},{8,9},{9,8},{10,11... | collective-permute-start | bytes 4328 | tf_op jit(solution)/shard_map/ppermute | solution.py:128
  72.1 12.0 %collective-permute-start.7 = (f32[2,4,45]{2,1,0:T(4,128)S(1)}, f32[2,4,45]{2,1,0:T(4,128)S(1)}, u32[]{:S(2)}, u32[]{:S(2)}) collective-permute-start(f32[2,4,45]{2,1,0:T(4,128)S(1)} %bitcast.1158), channel_id=1, source_target_pairs={{0,256},{1,2},{2,1},{3,259},{4,260},{5,6},{6,5},{7,263},{8,264},{9... | collective-permute-start | bytes 4328 | tf_op jit(solution)/shard_map/ppermute | solution.py:129
  74.5 9.9 %collective-permute-start.4 = (f32[2,4,128]{2,1,0:T(4,128)S(1)}, f32[2,4,128]{2,1,0:T(4,128)S(1)}, u32[]{:S(2)}, u32[]{:S(2)}) collective-permute-start(f32[2,4,128]{2,1,0:T(4,128)S(1)} %bitcast.1166), channel_id=1, source_target_pairs={{0,508},{4,0},{8,4},{12,8},{16,12},{20,16},{24,20},{28,24},{32,28}... | collective-permute-start | bytes 12296 | tf_op jit(solution)/shard_map/ppermute | solution.py:21
  78.4 6.4 %collective-permute-start.5 = (f32[2,4,128]{2,1,0:T(4,128)S(1)}, f32[2,4,128]{2,1,0:T(4,128)S(1)}, u32[]{:S(2)}, u32[]{:S(2)}) collective-permute-start(f32[2,4,128]{2,1,0:T(4,128)S(1)} %bitcast.1168), channel_id=1, source_target_pairs={{0,4},{4,8},{8,12},{12,16},{16,20},{20,24},{24,28},{28,32},{32,36}... | collective-permute-start | bytes 12296 | tf_op jit(solution)/shard_map/ppermute | solution.py:21
  87.1 21.0 %all-to-all-start.2 = ((f32[16,2,5,128]{3,1,2,0:T(2,128)}), f32[16,2,5,128]{3,1,2,0:T(2,128)S(1)}, u32[]{:S(2)}, u32[]{:S(2)}) async-start(f32[16,2,5,128]{3,1,2,0:T(2,128)} %broadcast_in_dim.43), calls=%async_computation.2 | async-start | bytes 163840 | tf_op jit(solution)/shard_map/all_to_all | solution.py:56
  109.0 12.2 %all-to-all-start.3 = ((f32[8,2,5,128]{3,1,2,0:T(2,128)}), f32[8,2,5,128]{3,1,2,0:T(2,128)S(1)}, u32[]{:S(2)}, u32[]{:S(2)}) async-start(f32[8,2,5,128]{3,1,2,0:T(2,128)} %broadcast_in_dim.44), calls=%async_computation.3 | async-start | bytes 81920 | tf_op jit(solution)/shard_map/all_to_all | solution.py:56

commit v5 on v4

--- a/solution.py
+++ b/solution.py
@@ -5,6 +5,7 @@
 
 ITERS = 2
 LON = ("lz", "lx", "lyc")
+GROUP = ("lx", "lyc")
 
 
 def axis_count(axis):
@@ -90,25 +91,25 @@
     return pick(options, index)
 
 
-def lon_inflow(own):
-    members = gathered(own, ("lx", "lyc"))
-    place = lax.axis_index("lx") * lax.axis_size("lyc") + lax.axis_index("lyc")
-    total, before, after = group_parts(members, place)
-    circle = gathered(total, "lz")
-    rest = cyclic_rest(circle, lax.axis_index("lz"))
-    excl = compose(before, compose(rest, after))
+def fixed_point(excl, own):
     rate, offset = own
     return (excl[0][:, None] * offset + excl[1]) / (1.0 - excl[0] * rate)[:, None]
 
 
-def halo_tendency(field, turning, lat_index, half_cycle):
+def group_place():
+    return lax.axis_index("lx") * lax.axis_size("lyc") + lax.axis_index("lyc")
+
+
+def lon_inflow(own):
+    total, before, after = group_parts(gathered(own, GROUP), group_place())
+    rest = cyclic_rest(gathered(total, "lz"), lax.axis_index("lz"))
+    return fixed_point(compose(before, compose(rest, after)), own)
+
+
+def lat_exchange(top, bottom, lat_index, half_cycle):
     lon_count = axis_count(LON)
     lat_count = lax.axis_size("lat")
     assert lat_count % 2 == 0
-    east = from_behind(field[:, :, 0, :], LON, -1)
-    west = from_behind(field[:, :, -1, :], LON, 1)
-    top = field[..., 0]
-    bottom = field[..., -1]
     odd = lat_index % 2 == 1
     pairs_a = []
     pairs_b = []
@@ -127,11 +128,16 @@
                 pairs_b.append((me, d * lat_count + l - 1))
     got_a = lax.ppermute(jnp.where(odd, top, bottom), LON + ("lat",), pairs_a)
     got_b = lax.ppermute(jnp.where(odd, bottom, top), LON + ("lat",), pairs_b)
-    flips = jnp.array([-1.0, -1.0, 1.0, 1.0], jnp.float32)[None, :, None]
     pole = (lat_index == 0) | (lat_index == lat_count - 1)
-    got_b = jnp.where(pole, got_b * flips, got_b)
-    north = jnp.where(odd, got_a, got_b)
-    south = jnp.where(odd, got_b, got_a)
+    got_b = jnp.where(pole, got_b * flips()[None, :, None], got_b)
+    return jnp.where(odd, got_a, got_b), jnp.where(odd, got_b, got_a)
+
+
+def flips():
+    return jnp.array([-1.0, -1.0, 1.0, 1.0], jnp.float32)
+
+
+def stencil(field, north, south, east, west, turning):
     north_rows = jnp.concatenate([north[..., None], field[..., :-1]], axis=3)
     south_rows = jnp.concatenate([field[..., 1:], south[..., None]], axis=3)
     east_cells = jnp.concatenate([field[:, :, 1:], east[:, :, None]], axis=2)
@@ -149,9 +155,12 @@
 
 
 def local(state, courant, band_mask):
-    rows = state.shape[3]
+    levels, comps, cols, rows = state.shape
     lat_index = lax.axis_index("lat")
     lat_count = lax.axis_size("lat")
+    z_index = lax.axis_index("lz")
+    z_count = lax.axis_size("lz")
+    assert z_count % 2 == 0 and ITERS == 2
     half_cycle = axis_count(LON) // 2
     total_rows = rows * lat_count
     row_ids = lat_index * rows + jnp.arange(rows, dtype=jnp.int32)
@@ -161,16 +170,36 @@
     rate = courant * inverse
     steps, carried = block_rates(rate)
     gain = carried[:, -1, :]
-    in_band = (band_mask == 1)[None, None, None, :]
-    estimate = state
-    for sweep in range(ITERS):
-        middle = 0.5 * (state + estimate)
-        star = state + halo_tendency(middle, turning, lat_index, half_cycle)
-        partial_value = block_scan(steps, star * inverse[:, None])
-        ends = partial_value[:, :, -1, :]
-        entry = lon_inflow((gain, ends))
-        solved = partial_value + carried[:, None] * entry[:, :, None, :]
-        estimate = jnp.where(in_band, solved, star)
+    band = band_mask == 1
+    in_band = band[None, None, None, :]
+
+    edge_rates = jnp.stack([rate[:, 0, :], inverse[:, 0, :]], axis=1)
+    got_east = from_behind(jnp.concatenate([state[:, :, 0, :], edge_rates], axis=1), LON, -1)
+    east, east_rates = got_east[:, :comps], got_east[:, comps:]
+    west = from_behind(state[:, :, -1, :], LON, 1)
+    north, south = lat_exchange(state[..., 0], state[..., -1], lat_index, half_cycle)
+    star = state + stencil(state, north, south, east, west, turning)
+    star_east = from_behind(star[:, :, 0, :], LON, -1)
+    star_west = from_behind(star[:, :, -1, :], LON, 1)
+    partial = block_scan(steps, star * inverse[:, None])
+    own = (gain, partial[:, :, -1, :])
+    entry = lon_inflow(own)
+    estimate = jnp.where(in_band, partial + carried[:, None] * entry[:, :, None, :], star)
+
+    band_col = band[None, None, :]
+    west = 0.5 * (west + jnp.where(band_col, entry, star_west))
+    carry_in = estimate[:, :, -1, :]
+    east_value = east_rates[:, 0:1] * carry_in + east_rates[:, 1:2] * star_east
+    east = 0.5 * (east + jnp.where(band_col, east_value, star_east))
+    middle = 0.5 * (state + estimate)
+    north, south = lat_exchange(middle[..., 0], middle[..., -1], lat_index, half_cycle)
+
+    for sweep in range(1, ITERS):
+        star = state + stencil(middle, north, south, east, west, turning)
+        partial = block_scan(steps, star * inverse[:, None])
+        own = (gain, partial[:, :, -1, :])
+        entry = lon_inflow(own)
+        estimate = jnp.where(in_band, partial + carried[:, None] * entry[:, :, None, :], star)
     return estimate
 
 

time: 123 us -> 118 us (0.959)
  waiting for transfers between devices: 32.6 us -> 28.8 us
    all_to_all x4, waiting for transfers between devices: 32.3 us -> 23 us  [gathered(): got = lax.all_to_all(spread, axis, 0, 0, tiled=False)]
    ppermute x4, waiting for transfers between devices: 0.01 us -> 5.77 us  [the longest x2 5.76 us: lat_exchange(): got_b = lax.ppermute(jnp.where(odd, bottom, top), LON + ('lat',), pairs_b)]
    unnamed x56 -> x57, local copies, waits for them, and re-layouts: 2.74 us -> 2.68 us
  transfers between devices with their start and end apart: 12 -> 12, of which waited for: 5 -> 5; matrix products, arithmetic and copies ran while one was open for 2% -> 4% of each run, Pallas kernels for 0% -> 0%
where the time goes in v5:
time: 118 us
  starting transfers between devices  72.9 us (62%)
  waiting for transfers between devices  28.8 us (24%)
  local copies, waits for them, and re-layouts  8.59 us (7%)
  other arithmetic  5.88 us (5%)
  between operations  1.62 us (1%)
    all_to_all x4, starting transfers between devices, gathered(): got = lax.all_to_all(spread, axis, 0, 0, tiled=False)  34.9 us
    all_to_all x4, waiting for transfers between devices, gathered(): got = lax.all_to_all(spread, axis, 0, 0, tiled=False)  23 us
    ppermute x4, starting transfers between devices, from_behind(): return lax.ppermute(value, axis, pairs)  19.1 us
    ppermute x2, starting transfers between devices, lat_exchange(): got_b = lax.ppermute(jnp.where(odd, bottom, top), LON + ('lat',), pairs_b)  13.1 us
    ppermute x2, starting transfers between devices, lat_exchange(): got_a = lax.ppermute(jnp.where(odd, top, bottom), LON + ('lat',), pairs_a)  5.95 us
    ppermute x2, waiting for transfers between devices, lat_exchange(): got_b = lax.ppermute(jnp.where(odd, bottom, top), LON + ('lat',), pairs_b)  5.76 us
    unnamed x57, local copies, waits for them, and re-layouts  2.68 us
    broadcast_in_dim x4, local copies, waits for them, and re-layouts, gathered(): spread = jnp.broadcast_to(packed[None], (count,) + packed.shape)  2.57 us
  transfers between devices with their start and end apart: 12, of which 5 were waited for; matrix products, arithmetic and copies ran while one was open for 4% of the time, Pallas kernels for 0%

profile of v5, /device:TPU:1, one launch (start us, length us, event | category | flops | bytes accessed | tf_op | source)
XLA Modules:
  0.0 117.8 jit_solution(8251211241309778003)
XLA Ops:
  0.0 1.0 copy.1327
  1.0 0.3 broadcast_select_fusion.2
  1.3 0.1 copy.1286
  1.4 4.0 %collective-permute-start.2 = (f32[2,4,45]{2,1,0:T(4,128)S(1)}, f32[2,4,45]{2,1,0:T(4,128)S(1)}, u32[]{:S(2)}, u32[]{:S(2)}) collective-permute-start(f32[2,4,45]{2,1,0:T(4,128)S(1)} %bitcast.1186), channel_id=1, source_target_pairs={{0,1},{1,0},{2,3},{3,2},{4,5},{5,4},{6,7},{7,6},{8,9},{9,8},{10,11... | collective-permute-start | bytes 4328 | tf_op jit(solution)/shard_map/ppermute | solution.py:129
  5.5 0.1 copy.1287
  5.6 10.6 %collective-permute-start.3 = (f32[2,4,45]{2,1,0:T(4,128)S(1)}, f32[2,4,45]{2,1,0:T(4,128)S(1)}, u32[]{:S(2)}, u32[]{:S(2)}) collective-permute-start(f32[2,4,45]{2,1,0:T(4,128)S(1)} %bitcast.1187), channel_id=1, source_target_pairs={{0,256},{1,2},{2,1},{3,259},{4,260},{5,6},{6,5},{7,263},{8,264},{9... | collective-permute-start | bytes 4328 | tf_op jit(solution)/shard_map/ppermute | solution.py:130
  16.4 3.1 %collective-permute-start = (f32[2,6,128]{2,1,0:T(8,128)S(1)}, f32[2,6,128]{2,1,0:T(8,128)S(1)}, u32[]{:S(2)}, u32[]{:S(2)}) collective-permute-start(f32[2,6,128]{2,1,0:T(8,128)S(1)} %pad_maximum_fusion.6), channel_id=1, source_target_pairs={{0,508},{4,0},{8,4},{12,8},{16,12},{20,16},{24,20},{28,24},{32,28}... | collective-permute-start | bytes 18440 | tf_op jit(solution)/shard_map/ppermute | solution.py:22
  19.5 6.5 %collective-permute-start.1 = (f32[2,4,128]{2,1,0:T(4,128)S(1)}, f32[2,4,128]{2,1,0:T(4,128)S(1)}, u32[]{:S(2)}, u32[]{:S(2)}) collective-permute-start(f32[2,4,128]{2,1,0:T(4,128)S(1)} %get-tuple-element.107), channel_id=1, source_target_pairs={{0,4},{4,8},{8,12},{12,16},{16,20},{20,24},{24,28},{28,32},{32,36}... | collective-permute-start | bytes 12296 | tf_op jit(solution)/shard_map/ppermute | solution.py:22
  26.0 0.3 fusion.117
  26.3 0.1 fusion.116
  26.8 0.0 copy-start.3
  26.8 0.6 copy-done.3
  27.5 0.1 pad.39.clone
  27.6 0.6 copy-done.2
  28.3 0.1 select_bitcast_fusion.3
  28.3 0.2 copy.1289
  28.5 0.2 copy.1291
  28.7 0.7 broadcast_multiply_fusion.2
  29.5 0.1 multiply_add_fusion.11
  29.6 0.1 multiply_add_fusion.10
  29.8 0.1 multiply_add_fusion.9
  29.9 0.1 multiply_add_fusion.8
  30.0 0.1 multiply_add_fusion.7
  30.1 0.1 multiply_add_fusion.6
  30.3 0.7 broadcast_in_dim.45
  30.9 12.9 %all-to-all-start = ((f32[16,2,5,128]{3,1,2,0:T(2,128)}), f32[16,2,5,128]{3,1,2,0:T(2,128)S(1)}, u32[]{:S(2)}, u32[]{:S(2)}) async-start(f32[16,2,5,128]{3,1,2,0:T(2,128)} %broadcast_in_dim.45), calls=%async_computation | async-start | bytes 163840 | tf_op jit(solution)/shard_map/all_to_all | solution.py:57
  43.9 2.1 %collective-permute-start.4 = (f32[2,4,128]{2,1,0:T(4,128)S(1)}, f32[2,4,128]{2,1,0:T(4,128)S(1)}, u32[]{:S(2)}, u32[]{:S(2)}) collective-permute-start(f32[2,4,128]{2,1,0:T(4,128)S(1)} %bitcast.1193), channel_id=1, source_target_pairs={{0,508},{4,0},{8,4},{12,8},{16,12},{20,16},{24,20},{28,24},{32,28}... | collective-permute-start | bytes 12296 | tf_op jit(solution)/shard_map/ppermute | solution.py:22
  46.1 7.3 %collective-permute-start.5 = (f32[2,4,128]{2,1,0:T(4,128)S(1)}, f32[2,4,128]{2,1,0:T(4,128)S(1)}, u32[]{:S(2)}, u32[]{:S(2)}) collective-permute-start(f32[2,4,128]{2,1,0:T(4,128)S(1)} %bitcast.1194), channel_id=1, source_target_pairs={{0,4},{4,8},{8,12},{12,16},{16,20},{20,24},{24,28},{28,32},{32,36}... | collective-permute-start | bytes 12296 | tf_op jit(solution)/shard_map/ppermute | solution.py:22
  53.4 0.3 all-to-all-done
  54.3 0.1 multiply_add_fusion.53
  54.4 0.6 broadcast_in_dim.46
  55.0 6.6 %all-to-all-start.1 = ((f32[8,2,5,128]{3,1,2,0:T(2,128)}), f32[8,2,5,128]{3,1,2,0:T(2,128)S(1)}, u32[]{:S(2)}, u32[]{:S(2)}) async-start(f32[8,2,5,128]{3,1,2,0:T(2,128)} %broadcast_in_dim.46), calls=%async_computation.1 | async-start | bytes 81920 | tf_op jit(solution)/shard_map/all_to_all | solution.py:57
  61.6 0.1 constant_dynamic-update-slice_fusion.55
  62.1 6.5 %all-to-all-done.1 = f32[8,2,5,128]{3,1,2,0:T(2,128)S(1)} async-done(((f32[8,2,5,128]{3,1,2,0:T(2,128)}), f32[8,2,5,128]{3,1,2,0:T(2,128)S(1)}, u32[]{:S(2)}, u32[]{:S(2)}) %all-to-all-start.1) | async-done | bytes 40992 | tf_op jit(solution)/shard_map/all_to_all | solution.py:57
  69.2 0.2 broadcast_multiply_fusion
  69.4 0.3 broadcast_select_fusion
  69.6 0.3 fusion.115
  69.9 0.1 fusion.113
  70.0 0.1 multiply_bitcast_fusion
  70.1 0.1 copy.1323
  70.2 1.9 %collective-permute-start.6 = (f32[2,4,45]{2,1,0:T(4,128)S(1)}, f32[2,4,45]{2,1,0:T(4,128)S(1)}, u32[]{:S(2)}, u32[]{:S(2)}) collective-permute-start(f32[2,4,45]{2,1,0:T(4,128)S(1)} %bitcast.1188), channel_id=1, source_target_pairs={{0,1},{1,0},{2,3},{3,2},{4,5},{5,4},{6,7},{7,6},{8,9},{9,8},{10,11... | collective-permute-start | bytes 4328 | tf_op jit(solution)/shard_map/ppermute | solution.py:129
  72.1 0.1 copy.1324
  72.3 2.4 %collective-permute-start.7 = (f32[2,4,45]{2,1,0:T(4,128)S(1)}, f32[2,4,45]{2,1,0:T(4,128)S(1)}, u32[]{:S(2)}, u32[]{:S(2)}) collective-permute-start(f32[2,4,45]{2,1,0:T(4,128)S(1)} %bitcast.1189), channel_id=1, source_target_pairs={{0,256},{1,2},{2,1},{3,259},{4,260},{5,6},{6,5},{7,263},{8,264},{9... | collective-permute-start | bytes 4328 | tf_op jit(solution)/shard_map/ppermute | solution.py:130
  74.8 5.8 %collective-permute-done.7 = f32[2,4,45]{2,1,0:T(4,128)S(1)} collective-permute-done((f32[2,4,45]{2,1,0:T(4,128)S(1)}, f32[2,4,45]{2,1,0:T(4,128)S(1)}, u32[]{:S(2)}, u32[]{:S(2)}) %collective-permute-start.7) | collective-permute-done | bytes 1472 | tf_op jit(solution)/shard_map/ppermute | solution.py:130
  80.6 0.1 select_bitcast_fusion.1
  80.6 0.2 copy.1325
  80.8 0.2 copy.1326
  81.0 0.7 broadcast_multiply_fusion.1
  81.7 0.1 multiply_add_fusion.5
  81.9 0.1 multiply_add_fusion.4
  82.0 0.1 multiply_add_fusion.3
  82.1 0.1 multiply_add_fusion.2
  82.3 0.1 multiply_add_fusion.1
  82.4 0.1 multiply_add_fusion
  82.5 0.7 broadcast_in_dim.55
  83.2 11.9 %all-to-all-start.2 = ((f32[16,2,5,128]{3,1,2,0:T(2,128)}), f32[16,2,5,128]{3,1,2,0:T(2,128)S(1)}, u32[]{:S(2)}, u32[]{:S(2)}) async-start(f32[16,2,5,128]{3,1,2,0:T(2,128)} %broadcast_in_dim.55), calls=%async_computation.2 | async-start | bytes 163840 | tf_op jit(solution)/shard_map/all_to_all | solution.py:57
  95.1 9.7 %all-to-all-done.2 = f32[16,2,5,128]{3,1,2,0:T(2,128)S(1)} async-done(((f32[16,2,5,128]{3,1,2,0:T(2,128)}), f32[16,2,5,128]{3,1,2,0:T(2,128)S(1)}, u32[]{:S(2)}, u32[]{:S(2)}) %all-to-all-start.2) | async-done | bytes 81952 | tf_op jit(solution)/shard_map/all_to_all | solution.py:57
  105.4 0.1 multiply_add_fusion.25
  105.5 0.6 broadcast_in_dim.56
  106.2 3.3 %all-to-all-start.3 = ((f32[8,2,5,128]{3,1,2,0:T(2,128)}), f32[8,2,5,128]{3,1,2,0:T(2,128)S(1)}, u32[]{:S(2)}, u32[]{:S(2)}) async-start(f32[8,2,5,128]{3,1,2,0:T(2,128)} %broadcast_in_dim.56), calls=%async_computation.3 | async-start | bytes 81920 | tf_op jit(solution)/shard_map/all_to_all | solution.py:57
  109.5 0.1 constant_dynamic-update-slice_fusion.135
  109.9 6.5 %all-to-all-done.3 = f32[8,2,5,128]{3,1,2,0:T(2,128)S(1)} async-done(((f32[8,2,5,128]{3,1,2,0:T(2,128)}), f32[8,2,5,128]{3,1,2,0:T(2,128)S(1)}, u32[]{:S(2)}, u32[]{:S(2)}) %all-to-all-start.3) | async-done | bytes 40992 | tf_op jit(solution)/shard_map/all_to_all | solution.py:57
  116.9 0.1 add_select_fusion
  117.1 0.7 copy.1339
  (274 shorter events, 2.9 us)
Async XLA Ops:
  1.3 15.0 %copy-start = (f32[2,4,45,128]{3,1,2,0:T(4,128)S(1)}, f32[2,4,45,128]{3,1,2,0:T(4,128)}, u32[]{:S(2)}) copy-start(f32[2,4,45,128]{3,1,2,0:T(4,128)} %param.5) | copy-start | bytes 552964
  1.4 26.2 %collective-permute-start.2 = (f32[2,4,45]{2,1,0:T(4,128)S(1)}, f32[2,4,45]{2,1,0:T(4,128)S(1)}, u32[]{:S(2)}, u32[]{:S(2)}) collective-permute-start(f32[2,4,45]{2,1,0:T(4,128)S(1)} %bitcast.1186), channel_id=1, source_target_pairs={{0,1},{1,0},{2,3},{3,2},{4,5},{5,4},{6,7},{7,6},{8,9},{9,8},{10,11... | collective-permute-start | bytes 4328 | tf_op jit(solution)/shard_map/ppermute | solution.py:129
  5.5 10.8 %copy-start.1 = (f32[2,45,128]{2,0,1:T(2,128)S(1)}, f32[2,45,128]{2,0,1:T(2,128)}, u32[]{:S(2)}) copy-start(f32[2,45,128]{2,0,1:T(2,128)} %param.6) | copy-start | bytes 138244
  5.6 22.0 %collective-permute-start.3 = (f32[2,4,45]{2,1,0:T(4,128)S(1)}, f32[2,4,45]{2,1,0:T(4,128)S(1)}, u32[]{:S(2)}, u32[]{:S(2)}) collective-permute-start(f32[2,4,45]{2,1,0:T(4,128)S(1)} %bitcast.1187), channel_id=1, source_target_pairs={{0,256},{1,2},{2,1},{3,259},{4,260},{5,6},{6,5},{7,263},{8,264},{9... | collective-permute-start | bytes 4328 | tf_op jit(solution)/shard_map/ppermute | solution.py:130
  16.4 12.3 %collective-permute-start = (f32[2,6,128]{2,1,0:T(8,128)S(1)}, f32[2,6,128]{2,1,0:T(8,128)S(1)}, u32[]{:S(2)}, u32[]{:S(2)}) collective-permute-start(f32[2,6,128]{2,1,0:T(8,128)S(1)} %pad_maximum_fusion.6), channel_id=1, source_target_pairs={{0,508},{4,0},{8,4},{12,8},{16,12},{20,16},{24,20},{28,24},{32,28}... | collective-permute-start | bytes 18440 | tf_op jit(solution)/shard_map/ppermute | solution.py:22
  19.5 9.1 %collective-permute-start.1 = (f32[2,4,128]{2,1,0:T(4,128)S(1)}, f32[2,4,128]{2,1,0:T(4,128)S(1)}, u32[]{:S(2)}, u32[]{:S(2)}) collective-permute-start(f32[2,4,128]{2,1,0:T(4,128)S(1)} %get-tuple-element.107), channel_id=1, source_target_pairs={{0,4},{4,8},{8,12},{12,16},{16,20},{20,24},{24,28},{28,32},{32,36}... | collective-permute-start | bytes 12296 | tf_op jit(solution)/shard_map/ppermute | solution.py:22
  26.8 0.7 copy-start.3
  27.6 0.7 copy-start.2
  30.9 22.7 %all-to-all-start = ((f32[16,2,5,128]{3,1,2,0:T(2,128)}), f32[16,2,5,128]{3,1,2,0:T(2,128)S(1)}, u32[]{:S(2)}, u32[]{:S(2)}) async-start(f32[16,2,5,128]{3,1,2,0:T(2,128)} %broadcast_in_dim.45), calls=%async_computation | async-start | bytes 163840 | tf_op jit(solution)/shard_map/all_to_all | solution.py:57
  43.9 30.8 %collective-permute-start.4 = (f32[2,4,128]{2,1,0:T(4,128)S(1)}, f32[2,4,128]{2,1,0:T(4,128)S(1)}, u32[]{:S(2)}, u32[]{:S(2)}) collective-permute-start(f32[2,4,128]{2,1,0:T(4,128)S(1)} %bitcast.1193), channel_id=1, source_target_pairs={{0,508},{4,0},{8,4},{12,8},{16,12},{20,16},{24,20},{28,24},{32,28}... | collective-permute-start | bytes 12296 | tf_op jit(solution)/shard_map/ppermute | solution.py:22
  46.1 28.7 %collective-permute-start.5 = (f32[2,4,128]{2,1,0:T(4,128)S(1)}, f32[2,4,128]{2,1,0:T(4,128)S(1)}, u32[]{:S(2)}, u32[]{:S(2)}) collective-permute-start(f32[2,4,128]{2,1,0:T(4,128)S(1)} %bitcast.1194), channel_id=1, source_target_pairs={{0,4},{4,8},{8,12},{12,16},{16,20},{20,24},{24,28},{28,32},{32,36}... | collective-permute-start | bytes 12296 | tf_op jit(solution)/shard_map/ppermute | solution.py:22
  55.0 13.6 %all-to-all-start.1 = ((f32[8,2,5,128]{3,1,2,0:T(2,128)}), f32[8,2,5,128]{3,1,2,0:T(2,128)S(1)}, u32[]{:S(2)}, u32[]{:S(2)}) async-start(f32[8,2,5,128]{3,1,2,0:T(2,128)} %broadcast_in_dim.46), calls=%async_computation.1 | async-start | bytes 81920 | tf_op jit(solution)/shard_map/all_to_all | solution.py:57
  70.2 4.6 %collective-permute-start.6 = (f32[2,4,45]{2,1,0:T(4,128)S(1)}, f32[2,4,45]{2,1,0:T(4,128)S(1)}, u32[]{:S(2)}, u32[]{:S(2)}) collective-permute-start(f32[2,4,45]{2,1,0:T(4,128)S(1)} %bitcast.1188), channel_id=1, source_target_pairs={{0,1},{1,0},{2,3},{3,2},{4,5},{5,4},{6,7},{7,6},{8,9},{9,8},{10,11... | collective-permute-start | bytes 4328 | tf_op jit(solution)/shard_map/ppermute | solution.py:129
  72.3 8.3 %collective-permute-start.7 = (f32[2,4,45]{2,1,0:T(4,128)S(1)}, f32[2,4,45]{2,1,0:T(4,128)S(1)}, u32[]{:S(2)}, u32[]{:S(2)}) collective-permute-start(f32[2,4,45]{2,1,0:T(4,128)S(1)} %bitcast.1189), channel_id=1, source_target_pairs={{0,256},{1,2},{2,1},{3,259},{4,260},{5,6},{6,5},{7,263},{8,264},{9... | collective-permute-start | bytes 4328 | tf_op jit(solution)/shard_map/ppermute | solution.py:130
  83.2 21.7 %all-to-all-start.2 = ((f32[16,2,5,128]{3,1,2,0:T(2,128)}), f32[16,2,5,128]{3,1,2,0:T(2,128)S(1)}, u32[]{:S(2)}, u32[]{:S(2)}) async-start(f32[16,2,5,128]{3,1,2,0:T(2,128)} %broadcast_in_dim.55), calls=%async_computation.2 | async-start | bytes 163840 | tf_op jit(solution)/shard_map/all_to_all | solution.py:57
  106.2 10.2 %all-to-all-start.3 = ((f32[8,2,5,128]{3,1,2,0:T(2,128)}), f32[8,2,5,128]{3,1,2,0:T(2,128)S(1)}, u32[]{:S(2)}, u32[]{:S(2)}) async-start(f32[8,2,5,128]{3,1,2,0:T(2,128)} %broadcast_in_dim.56), calls=%async_computation.3 | async-start | bytes 81920 | tf_op jit(solution)/shard_map/all_to_all | solution.py:57

commit v6 on v5

--- a/solution.py
+++ b/solution.py
@@ -59,12 +59,12 @@
 
 
 def pick(options, index):
-    rates = jnp.stack([o[0] for o in options])
-    offsets = jnp.stack([o[1] for o in options])
-    return (
-        lax.dynamic_index_in_dim(rates, index, 0, False),
-        lax.dynamic_index_in_dim(offsets, index, 0, False),
-    )
+    rate, offset = options[0]
+    for number in range(1, len(options)):
+        chosen = index == number
+        rate = jnp.where(chosen, options[number][0], rate)
+        offset = jnp.where(chosen, options[number][1], offset)
+    return rate, offset
 
 
 def group_parts(members, index):

time: 118 us -> 113 us (0.958)
  blocking collectives: 0 us -> 30.9 us
  starting transfers between devices: 72.9 us -> 53.7 us
  waiting for transfers between devices: 28.8 us -> 13.4 us
  local copies, waits for them, and re-layouts: 8.59 us -> 6.86 us
    all_to_all x0 -> x2, blocking collectives: none -> 30.9 us  [gathered(): got = lax.all_to_all(spread, axis, 0, 0, tiled=False)]
    all_to_all x4 -> x2, starting transfers between devices: 34.9 us -> 16.6 us  [gathered(): got = lax.all_to_all(spread, axis, 0, 0, tiled=False)]
    all_to_all x4 -> x2, waiting for transfers between devices: 23 us -> 7.34 us  [gathered(): got = lax.all_to_all(spread, axis, 0, 0, tiled=False)]
    ppermute x2, starting transfers between devices: 5.95 us -> 4.22 us  [lat_exchange(): got_a = lax.ppermute(jnp.where(odd, top, bottom), LON + ('lat',), pairs_a)]
    unnamed x86 -> x0, other arithmetic: 1.4 us -> none
    broadcast_in_dim x4, local copies, waits for them, and re-layouts: 2.57 us -> 1.32 us  [gathered(): spread = jnp.broadcast_to(packed[None], (count,) + packed.shape)]
    unnamed x57 -> x55, local copies, waits for them, and re-layouts: 2.68 us -> 1.45 us
  transfers between devices with their start and end apart: 12 -> 10, of which waited for: 5 -> 4; matrix products, arithmetic and copies ran while one was open for 4% -> 5% of each run, Pallas kernels for 0% -> 0%
where the time goes in v6:
time: 113 us
  starting transfers between devices  53.7 us (48%)
  blocking collectives  30.9 us (27%)
  waiting for transfers between devices  13.4 us (12%)
  local copies, waits for them, and re-layouts  6.86 us (6%)
  other arithmetic  6.42 us (6%)
  between operations  1.45 us (1%)
    all_to_all x2, blocking collectives, gathered(): got = lax.all_to_all(spread, axis, 0, 0, tiled=False)  30.9 us
    ppermute x4, starting transfers between devices, from_behind(): return lax.ppermute(value, axis, pairs)  20.1 us
    all_to_all x2, starting transfers between devices, gathered(): got = lax.all_to_all(spread, axis, 0, 0, tiled=False)  16.6 us
    ppermute x2, starting transfers between devices, lat_exchange(): got_b = lax.ppermute(jnp.where(odd, bottom, top), LON + ('lat',), pairs_b)  12.8 us
    all_to_all x2, waiting for transfers between devices, gathered(): got = lax.all_to_all(spread, axis, 0, 0, tiled=False)  7.34 us
    ppermute x2, waiting for transfers between devices, lat_exchange(): got_b = lax.ppermute(jnp.where(odd, bottom, top), LON + ('lat',), pairs_b)  5.87 us
    ppermute x2, starting transfers between devices, lat_exchange(): got_a = lax.ppermute(jnp.where(odd, top, bottom), LON + ('lat',), pairs_a)  4.22 us
  transfers between devices with their start and end apart: 10, of which 4 were waited for; matrix products, arithmetic and copies ran while one was open for 5% of the time, Pallas kernels for 0%

profile of v6, /device:TPU:1, one launch (start us, length us, event | category | flops | bytes accessed | tf_op | source)
XLA Modules:
  0.0 112.7 jit_solution(14342300288944462418)
XLA Ops:
  0.0 0.8 slice_bitcast_fusion.1
  0.8 8.8 %collective-permute-start.1 = (f32[2,4,128]{2,1,0:T(4,128)S(1)}, f32[2,4,128]{2,1,0:T(4,128)S(1)}, u32[]{:S(2)}, u32[]{:S(2)}) collective-permute-start(f32[2,4,128]{2,1,0:T(4,128)S(1)} %get-tuple-element.61), channel_id=1, source_target_pairs={{0,4},{4,8},{8,12},{12,16},{16,20},{20,24},{24,28},{28,32},{32,36}... | collective-permute-start | bytes 12296 | tf_op jit(solution)/shard_map/ppermute | solution.py:22
  9.6 0.8 copy_multiply_fusion
  10.4 0.8 pad_multiply_fusion.5
  11.3 1.9 %collective-permute-start = (f32[2,6,128]{2,1,0:T(8,128)S(1)}, f32[2,6,128]{2,1,0:T(8,128)S(1)}, u32[]{:S(2)}, u32[]{:S(2)}) collective-permute-start(f32[2,6,128]{2,1,0:T(8,128)S(1)} %pad_maximum_fusion.6), channel_id=1, source_target_pairs={{0,508},{4,0},{8,4},{12,8},{16,12},{20,16},{24,20},{28,24},{32,28}... | collective-permute-start | bytes 18440 | tf_op jit(solution)/shard_map/ppermute | solution.py:22
  13.2 0.1 copy.2475
  13.3 0.3 broadcast_select_fusion.2
  13.6 0.1 copy.2420
  13.7 2.3 %collective-permute-start.2 = (f32[2,4,45]{2,1,0:T(4,128)S(1)}, f32[2,4,45]{2,1,0:T(4,128)S(1)}, u32[]{:S(2)}, u32[]{:S(2)}) collective-permute-start(f32[2,4,45]{2,1,0:T(4,128)S(1)} %bitcast.623), channel_id=1, source_target_pairs={{0,1},{1,0},{2,3},{3,2},{4,5},{5,4},{6,7},{7,6},{8,9},{9,8},{10,11... | collective-permute-start | bytes 4328 | tf_op jit(solution)/shard_map/ppermute | solution.py:129
  16.0 0.1 copy.2421
  16.2 10.6 %collective-permute-start.3 = (f32[2,4,45]{2,1,0:T(4,128)S(1)}, f32[2,4,45]{2,1,0:T(4,128)S(1)}, u32[]{:S(2)}, u32[]{:S(2)}) collective-permute-start(f32[2,4,45]{2,1,0:T(4,128)S(1)} %bitcast.624), channel_id=1, source_target_pairs={{0,256},{1,2},{2,1},{3,259},{4,260},{5,6},{6,5},{7,263},{8,264},{9... | collective-permute-start | bytes 4328 | tf_op jit(solution)/shard_map/ppermute | solution.py:130
  26.9 0.1 fusion.53
  27.0 0.3 fusion.54
  27.3 0.7 copy-done.2
  28.4 0.1 pad.39.clone
  28.5 0.6 copy-done.1
  29.1 0.1 select_bitcast_fusion.3
  29.2 0.2 copy.2423
  29.3 0.2 copy.2425
  29.6 0.7 broadcast_multiply_fusion.2
  30.3 0.1 multiply_add_fusion.11
  30.5 0.1 multiply_add_fusion.10
  30.6 0.1 multiply_add_fusion.9
  30.7 0.1 multiply_add_fusion.8
  30.9 0.1 multiply_add_fusion.7
  31.0 0.1 multiply_add_fusion.6
  31.1 0.7 broadcast_in_dim.45
  31.8 10.6 %all-to-all-start = ((f32[16,2,5,128]{3,1,2,0:T(2,128)}), f32[16,2,5,128]{3,1,2,0:T(2,128)S(1)}, u32[]{:S(2)}, u32[]{:S(2)}) async-start(f32[16,2,5,128]{3,1,2,0:T(2,128)} %broadcast_in_dim.45), calls=%async_computation | async-start | bytes 163840 | tf_op jit(solution)/shard_map/all_to_all | solution.py:57
  42.4 7.5 %collective-permute-start.5 = (f32[2,4,128]{2,1,0:T(4,128)S(1)}, f32[2,4,128]{2,1,0:T(4,128)S(1)}, u32[]{:S(2)}, u32[]{:S(2)}) collective-permute-start(f32[2,4,128]{2,1,0:T(4,128)S(1)} %bitcast.636), channel_id=1, source_target_pairs={{0,4},{4,8},{8,12},{12,16},{16,20},{20,24},{24,28},{28,32},{32,36}... | collective-permute-start | bytes 12296 | tf_op jit(solution)/shard_map/ppermute | solution.py:22
  49.9 1.9 %collective-permute-start.4 = (f32[2,4,128]{2,1,0:T(4,128)S(1)}, f32[2,4,128]{2,1,0:T(4,128)S(1)}, u32[]{:S(2)}, u32[]{:S(2)}) collective-permute-start(f32[2,4,128]{2,1,0:T(4,128)S(1)} %bitcast.635), channel_id=1, source_target_pairs={{0,508},{4,0},{8,4},{12,8},{16,12},{20,16},{24,20},{28,24},{32,28}... | collective-permute-start | bytes 12296 | tf_op jit(solution)/shard_map/ppermute | solution.py:22
  51.8 0.4 all-to-all-done
  52.5 0.1 multiply_add_fusion.27
  52.6 0.6 broadcast_in_dim.46
  53.2 6.0 %all-to-all-start.1 = ((f32[8,2,5,128]{3,1,2,0:T(2,128)}), f32[8,2,5,128]{3,1,2,0:T(2,128)S(1)}, u32[]{:S(2)}, u32[]{:S(2)}) async-start(f32[8,2,5,128]{3,1,2,0:T(2,128)} %broadcast_in_dim.46), calls=%async_computation.1 | async-start | bytes 81920 | tf_op jit(solution)/shard_map/all_to_all | solution.py:57
  59.2 7.0 %all-to-all-done.1 = f32[8,2,5,128]{3,1,2,0:T(2,128)S(1)} async-done(((f32[8,2,5,128]{3,1,2,0:T(2,128)}), f32[8,2,5,128]{3,1,2,0:T(2,128)S(1)}, u32[]{:S(2)}, u32[]{:S(2)}) %all-to-all-start.1) | async-done | bytes 40992 | tf_op jit(solution)/shard_map/all_to_all | solution.py:57
  66.3 0.1 multiply_subtract_fusion.1
  66.5 0.2 multiply_bitcast_fusion.2
  66.7 0.2 broadcast_multiply_fusion
  66.9 0.1 fusion.50
  67.0 0.3 broadcast_select_fusion
  67.3 0.3 fusion.52
  67.6 0.1 copy.2472
  67.7 0.1 copy.2471
  67.9 1.9 %collective-permute-start.6 = (f32[2,4,45]{2,1,0:T(4,128)S(1)}, f32[2,4,45]{2,1,0:T(4,128)S(1)}, u32[]{:S(2)}, u32[]{:S(2)}) collective-permute-start(f32[2,4,45]{2,1,0:T(4,128)S(1)} %bitcast.626), channel_id=1, source_target_pairs={{0,1},{1,0},{2,3},{3,2},{4,5},{5,4},{6,7},{7,6},{8,9},{9,8},{10,11... | collective-permute-start | bytes 4328 | tf_op jit(solution)/shard_map/ppermute | solution.py:129
  69.8 2.1 %collective-permute-start.7 = (f32[2,4,45]{2,1,0:T(4,128)S(1)}, f32[2,4,45]{2,1,0:T(4,128)S(1)}, u32[]{:S(2)}, u32[]{:S(2)}) collective-permute-start(f32[2,4,45]{2,1,0:T(4,128)S(1)} %bitcast.625), channel_id=1, source_target_pairs={{0,256},{1,2},{2,1},{3,259},{4,260},{5,6},{6,5},{7,263},{8,264},{9... | collective-permute-start | bytes 4328 | tf_op jit(solution)/shard_map/ppermute | solution.py:130
  72.0 0.2 collective-permute-done.6
  72.2 5.9 %collective-permute-done.7 = f32[2,4,45]{2,1,0:T(4,128)S(1)} collective-permute-done((f32[2,4,45]{2,1,0:T(4,128)S(1)}, f32[2,4,45]{2,1,0:T(4,128)S(1)}, u32[]{:S(2)}, u32[]{:S(2)}) %collective-permute-start.7) | collective-permute-done | bytes 1472 | tf_op jit(solution)/shard_map/ppermute | solution.py:130
  78.1 0.1 select_bitcast_fusion.1
  78.1 0.2 copy.2473
  78.3 0.2 copy.2474
  78.5 0.7 broadcast_multiply_fusion.1
  79.2 0.1 multiply_add_fusion.5
  79.4 0.1 multiply_add_fusion.4
  79.5 0.1 multiply_add_fusion.3
  79.7 0.1 multiply_add_fusion.2
  79.8 0.1 multiply_add_fusion.1
  79.9 0.1 multiply_add_fusion
  80.1 21.5 %all_to_all.20 = f32[16,2,5,128]{3,1,2,0:T(2,128)S(1)} all-to-all(f32[16,2,5,128]{3,1,2,0:T(2,128)S(1)} %broadcast_in_dim.55), channel_id=1, replica_groups=mesh['lz'=8,'lx'=4,'lyc'=4,'lat'=4] {'lx','lyc'}, dimensions={0} | all-to-all | bytes 163840 | tf_op jit(solution)/shard_map/all_to_all | solution.py:57
  102.0 0.1 multiply_add_fusion.12
  102.1 9.3 %all_to_all.21 = f32[8,2,5,128]{3,1,2,0:T(2,128)S(1)} all-to-all(f32[8,2,5,128]{3,1,2,0:T(2,128)S(1)} %broadcast_in_dim.56), channel_id=1, replica_groups=mesh['lz'=8,'lx'=4,'lyc'=4,'lat'=4] {'lz'}, dimensions={0} | all-to-all | bytes 81920 | tf_op jit(solution)/shard_map/all_to_all | solution.py:57
  111.6 0.1 multiply_subtract_fusion
  111.7 0.2 add_divide_fusion.1
  111.9 0.1 add_select_fusion
  112.0 0.7 copy.2504
  (162 shorter events, 1.2 us)
Async XLA Ops:
  0.0 13.2 %copy-start = (f32[2,4,45,128]{3,1,2,0:T(4,128)S(1)}, f32[2,4,45,128]{3,1,2,0:T(4,128)}, u32[]{:S(2)}) copy-start(f32[2,4,45,128]{3,1,2,0:T(4,128)} %param.5) | copy-start | bytes 552964
  0.8 28.7 %collective-permute-start.1 = (f32[2,4,128]{2,1,0:T(4,128)S(1)}, f32[2,4,128]{2,1,0:T(4,128)S(1)}, u32[]{:S(2)}, u32[]{:S(2)}) collective-permute-start(f32[2,4,128]{2,1,0:T(4,128)S(1)} %get-tuple-element.61), channel_id=1, source_target_pairs={{0,4},{4,8},{8,12},{12,16},{16,20},{20,24},{24,28},{28,32},{32,36}... | collective-permute-start | bytes 12296 | tf_op jit(solution)/shard_map/ppermute | solution.py:22
  11.3 18.3 %collective-permute-start = (f32[2,6,128]{2,1,0:T(8,128)S(1)}, f32[2,6,128]{2,1,0:T(8,128)S(1)}, u32[]{:S(2)}, u32[]{:S(2)}) collective-permute-start(f32[2,6,128]{2,1,0:T(8,128)S(1)} %pad_maximum_fusion.6), channel_id=1, source_target_pairs={{0,508},{4,0},{8,4},{12,8},{16,12},{20,16},{24,20},{28,24},{32,28}... | collective-permute-start | bytes 18440 | tf_op jit(solution)/shard_map/ppermute | solution.py:22
  13.7 14.8 %collective-permute-start.2 = (f32[2,4,45]{2,1,0:T(4,128)S(1)}, f32[2,4,45]{2,1,0:T(4,128)S(1)}, u32[]{:S(2)}, u32[]{:S(2)}) collective-permute-start(f32[2,4,45]{2,1,0:T(4,128)S(1)} %bitcast.623), channel_id=1, source_target_pairs={{0,1},{1,0},{2,3},{3,2},{4,5},{5,4},{6,7},{7,6},{8,9},{9,8},{10,11... | collective-permute-start | bytes 4328 | tf_op jit(solution)/shard_map/ppermute | solution.py:129
  16.2 12.3 %collective-permute-start.3 = (f32[2,4,45]{2,1,0:T(4,128)S(1)}, f32[2,4,45]{2,1,0:T(4,128)S(1)}, u32[]{:S(2)}, u32[]{:S(2)}) collective-permute-start(f32[2,4,45]{2,1,0:T(4,128)S(1)} %bitcast.624), channel_id=1, source_target_pairs={{0,256},{1,2},{2,1},{3,259},{4,260},{5,6},{6,5},{7,263},{8,264},{9... | collective-permute-start | bytes 4328 | tf_op jit(solution)/shard_map/ppermute | solution.py:130
  27.3 0.7 copy-start.2
  28.4 0.7 copy-start.1
  31.8 20.4 %all-to-all-start = ((f32[16,2,5,128]{3,1,2,0:T(2,128)}), f32[16,2,5,128]{3,1,2,0:T(2,128)S(1)}, u32[]{:S(2)}, u32[]{:S(2)}) async-start(f32[16,2,5,128]{3,1,2,0:T(2,128)} %broadcast_in_dim.45), calls=%async_computation | async-start | bytes 163840 | tf_op jit(solution)/shard_map/all_to_all | solution.py:57
  42.4 24.1 %collective-permute-start.5 = (f32[2,4,128]{2,1,0:T(4,128)S(1)}, f32[2,4,128]{2,1,0:T(4,128)S(1)}, u32[]{:S(2)}, u32[]{:S(2)}) collective-permute-start(f32[2,4,128]{2,1,0:T(4,128)S(1)} %bitcast.636), channel_id=1, source_target_pairs={{0,4},{4,8},{8,12},{12,16},{16,20},{20,24},{24,28},{28,32},{32,36}... | collective-permute-start | bytes 12296 | tf_op jit(solution)/shard_map/ppermute | solution.py:22
  49.9 22.1 %collective-permute-start.4 = (f32[2,4,128]{2,1,0:T(4,128)S(1)}, f32[2,4,128]{2,1,0:T(4,128)S(1)}, u32[]{:S(2)}, u32[]{:S(2)}) collective-permute-start(f32[2,4,128]{2,1,0:T(4,128)S(1)} %bitcast.635), channel_id=1, source_target_pairs={{0,508},{4,0},{8,4},{12,8},{16,12},{20,16},{24,20},{28,24},{32,28}... | collective-permute-start | bytes 12296 | tf_op jit(solution)/shard_map/ppermute | solution.py:22
  53.2 12.9 %all-to-all-start.1 = ((f32[8,2,5,128]{3,1,2,0:T(2,128)}), f32[8,2,5,128]{3,1,2,0:T(2,128)S(1)}, u32[]{:S(2)}, u32[]{:S(2)}) async-start(f32[8,2,5,128]{3,1,2,0:T(2,128)} %broadcast_in_dim.46), calls=%async_computation.1 | async-start | bytes 81920 | tf_op jit(solution)/shard_map/all_to_all | solution.py:57
  67.9 4.4 %collective-permute-start.6 = (f32[2,4,45]{2,1,0:T(4,128)S(1)}, f32[2,4,45]{2,1,0:T(4,128)S(1)}, u32[]{:S(2)}, u32[]{:S(2)}) collective-permute-start(f32[2,4,45]{2,1,0:T(4,128)S(1)} %bitcast.626), channel_id=1, source_target_pairs={{0,1},{1,0},{2,3},{3,2},{4,5},{5,4},{6,7},{7,6},{8,9},{9,8},{10,11... | collective-permute-start | bytes 4328 | tf_op jit(solution)/shard_map/ppermute | solution.py:129
  69.8 8.3 %collective-permute-start.7 = (f32[2,4,45]{2,1,0:T(4,128)S(1)}, f32[2,4,45]{2,1,0:T(4,128)S(1)}, u32[]{:S(2)}, u32[]{:S(2)}) collective-permute-start(f32[2,4,45]{2,1,0:T(4,128)S(1)} %bitcast.625), channel_id=1, source_target_pairs={{0,256},{1,2},{2,1},{3,259},{4,260},{5,6},{6,5},{7,263},{8,264},{9... | collective-permute-start | bytes 4328 | tf_op jit(solution)/shard_map/ppermute | solution.py:130

commit v7 on v6

--- a/solution.py
+++ b/solution.py
@@ -154,6 +154,19 @@
     return result + coriolis
 
 
+def column_star(field, east, west, north_end, south_end, turning):
+    north_rows = jnp.concatenate([north_end[..., None], field[..., :-1]], axis=-1)
+    south_rows = jnp.concatenate([field[..., 1:], south_end[..., None]], axis=-1)
+    u_wind = field[:, 0:1]
+    v_wind = field[:, 1:2]
+    result = 0.1 * (east + west - 2.0 * field) + 0.1 * (north_rows + south_rows - 2.0 * field)
+    result = result - 0.25 * v_wind * (north_rows - south_rows)
+    coriolis = jnp.concatenate(
+        [turning * v_wind, -turning * u_wind, jnp.zeros_like(field[:, 2:])], axis=1
+    )
+    return field + (result + coriolis)
+
+
 def local(state, courant, band_mask):
     levels, comps, cols, rows = state.shape
     lat_index = lax.axis_index("lat")
@@ -174,25 +187,38 @@
     in_band = band[None, None, None, :]
 
     edge_rates = jnp.stack([rate[:, 0, :], inverse[:, 0, :]], axis=1)
-    got_east = from_behind(jnp.concatenate([state[:, :, 0, :], edge_rates], axis=1), LON, -1)
-    east, east_rates = got_east[:, :comps], got_east[:, comps:]
-    west = from_behind(state[:, :, -1, :], LON, 1)
+    east_message = jnp.concatenate([state[:, :, 0, :], state[:, :, 1, :], edge_rates], axis=1)
+    got_east = from_behind(east_message, LON, -1)
+    east, east_next = got_east[:, :comps], got_east[:, comps:2 * comps]
+    east_rates = got_east[:, 2 * comps:]
+    got_west = from_behind(jnp.concatenate([state[:, :, -1, :], state[:, :, -2, :]], axis=1), LON, 1)
+    west, west_next = got_west[:, :comps], got_west[:, comps:]
     north, south = lat_exchange(state[..., 0], state[..., -1], lat_index, half_cycle)
     star = state + stencil(state, north, south, east, west, turning)
-    star_east = from_behind(star[:, :, 0, :], LON, -1)
-    star_west = from_behind(star[:, :, -1, :], LON, 1)
     partial = block_scan(steps, star * inverse[:, None])
     own = (gain, partial[:, :, -1, :])
     entry = lon_inflow(own)
     estimate = jnp.where(in_band, partial + carried[:, None] * entry[:, :, None, :], star)
+
+    middle = 0.5 * (state + estimate)
+    top = jnp.concatenate([middle[..., 0], east[..., 0][..., None], west[..., 0][..., None]], axis=2)
+    bottom = jnp.concatenate(
+        [middle[..., -1], east[..., -1][..., None], west[..., -1][..., None]], axis=2
+    )
+    got_north, got_south = lat_exchange(top, bottom, lat_index, half_cycle)
+    star_east = column_star(
+        east, east_next, state[:, :, -1, :], got_north[..., cols], got_south[..., cols], turning
+    )
+    star_west = column_star(
+        west, state[:, :, 0, :], west_next, got_north[..., cols + 1], got_south[..., cols + 1], turning
+    )
 
     band_col = band[None, None, :]
     west = 0.5 * (west + jnp.where(band_col, entry, star_west))
     carry_in = estimate[:, :, -1, :]
     east_value = east_rates[:, 0:1] * carry_in + east_rates[:, 1:2] * star_east
     east = 0.5 * (east + jnp.where(band_col, east_value, star_east))
-    middle = 0.5 * (state + estimate)
-    north, south = lat_exchange(middle[..., 0], middle[..., -1], lat_index, half_cycle)
+    north, south = got_north[..., :cols], got_south[..., :cols]
 
     for sweep in range(1, ITERS):
         star = state + stencil(middle, north, south, east, west, turning)

time: 113 us -> 104 us (0.920)
  starting transfers between devices: 53.7 us -> 43.8 us
  waiting for transfers between devices: 13.4 us -> 20.7 us
  blocking collectives: 30.9 us -> 26.9 us
  other arithmetic: 6.42 us -> 3.69 us
    ppermute x4 -> x2, starting transfers between devices: 20.1 us -> 10.9 us  [from_behind(): return lax.ppermute(value, axis, pairs)]
    all_to_all x2, waiting for transfers between devices: 7.34 us -> 16.6 us  [gathered(): got = lax.all_to_all(spread, axis, 0, 0, tiled=False)]
    all_to_all x2, blocking collectives: 30.9 us -> 26.9 us  [gathered(): got = lax.all_to_all(spread, axis, 0, 0, tiled=False)]
    ppermute x2, waiting for transfers between devices: 5.87 us -> 3.27 us  [lat_exchange(): got_b = lax.ppermute(jnp.where(odd, bottom, top), LON + ('lat',), pairs_b)]
  transfers between devices with their start and end apart: 10 -> 8, of which waited for: 4 -> 4; matrix products, arithmetic and copies ran while one was open for 5% -> 2% of each run, Pallas kernels for 0% -> 0%
where the time goes in v7:
time: 104 us; the launch traced here: 103 us
  starting transfers between devices  43.8 us (42%)
  blocking collectives  26.9 us (26%)
  waiting for transfers between devices  20.7 us (20%)
  local copies, waits for them, and re-layouts  6.66 us (6%)
  other arithmetic  3.69 us (4%)
  between operations  1.29 us (1%)
    all_to_all x2, blocking collectives, gathered(): got = lax.all_to_all(spread, axis, 0, 0, tiled=False)  26.9 us
    all_to_all x2, waiting for transfers between devices, gathered(): got = lax.all_to_all(spread, axis, 0, 0, tiled=False)  16.6 us
    all_to_all x2, starting transfers between devices, gathered(): got = lax.all_to_all(spread, axis, 0, 0, tiled=False)  15.5 us
    ppermute x2, starting transfers between devices, lat_exchange(): got_b = lax.ppermute(jnp.where(odd, bottom, top), LON + ('lat',), pairs_b)  13.1 us
    ppermute x2, starting transfers between devices, from_behind(): return lax.ppermute(value, axis, pairs)  10.9 us
    ppermute x2, starting transfers between devices, lat_exchange(): got_a = lax.ppermute(jnp.where(odd, top, bottom), LON + ('lat',), pairs_a)  4.39 us
    ppermute x2, waiting for transfers between devices, lat_exchange(): got_b = lax.ppermute(jnp.where(odd, bottom, top), LON + ('lat',), pairs_b)  3.27 us
  transfers between devices with their start and end apart: 8, of which 4 were waited for; matrix products, arithmetic and copies ran while one was open for 2% of the time, Pallas kernels for 0%

profile of v7, /device:TPU:1, one launch (start us, length us, event | category | flops | bytes accessed | tf_op | source)
XLA Modules:
  0.0 103.1 jit_solution(16093674547734686112)
XLA Ops:
  0.0 0.7 slice_bitcast_fusion.8
  0.8 9.0 %collective-permute-start.1 = (f32[2,8,128]{2,1,0:T(8,128)S(1)}, f32[2,8,128]{2,1,0:T(8,128)S(1)}, u32[]{:S(2)}, u32[]{:S(2)}) collective-permute-start(f32[2,8,128]{2,1,0:T(8,128)S(1)} %pad_maximum_fusion.7), channel_id=1, source_target_pairs={{0,4},{4,8},{8,12},{12,16},{16,20},{20,24},{24,28},{28,32},{32,36}... | collective-permute-start | bytes 24584 | tf_op jit(solution)/shard_map/ppermute | solution.py:22
  9.8 1.9 %collective-permute-start = (f32[2,10,128]{2,1,0:T(8,128)S(1)}, f32[2,10,128]{2,1,0:T(8,128)S(1)}, u32[]{:S(2)}, u32[]{:S(2)}) collective-permute-start(f32[2,10,128]{2,1,0:T(8,128)S(1)} %pad_maximum_fusion.4), channel_id=1, source_target_pairs={{0,508},{4,0},{8,4},{12,8},{16,12},{20,16},{24,20},{28,24},{32,28}... | collective-permute-start | bytes 30728 | tf_op jit(solution)/shard_map/ppermute | solution.py:22
  11.8 0.2 fusion.72
  12.0 0.1 copy.272
  12.1 0.1 copy.271
  12.3 10.6 %collective-permute-start.3 = (f32[2,4,45]{2,1,0:T(4,128)S(1)}, f32[2,4,45]{2,1,0:T(4,128)S(1)}, u32[]{:S(2)}, u32[]{:S(2)}) collective-permute-start(f32[2,4,45]{2,1,0:T(4,128)S(1)} %get-tuple-element.157), channel_id=1, source_target_pairs={{0,256},{1,2},{2,1},{3,259},{4,260},{5,6},{6,5},{7,263},{8,264},{9... | collective-permute-start | bytes 4328 | tf_op jit(solution)/shard_map/ppermute | solution.py:130
  22.9 1.9 %collective-permute-start.2 = (f32[2,4,45]{2,1,0:T(4,128)S(1)}, f32[2,4,45]{2,1,0:T(4,128)S(1)}, u32[]{:S(2)}, u32[]{:S(2)}) collective-permute-start(f32[2,4,45]{2,1,0:T(4,128)S(1)} %get-tuple-element.158), channel_id=1, source_target_pairs={{0,1},{1,0},{2,3},{3,2},{4,5},{5,4},{6,7},{7,6},{8,9},{9,8},{10,11... | collective-permute-start | bytes 4328 | tf_op jit(solution)/shard_map/ppermute | solution.py:129
  25.0 0.2 fusion.71
  25.2 0.7 copy-done.3
  26.0 0.1 slice_multiply_fusion.5
  26.4 0.1 pad.59.clone
  26.4 0.8 collective-permute-done.2
  27.3 0.1 select_bitcast_fusion.1
  27.3 0.2 copy.198
  27.5 0.2 copy.200
  27.7 0.1 fusion.81
  27.8 0.1 fusion.82
  27.9 0.4 broadcast_multiply_fusion.2
  28.3 0.1 multiply_add_fusion.11
  28.4 0.1 multiply_add_fusion.10
  28.5 0.1 multiply_add_fusion.9
  28.7 0.1 multiply_add_fusion.8
  28.8 0.1 multiply_add_fusion.7
  28.9 0.1 multiply_add_fusion.6
  29.0 0.7 broadcast_in_dim.45
  29.6 11.2 %all-to-all-start = ((f32[16,2,5,128]{3,1,2,0:T(2,128)}), f32[16,2,5,128]{3,1,2,0:T(2,128)S(1)}, u32[]{:S(2)}, u32[]{:S(2)}) async-start(f32[16,2,5,128]{3,1,2,0:T(2,128)} %broadcast_in_dim.45), calls=%async_computation | async-start | bytes 163840 | tf_op jit(solution)/shard_map/all_to_all | solution.py:57
  40.9 0.1 fusion.79
  40.9 0.1 fusion.78
  41.0 9.6 %all-to-all-done = f32[16,2,5,128]{3,1,2,0:T(2,128)S(1)} async-done(((f32[16,2,5,128]{3,1,2,0:T(2,128)}), f32[16,2,5,128]{3,1,2,0:T(2,128)S(1)}, u32[]{:S(2)}, u32[]{:S(2)}) %all-to-all-start) | async-done | bytes 81952 | tf_op jit(solution)/shard_map/all_to_all | solution.py:57
  51.0 0.6 broadcast_in_dim.46
  51.7 4.3 %all-to-all-start.1 = ((f32[8,2,5,128]{3,1,2,0:T(2,128)}), f32[8,2,5,128]{3,1,2,0:T(2,128)S(1)}, u32[]{:S(2)}, u32[]{:S(2)}) async-start(f32[8,2,5,128]{3,1,2,0:T(2,128)} %broadcast_in_dim.46), calls=%async_computation.1 | async-start | bytes 81920 | tf_op jit(solution)/shard_map/all_to_all | solution.py:57
  56.0 7.0 %all-to-all-done.1 = f32[8,2,5,128]{3,1,2,0:T(2,128)S(1)} async-done(((f32[8,2,5,128]{3,1,2,0:T(2,128)}), f32[8,2,5,128]{3,1,2,0:T(2,128)S(1)}, u32[]{:S(2)}, u32[]{:S(2)}) %all-to-all-start.1) | async-done | bytes 40992 | tf_op jit(solution)/shard_map/all_to_all | solution.py:57
  63.1 0.1 multiply_subtract_fusion.1
  63.2 0.2 add_divide_fusion.2
  63.4 0.1 broadcast_multiply_fusion
  63.6 0.2 fusion.68
  63.7 0.2 fusion.69
  63.9 0.1 copy.239
  64.0 0.2 copy.240
  64.2 0.1 broadcast_select_fusion
  64.3 2.4 %collective-permute-start.5 = (f32[2,4,47]{2,1,0:T(4,128)S(1)}, f32[2,4,47]{2,1,0:T(4,128)S(1)}, u32[]{:S(2)}, u32[]{:S(2)}) collective-permute-start(f32[2,4,47]{2,1,0:T(4,128)S(1)} %get-tuple-element.117), channel_id=1, source_target_pairs={{0,256},{1,2},{2,1},{3,259},{4,260},{5,6},{6,5},{7,263},{8,264},{9... | collective-permute-start | bytes 4520 | tf_op jit(solution)/shard_map/ppermute | solution.py:130
  66.7 2.5 %collective-permute-start.4 = (f32[2,4,47]{2,1,0:T(4,128)S(1)}, f32[2,4,47]{2,1,0:T(4,128)S(1)}, u32[]{:S(2)}, u32[]{:S(2)}) collective-permute-start(f32[2,4,47]{2,1,0:T(4,128)S(1)} %get-tuple-element.118), channel_id=1, source_target_pairs={{0,1},{1,0},{2,3},{3,2},{4,5},{5,4},{6,7},{7,6},{8,9},{9,8},{10,11... | collective-permute-start | bytes 4520 | tf_op jit(solution)/shard_map/ppermute | solution.py:129
  69.2 0.1 slice_multiply_fusion.3
  69.3 3.3 %collective-permute-done.5 = f32[2,4,47]{2,1,0:T(4,128)S(1)} collective-permute-done((f32[2,4,47]{2,1,0:T(4,128)S(1)}, f32[2,4,47]{2,1,0:T(4,128)S(1)}, u32[]{:S(2)}, u32[]{:S(2)}) %collective-permute-start.5) | collective-permute-done | bytes 1536 | tf_op jit(solution)/shard_map/ppermute | solution.py:130
  72.6 0.1 fusion.57
  72.6 0.1 fusion.85
  72.7 0.1 fusion.84
  72.8 0.2 copy.242
  73.0 0.2 copy.241
  73.1 0.1 multiply_bitcast_fusion
  73.2 0.1 fusion.55
  73.3 0.4 broadcast_multiply_fusion.1
  73.8 0.1 multiply_add_fusion.5
  73.9 0.1 multiply_add_fusion.4
  74.0 0.1 multiply_add_fusion.3
  74.1 0.1 multiply_add_fusion.2
  74.2 0.1 multiply_add_fusion.1
  74.4 15.3 %all_to_all.20 = f32[16,2,5,128]{3,1,2,0:T(2,128)S(1)} all-to-all(f32[16,2,5,128]{3,1,2,0:T(2,128)S(1)} %broadcast_in_dim.55), channel_id=1, replica_groups=mesh['lz'=8,'lx'=4,'lyc'=4,'lat'=4] {'lx','lyc'}, dimensions={0} | all-to-all | bytes 163840 | tf_op jit(solution)/shard_map/all_to_all | solution.py:57
  90.2 11.7 %all_to_all.21 = f32[8,2,5,128]{3,1,2,0:T(2,128)S(1)} all-to-all(f32[8,2,5,128]{3,1,2,0:T(2,128)S(1)} %broadcast_in_dim.56), channel_id=1, replica_groups=mesh['lz'=8,'lx'=4,'lyc'=4,'lat'=4] {'lz'}, dimensions={0} | all-to-all | bytes 81920 | tf_op jit(solution)/shard_map/all_to_all | solution.py:57
  102.0 0.1 multiply_subtract_fusion
  102.1 0.2 add_divide_fusion.1
  102.3 0.1 add_select_fusion
  102.4 0.7 copy.270
  (161 shorter events, 1.4 us)
Async XLA Ops:
  0.0 9.7 %copy-start.1 = (f32[2,45,128]{2,0,1:T(2,128)S(1)}, f32[2,45,128]{2,0,1:T(2,128)}, u32[]{:S(2)}) copy-start(f32[2,45,128]{2,0,1:T(2,128)} %param.6) | copy-start | bytes 138244
  0.7 11.0 %copy-start = (f32[2,4,45,128]{3,1,2,0:T(4,128)S(1)}, f32[2,4,45,128]{3,1,2,0:T(4,128)}, u32[]{:S(2)}) copy-start(f32[2,4,45,128]{3,1,2,0:T(4,128)} %param.5) | copy-start | bytes 552964
  0.8 26.9 %collective-permute-start.1 = (f32[2,8,128]{2,1,0:T(8,128)S(1)}, f32[2,8,128]{2,1,0:T(8,128)S(1)}, u32[]{:S(2)}, u32[]{:S(2)}) collective-permute-start(f32[2,8,128]{2,1,0:T(8,128)S(1)} %pad_maximum_fusion.7), channel_id=1, source_target_pairs={{0,4},{4,8},{8,12},{12,16},{16,20},{20,24},{24,28},{28,32},{32,36}... | collective-permute-start | bytes 24584 | tf_op jit(solution)/shard_map/ppermute | solution.py:22
  9.8 18.0 %collective-permute-start = (f32[2,10,128]{2,1,0:T(8,128)S(1)}, f32[2,10,128]{2,1,0:T(8,128)S(1)}, u32[]{:S(2)}, u32[]{:S(2)}) collective-permute-start(f32[2,10,128]{2,1,0:T(8,128)S(1)} %pad_maximum_fusion.4), channel_id=1, source_target_pairs={{0,508},{4,0},{8,4},{12,8},{16,12},{20,16},{24,20},{28,24},{32,28}... | collective-permute-start | bytes 30728 | tf_op jit(solution)/shard_map/ppermute | solution.py:22
  12.3 14.2 %collective-permute-start.3 = (f32[2,4,45]{2,1,0:T(4,128)S(1)}, f32[2,4,45]{2,1,0:T(4,128)S(1)}, u32[]{:S(2)}, u32[]{:S(2)}) collective-permute-start(f32[2,4,45]{2,1,0:T(4,128)S(1)} %get-tuple-element.157), channel_id=1, source_target_pairs={{0,256},{1,2},{2,1},{3,259},{4,260},{5,6},{6,5},{7,263},{8,264},{9... | collective-permute-start | bytes 4328 | tf_op jit(solution)/shard_map/ppermute | solution.py:130
  22.9 4.4 %collective-permute-start.2 = (f32[2,4,45]{2,1,0:T(4,128)S(1)}, f32[2,4,45]{2,1,0:T(4,128)S(1)}, u32[]{:S(2)}, u32[]{:S(2)}) collective-permute-start(f32[2,4,45]{2,1,0:T(4,128)S(1)} %get-tuple-element.158), channel_id=1, source_target_pairs={{0,1},{1,0},{2,3},{3,2},{4,5},{5,4},{6,7},{7,6},{8,9},{9,8},{10,11... | collective-permute-start | bytes 4328 | tf_op jit(solution)/shard_map/ppermute | solution.py:129
  25.1 0.7 copy-start.3
  26.4 0.9 copy-start.2
  29.6 21.0 %all-to-all-start = ((f32[16,2,5,128]{3,1,2,0:T(2,128)}), f32[16,2,5,128]{3,1,2,0:T(2,128)S(1)}, u32[]{:S(2)}, u32[]{:S(2)}) async-start(f32[16,2,5,128]{3,1,2,0:T(2,128)} %broadcast_in_dim.45), calls=%async_computation | async-start | bytes 163840 | tf_op jit(solution)/shard_map/all_to_all | solution.py:57
  51.7 11.3 %all-to-all-start.1 = ((f32[8,2,5,128]{3,1,2,0:T(2,128)}), f32[8,2,5,128]{3,1,2,0:T(2,128)S(1)}, u32[]{:S(2)}, u32[]{:S(2)}) async-start(f32[8,2,5,128]{3,1,2,0:T(2,128)} %broadcast_in_dim.46), calls=%async_computation.1 | async-start | bytes 81920 | tf_op jit(solution)/shard_map/all_to_all | solution.py:57
  64.3 8.3 %collective-permute-start.5 = (f32[2,4,47]{2,1,0:T(4,128)S(1)}, f32[2,4,47]{2,1,0:T(4,128)S(1)}, u32[]{:S(2)}, u32[]{:S(2)}) collective-permute-start(f32[2,4,47]{2,1,0:T(4,128)S(1)} %get-tuple-element.117), channel_id=1, source_target_pairs={{0,256},{1,2},{2,1},{3,259},{4,260},{5,6},{6,5},{7,263},{8,264},{9... | collective-permute-start | bytes 4520 | tf_op jit(solution)/shard_map/ppermute | solution.py:130
  66.7 5.8 %collective-permute-start.4 = (f32[2,4,47]{2,1,0:T(4,128)S(1)}, f32[2,4,47]{2,1,0:T(4,128)S(1)}, u32[]{:S(2)}, u32[]{:S(2)}) collective-permute-start(f32[2,4,47]{2,1,0:T(4,128)S(1)} %get-tuple-element.118), channel_id=1, source_target_pairs={{0,1},{1,0},{2,3},{3,2},{4,5},{5,4},{6,7},{7,6},{8,9},{9,8},{10,11... | collective-permute-start | bytes 4520 | tf_op jit(solution)/shard_map/ppermute | solution.py:129
